TPU v7x, 128 devices: a whole 4x4x4 slice. The times are simulated.
128 devices in a mesh: dp: 8 (over x, core), tensor: 16 (over z, y).
Axes of the slice: x: 4, y: 4, z: 4, core: 2. Of those that a mesh axis runs over, the one named last changes fastest.
Arguments:
- hidden: bfloat16 [2048, 8192], P('dp', 'tensor'), may hold values from -170 to 170, as said below
- neighbour_ids: int32 [32, 2], P('dp'), may hold values from 0 to 255, as said below
- database: bfloat16 [256, 128, 8192], P('dp', None, 'tensor'), may hold values from -6 to 6
- w_query: bfloat16 [8192, 4096], P(None, 'tensor'), may hold values from -0.0625 to 0.0625
- w_key: bfloat16 [8192, 4096], P(None, 'tensor'), may hold values from -0.0625 to 0.0625
- w_value: bfloat16 [8192, 4096], P(None, 'tensor'), may hold values from -0.0625 to 0.0625
- w_out: bfloat16 [4096, 8192], P('tensor'), may hold values from -0.09375 to 0.09375
Outputs:
- mixed: bfloat16 [2048, 8192], P('dp', 'tensor')
Inputs may be any that keep to these rules, and one draw needn't show every extreme that they name: `neighbour_ids`: database block b is held by index b // 32 of dp. Among the 8 neighbour ids of one sequence (the rows of one device), at most 4 belong to the same holder, and in every sequence exactly 4 do. `hidden`: hidden states may be large for some tokens.
All inputs are finite; a program needn't handle non-finite values.
Results may differ from a plain program's by a relative error of at most 0.02.
Values may be sent and summed in bfloat16 or wider, within the bound.
No kernel may reach another device: no remote copies, remote signals or barrier semaphores. Data moves between devices by JAX's collectives and lax.ppermute only.
A program may use at most 128 MiB of HBM per device.

v0:
```python
import jax
import jax.numpy as jnp
from jax import lax
from jax.sharding import PartitionSpec as P

HD = 128


def attend(query_rows, key_rows, value_rows, heads_count, group_len):
    tok_count, width = query_rows.shape
    groups = tok_count // group_len
    head_size = width // heads_count
    shifted = jnp.concatenate(
        [query_rows[group_len - 1 :], jnp.zeros((group_len - 1, width), jnp.bfloat16)], 0
    )
    shifted = shifted.reshape(groups, group_len, heads_count, head_size)
    key_block = key_rows.reshape(groups, -1, heads_count, head_size)
    value_block = value_rows.reshape(groups, -1, heads_count, head_size)
    scores = jnp.einsum(
        "cqhd,ckhd->chqk", shifted, key_block, preferred_element_type=jnp.float32
    ) / jnp.sqrt(jnp.float32(head_size))
    top_score = jnp.max(scores, axis=-1, keepdims=True)
    weights_raw = jnp.exp(scores - top_score)
    soft = (weights_raw / jnp.sum(weights_raw, axis=-1, keepdims=True)).astype(jnp.bfloat16)
    blended = jnp.einsum(
        "chqk,ckhd->cqhd", soft, value_block, preferred_element_type=jnp.float32
    ).astype(jnp.bfloat16)
    blended = blended.reshape(tok_count, width)
    return jnp.concatenate(
        [jnp.zeros((group_len - 1, width), jnp.bfloat16), blended[: tok_count - group_len + 1]], 0
    )


def shards(hidden, neighbour_ids, database, w_query, w_key, w_value, w_out):
    dp_count = lax.axis_size("dp")
    tok_rows = hidden.shape[0]
    group_count = neighbour_ids.shape[0]
    per_reader = group_count * neighbour_ids.shape[1]
    capacity = per_reader // 2
    db_count = database.shape[0]
    ret_len = database.shape[1]
    col_count = database.shape[2]
    head_cols = w_query.shape[1]
    heads_local = head_cols // HD
    query_sum = jnp.dot(
        lax.all_gather(hidden, "tensor", axis=1, tiled=True),
        w_query,
        preferred_element_type=jnp.float32,
    )
    query_rows = query_sum.astype(jnp.bfloat16)
    block_ids = neighbour_ids.reshape(per_reader)
    owners = block_ids // db_count
    earlier = jnp.arange(per_reader)[:, None] > jnp.arange(per_reader)[None, :]
    slot_rank = jnp.sum(((owners[:, None] == owners[None, :]) & earlier).astype(jnp.int32), 1)
    slot_range = jnp.arange(capacity, dtype=jnp.int32)
    local_index = block_ids % db_count
    owner_range = jnp.arange(dp_count, dtype=jnp.int32)
    slot_hit = (owners[:, None, None] == owner_range[None, :, None]) & (
        slot_rank[:, None, None] == slot_range[None, None, :]
    )
    request_table = jnp.sum(slot_hit.astype(jnp.int32) * local_index[:, None, None], 0)
    requested = lax.all_to_all(request_table, "dp", split_axis=0, concat_axis=0, tiled=True)
    outgoing = jnp.take(database, requested.reshape(-1), axis=0).reshape(
        dp_count, capacity, ret_len, col_count
    )
    arrived = lax.all_to_all(outgoing, "dp", split_axis=0, concat_axis=0, tiled=True)
    neighbour_rows = jnp.take(
        arrived.reshape(dp_count * capacity, ret_len, col_count),
        owners * capacity + slot_rank,
        axis=0,
    )
    assembled = lax.all_gather(neighbour_rows, "tensor", axis=2, tiled=True).reshape(
        per_reader * ret_len, -1
    )
    key_sum = jnp.dot(assembled, w_key, preferred_element_type=jnp.float32)
    value_sum = jnp.dot(assembled, w_value, preferred_element_type=jnp.float32)
    key_rows = key_sum.astype(jnp.bfloat16)
    value_rows = value_sum.astype(jnp.bfloat16)
    context = attend(query_rows, key_rows, value_rows, heads_local, tok_rows // group_count)
    partial_out = jnp.dot(context, w_out, preferred_element_type=jnp.float32)
    return lax.psum_scatter(
        partial_out.astype(jnp.bfloat16), "tensor", scatter_dimension=1, tiled=True
    )


def solution(mesh):
    placed = (
        P("dp", "tensor"),
        P("dp", None),
        P("dp", None, "tensor"),
        P(None, "tensor"),
        P(None, "tensor"),
        P(None, "tensor"),
        P("tensor", None),
    )
    return jax.shard_map(
        shards, mesh=mesh, in_specs=placed, out_specs=P("dp", "tensor"), check_vma=False
    )
```

profile of v0, /device:TPU:0, one launch (start us, length us, event | category | flops | bytes accessed | tf_op | source)
XLA Modules:
  0.0 323.0 jit_solution(10386996719630286824)
XLA Ops:
  6.5 0.0 all-gather.5.cloned.1.call-start
  6.5 0.7 all-gather.5.cloned.1.call-update
  7.3 0.8 copy.32
  8.0 0.1 reshape.299
  8.1 0.2 convert_reduce_fusion
  8.3 0.1 iota_compare_fusion
  8.4 0.1 select_reduce_fusion
  8.5 0.1 copy.33
  8.6 9.5 %all_to_all.14 = s32[8,1,4]{2,1,0:T(1,128)S(1)} all-to-all(s32[8,1,4]{2,1,0:T(1,128)S(1)} %copy.33), channel_id=1, replica_groups=mesh['dp'=8,'tensor'=16] {'dp'}, dimensions={0} | all-to-all | bytes 256 | tf_op jit(solution)/shard_map/all_to_all | solution.py:62
  18.1 0.5 broadcast.312
  18.6 0.7 reduce.3
  19.2 0.1 reshape.301
  19.3 0.1 copy.34
  19.4 0.1 copy.35
  19.5 5.1 %gather_fusion = bf16[32,128,512]{2,1,0:T(8,128)(2,1)} fusion(bf16[32,128,512]{2,1,0:T(8,128)(2,1)} %param.9, s32[1024]{0:T(1024)S(1)} %pad_clamp_fusion.1), kind=kCustom, calls=%fused_computation | custom fusion | bytes 8388736 | tf_op jit(solution)/shard_map/jit(_take)/gather | solution.py:63
  24.6 4.6 %broadcast_select_fusion = bf16[8,4,128,512]{3,2,1,0:T(8,128)(2,1)} fusion(bf16[8,4,128,512]{3,2,1,0:T(8,128)(2,1)} %bitcast.32, pred[8,4]{1,0:T(8,128)(4,1)S(1)} %copy.35), kind=kLoop, calls=%fused_computation.4 | loop fusion | flops 2097152 | bytes 8388640 | tf_op jit(solution)/shard_map/jit(_take)/select_n | solution.py:63
  29.2 4.6 %all-to-all-start.1 = ((bf16[8,4,128,512]{3,2,1,0:T(8,128)(2,1)}), bf16[8,4,128,512]{3,2,1,0:T(8,128)(2,1)}, u32[]{:S(2)}, u32[]{:S(2)}) async-start(bf16[8,4,128,512]{3,2,1,0:T(8,128)(2,1)} %broadcast_select_fusion), calls=%async_computation.1 | async-start | bytes 8388608 | tf_op jit(solution)/shard_map/all_to_all | solution.py:66
  33.7 0.0 all-gather.3.cloned.1.call-start
  33.8 0.1 reshape.303
  33.9 49.5 %all-to-all-done.1 = bf16[8,4,128,512]{3,2,1,0:T(8,128)(2,1)} async-done(((bf16[8,4,128,512]{3,2,1,0:T(8,128)(2,1)}), bf16[8,4,128,512]{3,2,1,0:T(8,128)(2,1)}, u32[]{:S(2)}, u32[]{:S(2)}) %all-to-all-start.1) | async-done | bytes 4194336 | tf_op jit(solution)/shard_map/all_to_all | solution.py:66
  83.4 2.8 gather_fusion.1
  86.2 1.1 broadcast_select_fusion.1
  87.3 0.0 all-gather.3.cloned.1.call-update
  87.3 0.0 reduce-scatter.2.cloned.1.call-start
  87.4 0.0 all-gather.5.cloned.1.call-done
  87.4 4.7 %fusion.15 = bf16[256,256]{1,0:T(8,128)(2,1)S(1)} fusion(bf16[256,8192]{1,0:T(8,128)(2,1)} %all-gather.5.cloned.1.call-done, bf16[8192,256]{1,0:T(8,128)(2,1)} %param.10), kind=kOutput, calls=%fused_computation.50 | convolution fusion | flops 1073741824 | bytes 8519680 | tf_op jit(solution)/shard_map/dot_general | solution.py:45
  92.2 115.9 %all-gather.3.cloned.1.call-done = bf16[8,128,8192]{2,1,0:T(8,128)(2,1)} async-done(((bf16[8,128,512]{2,1,0:T(8,128)(2,1)}), bf16[8,128,8192]{2,1,0:T(8,128)(2,1)}) %all-gather.3.cloned.1.call-update) | async-done | bytes 16777232 | tf_op jit(solution)/shard_map/all_gather | solution.py:72
  208.1 11.4 %convolution_convert_fusion.2 = bf16[1024,256]{1,0:T(8,128)(2,1)S(1)} fusion(bf16[1024,8192]{1,0:T(8,128)(2,1)} %bitcast.36, bf16[8192,256]{1,0:T(8,128)(2,1)} %param.12), kind=kOutput, calls=%fused_computation.6 | convolution fusion | flops 4295229440 | bytes 21495808 | tf_op jit(solution)/shard_map/dot_general | solution.py:76
  219.6 0.1 reshape.305
  219.7 11.4 %convolution_convert_fusion.1 = bf16[1024,256]{1,0:T(8,128)(2,1)S(1)} fusion(bf16[1024,8192]{1,0:T(8,128)(2,1)} %bitcast.37, bf16[8192,256]{1,0:T(8,128)(2,1)} %param.11), kind=kOutput, calls=%fused_computation.5 | convolution fusion | flops 4295229440 | bytes 21495808 | tf_op jit(solution)/shard_map/dot_general | solution.py:75
  231.1 0.1 reshape.307
  231.3 0.3 convolution_multiply_fusion
  231.6 0.3 fusion.14
  231.8 1.0 fusion.3
  232.8 0.1 copy.40
  233.0 5.4 %convolution_convert_fusion = bf16[256,8192]{1,0:T(8,128)(2,1)} fusion(bf16[256,8192]{1,0:T(8,128)(2,1)} %param.13, bf16[193,256]{1,0:T(8,128)(2,1)S(1)} %slice.13), kind=kOutput, calls=%fused_computation.3 | convolution fusion | flops 1075838976 | bytes 8487424 | tf_op jit(solution)/shard_map/dot_general | solution.py:80
  238.4 0.0 reduce-scatter.2.cloned.1.call-update
  238.4 78.1 %reduce-scatter.2.cloned.1.call-done = bf16[256,512]{1,0:T(8,128)(2,1)} async-done(((bf16[256,8192]{1,0:T(8,128)(2,1)}), bf16[256,512]{1,0:T(8,128)(2,1)}) %reduce-scatter.2.cloned.1.call-update) | async-done | bytes 262160 | tf_op jit(solution)/shard_map/reduce_scatter | solution.py:81
  (13 shorter events, 0.2 us)
Async XLA Ops:
  6.5 80.9 %all-gather.5.cloned.1.call-start = ((), (), s32[]{:S(2)}) async-start(), calls=%async_computation.4 | async-start | bytes 4456448 | tf_op jit(solution)/shard_map/all_gather | solution.py:46
  29.2 54.2 %all-to-all-start.1 = ((bf16[8,4,128,512]{3,2,1,0:T(8,128)(2,1)}), bf16[8,4,128,512]{3,2,1,0:T(8,128)(2,1)}, u32[]{:S(2)}, u32[]{:S(2)}) async-start(bf16[8,4,128,512]{3,2,1,0:T(8,128)(2,1)} %broadcast_select_fusion), calls=%async_computation.1 | async-start | bytes 8388608 | tf_op jit(solution)/shard_map/all_to_all | solution.py:66
  33.7 174.4 %all-gather.3.cloned.1.call-start = ((), (), s32[]{:S(2)}) async-start(), calls=%async_computation.3 | async-start | bytes 17825792 | tf_op jit(solution)/shard_map/all_gather | solution.py:72
  87.3 229.1 %reduce-scatter.2.cloned.1.call-start = ((), (), s32[]{:S(2)}) async-start(), calls=%async_computation.5 | async-start | bytes 4456448 | tf_op jit(solution)/shard_map/reduce_scatter | solution.py:81
Sparse Core Ops, SparseCore 0:
  9.4 59.4 all-gather.4
  87.5 120.6 all-gather.2
  238.5 77.8 reduce-scatter.1
where the time goes:
time: 323 us
  waiting for transfers between devices  244 us (76%)
  matrix products  34.2 us (11%)
  between operations  13.2 us (4%)
  local copies, waits for them, and re-layouts  10.1 us (3%)
  blocking collectives  9.49 us (3%)
  other arithmetic  7.06 us (2%)
  starting transfers between devices  4.64 us (1%)
    all_gather x1, waiting for transfers between devices, shards(): lax.all_gather(neighbour_rows, 'tensor', axis=2, tiled=True)  116 us
    reduce_scatter x1, waiting for transfers between devices, shards(): lax.psum_scatter(partial_out.astype(jnp.bfloat16), 'tensor', scatter_dime...  78.1 us
    all_to_all x1, waiting for transfers between devices, shards(): lax.all_to_all(outgoing, 'dp', split_axis=0, concat_axis=0, tiled=True)  49.5 us
    dot_general x1, matrix products, shards(): key_sum = jnp.dot(assembled, w_key, preferred_element_type=jnp.float32)  11.4 us
    dot_general x1, matrix products, shards(): value_sum = jnp.dot(assembled, w_value, preferred_element_type=jnp.float32)  11.4 us
    all_to_all x1, blocking collectives, shards(): lax.all_to_all(request_table, 'dp', split_axis=0, concat_axis=0, tiled=True)  9.49 us
  transfers between devices with their start and end apart: 4, of which 3 were waited for; matrix products, arithmetic and copies ran while one was open for 7% of the time, Pallas kernels for 0%

commit v1 on v0

--- a/solution.py
+++ b/solution.py
@@ -76,11 +76,17 @@
     value_sum = jnp.dot(assembled, w_value, preferred_element_type=jnp.float32)
     key_rows = key_sum.astype(jnp.bfloat16)
     value_rows = value_sum.astype(jnp.bfloat16)
-    context = attend(query_rows, key_rows, value_rows, heads_local, tok_rows // group_count)
-    partial_out = jnp.dot(context, w_out, preferred_element_type=jnp.float32)
-    return lax.psum_scatter(
-        partial_out.astype(jnp.bfloat16), "tensor", scatter_dimension=1, tiled=True
+    group_len = tok_rows // group_count
+    context = attend(query_rows, key_rows, value_rows, heads_local, group_len)
+    live = context[group_len - 1 :]
+    live_rows = live.shape[0]
+    tensor_count = lax.axis_size("tensor")
+    partial_out = jnp.dot(live, w_out, preferred_element_type=jnp.float32).astype(jnp.bfloat16)
+    spread = lax.all_to_all(
+        partial_out.reshape(live_rows, tensor_count, -1), "tensor", split_axis=1, concat_axis=1, tiled=True
     )
+    summed = jnp.sum(spread.astype(jnp.float32), axis=1).astype(jnp.bfloat16)
+    return jnp.concatenate([jnp.zeros((group_len - 1, summed.shape[1]), jnp.bfloat16), summed], 0)
 
 
 def solution(mesh):

time: 323 us -> 294 us (0.910)
  waiting for transfers between devices: 244 us -> 166 us
  blocking collectives: 9.49 us -> 55.3 us
  local copies, waits for them, and re-layouts: 10.1 us -> 14.6 us
    reduce_scatter x1 -> x0, waiting for transfers between devices: 78.1 us -> none  [shards(): lax.psum_scatter(partial_out.astype(jnp.bfloat16), 'tensor', scatter_dime...]
    all_to_all x0 -> x1, blocking collectives: none -> 45.8 us  [shards(): lax.all_to_all(partial_out.reshape(live_rows, tensor_count, -1), 'tensor'...]
  transfers between devices with their start and end apart: 4 -> 3, of which waited for: 3 -> 2; matrix products, arithmetic and copies ran while one was open for 7% -> 7% of each run, Pallas kernels for 0% -> 0%
where the time goes in v1:
time: 294 us
  waiting for transfers between devices  166 us (56%)
  blocking collectives  55.3 us (19%)
  matrix products  32.1 us (11%)
  local copies, waits for them, and re-layouts  14.6 us (5%)
  between operations  13.6 us (5%)
  other arithmetic  7.61 us (3%)
  starting transfers between devices  4.6 us (2%)
    all_gather x1, waiting for transfers between devices, shards(): lax.all_gather(neighbour_rows, 'tensor', axis=2, tiled=True)  116 us
    all_to_all x1, waiting for transfers between devices, shards(): lax.all_to_all(outgoing, 'dp', split_axis=0, concat_axis=0, tiled=True)  49.5 us
    all_to_all x1, blocking collectives, shards(): lax.all_to_all(partial_out.reshape(live_rows, tensor_count, -1), 'tensor'...  45.8 us
    dot_general x1, matrix products, shards(): value_sum = jnp.dot(assembled, w_value, preferred_element_type=jnp.float32)  11.4 us
    dot_general x1, matrix products, shards(): key_sum = jnp.dot(assembled, w_key, preferred_element_type=jnp.float32)  11.4 us
    all_to_all x1, blocking collectives, shards(): lax.all_to_all(request_table, 'dp', split_axis=0, concat_axis=0, tiled=True)  9.49 us
  transfers between devices with their start and end apart: 3, of which 2 were waited for; matrix products, arithmetic and copies ran while one was open for 7% of the time, Pallas kernels for 0%

profile of v1, /device:TPU:0, one launch (start us, length us, event | category | flops | bytes accessed | tf_op | source)
XLA Modules:
  0.0 293.9 jit_solution(2541385137041955387)
XLA Ops:
  6.5 0.0 all-gather.5.cloned.1.call-start
  6.5 0.7 all-gather.5.cloned.1.call-update
  7.3 0.8 copy.33
  8.0 0.1 reshape.302
  8.1 0.2 convert_reduce_fusion
  8.3 0.1 iota_compare_fusion
  8.4 0.1 select_reduce_fusion
  8.5 0.1 copy.34
  8.6 9.5 %all_to_all.19 = s32[8,1,4]{2,1,0:T(1,128)S(1)} all-to-all(s32[8,1,4]{2,1,0:T(1,128)S(1)} %copy.34), channel_id=1, replica_groups=mesh['dp'=8,'tensor'=16] {'dp'}, dimensions={0} | all-to-all | bytes 256 | tf_op jit(solution)/shard_map/all_to_all | solution.py:62
  18.1 0.5 broadcast.311
  18.6 0.7 reduce.4
  19.2 0.1 reshape.304
  19.3 0.1 copy.35
  19.4 0.1 copy.36
  19.5 5.1 %gather_fusion = bf16[32,128,512]{2,1,0:T(8,128)(2,1)} fusion(bf16[32,128,512]{2,1,0:T(8,128)(2,1)} %param.9, s32[1024]{0:T(1024)S(1)} %pad_clamp_fusion.1), kind=kCustom, calls=%fused_computation | custom fusion | bytes 8388736 | tf_op jit(solution)/shard_map/jit(_take)/gather | solution.py:63
  24.6 4.6 %broadcast_select_fusion = bf16[8,4,128,512]{3,2,1,0:T(8,128)(2,1)} fusion(bf16[8,4,128,512]{3,2,1,0:T(8,128)(2,1)} %bitcast.36, pred[8,4]{1,0:T(8,128)(4,1)S(1)} %copy.36), kind=kLoop, calls=%fused_computation.4 | loop fusion | flops 2097152 | bytes 8388640 | tf_op jit(solution)/shard_map/jit(_take)/select_n | solution.py:63
  29.2 4.6 %all-to-all-start.1 = ((bf16[8,4,128,512]{3,2,1,0:T(8,128)(2,1)}), bf16[8,4,128,512]{3,2,1,0:T(8,128)(2,1)}, u32[]{:S(2)}, u32[]{:S(2)}) async-start(bf16[8,4,128,512]{3,2,1,0:T(8,128)(2,1)} %broadcast_select_fusion), calls=%async_computation.1 | async-start | bytes 8388608 | tf_op jit(solution)/shard_map/all_to_all | solution.py:66
  33.7 0.0 all-gather.3.cloned.1.call-start
  33.8 0.1 reshape.306
  33.9 49.5 %all-to-all-done.1 = bf16[8,4,128,512]{3,2,1,0:T(8,128)(2,1)} async-done(((bf16[8,4,128,512]{3,2,1,0:T(8,128)(2,1)}), bf16[8,4,128,512]{3,2,1,0:T(8,128)(2,1)}, u32[]{:S(2)}, u32[]{:S(2)}) %all-to-all-start.1) | async-done | bytes 4194336 | tf_op jit(solution)/shard_map/all_to_all | solution.py:66
  83.4 2.8 gather_fusion.1
  86.2 1.1 broadcast_select_fusion.1
  87.3 0.0 all-gather.3.cloned.1.call-update
  87.3 0.0 all-gather.5.cloned.1.call-done
  87.4 4.7 %fusion.14 = bf16[256,256]{1,0:T(8,128)(2,1)S(1)} fusion(bf16[256,8192]{1,0:T(8,128)(2,1)} %all-gather.5.cloned.1.call-done, bf16[8192,256]{1,0:T(8,128)(2,1)} %param.10), kind=kOutput, calls=%fused_computation.49 | convolution fusion | flops 1073741824 | bytes 8519680 | tf_op jit(solution)/shard_map/dot_general | solution.py:45
  92.2 115.9 %all-gather.3.cloned.1.call-done = bf16[8,128,8192]{2,1,0:T(8,128)(2,1)} async-done(((bf16[8,128,512]{2,1,0:T(8,128)(2,1)}), bf16[8,128,8192]{2,1,0:T(8,128)(2,1)}) %all-gather.3.cloned.1.call-update) | async-done | bytes 16777232 | tf_op jit(solution)/shard_map/all_gather | solution.py:72
  208.1 11.4 %convolution_convert_fusion.2 = bf16[1024,256]{1,0:T(8,128)(2,1)S(1)} fusion(bf16[1024,8192]{1,0:T(8,128)(2,1)} %bitcast.41, bf16[8192,256]{1,0:T(8,128)(2,1)} %param.12), kind=kOutput, calls=%fused_computation.6 | convolution fusion | flops 4295229440 | bytes 21495808 | tf_op jit(solution)/shard_map/dot_general | solution.py:76
  219.6 0.1 reshape.308
  219.7 11.4 %convolution_convert_fusion.1 = bf16[1024,256]{1,0:T(8,128)(2,1)S(1)} fusion(bf16[1024,8192]{1,0:T(8,128)(2,1)} %bitcast.42, bf16[8192,256]{1,0:T(8,128)(2,1)} %param.11), kind=kOutput, calls=%fused_computation.5 | convolution fusion | flops 4295229440 | bytes 21495808 | tf_op jit(solution)/shard_map/dot_general | solution.py:75
  231.1 0.1 reshape.310
  231.3 0.3 convolution_multiply_fusion
  231.6 0.3 fusion.13
  231.8 1.0 fusion.3
  232.8 0.1 copy.41
  233.0 3.2 %convolution_convert_fusion = bf16[193,8192]{1,0:T(8,128)(2,1)S(1)} fusion(bf16[256,8192]{1,0:T(8,128)(2,1)} %param.13, bf16[256,256]{1,0:T(8,128)(2,1)S(1)} %bitcast.38), kind=kOutput, calls=%fused_computation.3 | convolution fusion | flops 811081728 | bytes 7458816 | tf_op jit(solution)/shard_map/dot_general | solution.py:84
  236.2 1.6 copy.44
  237.8 0.3 slice.14
  238.2 1.8 copy.42
  239.9 45.8 %all_to_all.20 = bf16[193,16,512]{2,0,1:T(8,128)(2,1)S(1)} all-to-all(bf16[193,16,512]{2,0,1:T(8,128)(2,1)S(1)} %copy.42), channel_id=1, replica_groups=mesh['dp'=8,'tensor'=16] {'tensor'}, dimensions={1} | all-to-all | bytes 6324224 | tf_op jit(solution)/shard_map/all_to_all | solution.py:85
  285.7 0.5 reduce_sum.45
  286.3 0.8 concatenate.7
  (12 shorter events, 0.2 us)
Async XLA Ops:
  6.5 80.8 %all-gather.5.cloned.1.call-start = ((), (), s32[]{:S(2)}) async-start(), calls=%async_computation.4 | async-start | bytes 4456448 | tf_op jit(solution)/shard_map/all_gather | solution.py:46
  29.2 54.2 %all-to-all-start.1 = ((bf16[8,4,128,512]{3,2,1,0:T(8,128)(2,1)}), bf16[8,4,128,512]{3,2,1,0:T(8,128)(2,1)}, u32[]{:S(2)}, u32[]{:S(2)}) async-start(bf16[8,4,128,512]{3,2,1,0:T(8,128)(2,1)} %broadcast_select_fusion), calls=%async_computation.1 | async-start | bytes 8388608 | tf_op jit(solution)/shard_map/all_to_all | solution.py:66
  33.7 174.4 %all-gather.3.cloned.1.call-start = ((), (), s32[]{:S(2)}) async-start(), calls=%async_computation.3 | async-start | bytes 17825792 | tf_op jit(solution)/shard_map/all_gather | solution.py:72
Sparse Core Ops, SparseCore 0:
  9.4 59.4 all-gather.4
  87.5 120.6 all-gather.2

commit v2 on v1

--- a/solution.py
+++ b/solution.py
@@ -6,12 +6,11 @@
 HD = 128
 
 
-def attend(query_rows, key_rows, value_rows, heads_count, group_len):
-    tok_count, width = query_rows.shape
-    groups = tok_count // group_len
+def attend(query_live, key_rows, value_rows, heads_count, group_len, groups):
+    live_count, width = query_live.shape
     head_size = width // heads_count
     shifted = jnp.concatenate(
-        [query_rows[group_len - 1 :], jnp.zeros((group_len - 1, width), jnp.bfloat16)], 0
+        [query_live, jnp.zeros((groups * group_len - live_count, width), jnp.bfloat16)], 0
     )
     shifted = shifted.reshape(groups, group_len, heads_count, head_size)
     key_block = key_rows.reshape(groups, -1, heads_count, head_size)
@@ -25,10 +24,7 @@
     blended = jnp.einsum(
         "chqk,ckhd->cqhd", soft, value_block, preferred_element_type=jnp.float32
     ).astype(jnp.bfloat16)
-    blended = blended.reshape(tok_count, width)
-    return jnp.concatenate(
-        [jnp.zeros((group_len - 1, width), jnp.bfloat16), blended[: tok_count - group_len + 1]], 0
-    )
+    return blended.reshape(groups * group_len, width)[:live_count]
 
 
 def shards(hidden, neighbour_ids, database, w_query, w_key, w_value, w_out):
@@ -42,9 +38,13 @@
     col_count = database.shape[2]
     head_cols = w_query.shape[1]
     heads_local = head_cols // HD
-    query_sum = jnp.dot(
-        lax.all_gather(hidden, "tensor", axis=1, tiled=True),
-        w_query,
+    tensor_count = lax.axis_size("tensor")
+    group_len = tok_rows // group_count
+    hidden_parts = lax.all_gather(hidden[group_len - 1 :], "tensor", axis=0, tiled=False)
+    query_sum = jnp.einsum(
+        "srf,sfc->rc",
+        hidden_parts,
+        w_query.reshape(tensor_count, -1, head_cols),
         preferred_element_type=jnp.float32,
     )
     query_rows = query_sum.astype(jnp.bfloat16)
@@ -60,7 +60,7 @@
     )
     request_table = jnp.sum(slot_hit.astype(jnp.int32) * local_index[:, None, None], 0)
     requested = lax.all_to_all(request_table, "dp", split_axis=0, concat_axis=0, tiled=True)
-    outgoing = jnp.take(database, requested.reshape(-1), axis=0).reshape(
+    outgoing = jnp.take(database, requested.reshape(-1), axis=0, mode="clip").reshape(
         dp_count, capacity, ret_len, col_count
     )
     arrived = lax.all_to_all(outgoing, "dp", split_axis=0, concat_axis=0, tiled=True)
@@ -68,6 +68,7 @@
         arrived.reshape(dp_count * capacity, ret_len, col_count),
         owners * capacity + slot_rank,
         axis=0,
+        mode="clip",
     )
     assembled = lax.all_gather(neighbour_rows, "tensor", axis=2, tiled=True).reshape(
         per_reader * ret_len, -1
@@ -76,11 +77,8 @@
     value_sum = jnp.dot(assembled, w_value, preferred_element_type=jnp.float32)
     key_rows = key_sum.astype(jnp.bfloat16)
     value_rows = value_sum.astype(jnp.bfloat16)
-    group_len = tok_rows // group_count
-    context = attend(query_rows, key_rows, value_rows, heads_local, group_len)
-    live = context[group_len - 1 :]
+    live = attend(query_rows, key_rows, value_rows, heads_local, group_len, group_count)
     live_rows = live.shape[0]
-    tensor_count = lax.axis_size("tensor")
     partial_out = jnp.dot(live, w_out, preferred_element_type=jnp.float32).astype(jnp.bfloat16)
     spread = lax.all_to_all(
         partial_out.reshape(live_rows, tensor_count, -1), "tensor", split_axis=1, concat_axis=1, tiled=True

time: 294 us -> 290 us (0.986)
  other arithmetic: 7.61 us -> 1.91 us
    select_n x4 -> x0, other arithmetic: 5.74 us -> none  [the longest x2 4.58 us: shards(): jnp.take(database, requested.reshape(-1), axis=0)]
  transfers between devices with their start and end apart: 3 -> 3, of which waited for: 2 -> 2; matrix products, arithmetic and copies ran while one was open for 7% -> 6% of each run, Pallas kernels for 0% -> 0%
where the time goes in v2:
time: 290 us
  waiting for transfers between devices  166 us (57%)
  blocking collectives  55.3 us (19%)
  matrix products  31.6 us (11%)
  local copies, waits for them, and re-layouts  17.2 us (6%)
  between operations  13.5 us (5%)
  starting transfers between devices  4.61 us (2%)
    all_gather x1, waiting for transfers between devices, shards(): lax.all_gather(neighbour_rows, 'tensor', axis=2, tiled=True)  116 us
    all_to_all x1, waiting for transfers between devices, shards(): lax.all_to_all(outgoing, 'dp', split_axis=0, concat_axis=0, tiled=True)  49.5 us
    all_to_all x1, blocking collectives, shards(): lax.all_to_all(partial_out.reshape(live_rows, tensor_count, -1), 'tensor'...  45.8 us
    dot_general x1, matrix products, shards(): key_sum = jnp.dot(assembled, w_key, preferred_element_type=jnp.float32)  11.4 us
    dot_general x1, matrix products, shards(): value_sum = jnp.dot(assembled, w_value, preferred_element_type=jnp.float32)  11.4 us
    all_to_all x1, blocking collectives, shards(): lax.all_to_all(request_table, 'dp', split_axis=0, concat_axis=0, tiled=True)  9.49 us
  transfers between devices with their start and end apart: 3, of which 2 were waited for; matrix products, arithmetic and copies ran while one was open for 6% of the time, Pallas kernels for 0%

profile of v2, /device:TPU:0, one launch (start us, length us, event | category | flops | bytes accessed | tf_op | source)
XLA Modules:
  0.0 289.9 jit_solution(16193777343151937756)
XLA Ops:
  6.5 0.0 all-gather.8.cloned.1.call-start
  6.5 1.7 slice_bitcast_fusion
  8.2 0.0 all-gather.8.cloned.1.call-update
  8.2 0.8 copy.29
  9.0 0.1 reshape.250
  9.1 0.2 convert_reduce_fusion
  9.3 0.1 iota_compare_fusion.1
  9.4 0.1 select_reduce_fusion
  9.4 0.1 copy.30
  9.5 9.5 %all_to_all.19 = s32[8,1,4]{2,1,0:T(1,128)S(1)} all-to-all(s32[8,1,4]{2,1,0:T(1,128)S(1)} %copy.30), channel_id=1, replica_groups=mesh['dp'=8,'tensor'=16] {'dp'}, dimensions={0} | all-to-all | bytes 256 | tf_op jit(solution)/shard_map/all_to_all | solution.py:62
  19.0 0.6 broadcast.228
  19.6 0.7 reduce.4
  20.3 0.1 reshape.263
  20.4 5.1 %gather_fusion = bf16[32,128,512]{2,1,0:T(8,128)(2,1)} fusion(bf16[32,128,512]{2,1,0:T(8,128)(2,1)} %param.9, s32[1024]{0:T(1024)S(1)} %pad_clamp_fusion.1), kind=kCustom, calls=%fused_computation | custom fusion | bytes 8388736 | tf_op jit(solution)/shard_map/jit(_take)/gather | solution.py:63
  25.5 4.6 %all-to-all-start.1 = ((bf16[8,4,128,512]{3,2,1,0:T(8,128)(2,1)}), bf16[8,4,128,512]{3,2,1,0:T(8,128)(2,1)}, u32[]{:S(2)}, u32[]{:S(2)}) async-start(bf16[8,4,128,512]{3,2,1,0:T(8,128)(2,1)} %bitcast.37), calls=%async_computation.1 | async-start | bytes 8388608 | tf_op jit(solution)/shard_map/all_to_all | solution.py:66
  30.1 0.0 all-gather.6.cloned.1.call-start
  30.1 0.1 reshape.253
  30.3 49.5 %all-to-all-done.1 = bf16[8,4,128,512]{3,2,1,0:T(8,128)(2,1)} async-done(((bf16[8,4,128,512]{3,2,1,0:T(8,128)(2,1)}), bf16[8,4,128,512]{3,2,1,0:T(8,128)(2,1)}, u32[]{:S(2)}, u32[]{:S(2)}) %all-to-all-start.1) | async-done | bytes 4194336 | tf_op jit(solution)/shard_map/all_to_all | solution.py:66
  79.7 3.8 %gather_fusion.1 = bf16[8,128,512]{2,1,0:T(8,128)(2,1)} fusion(bf16[32,128,512]{2,1,0:T(8,128)(2,1)} %bitcast.2, s32[1024]{0:T(1024)S(1)} %pad_clamp_fusion), kind=kCustom, calls=%fused_computation.1 | custom fusion | bytes 2097184 | tf_op jit(solution)/shard_map/jit(_take)/gather | solution.py:67
  83.5 0.0 all-gather.6.cloned.1.call-update
  83.5 0.0 all-gather.8.cloned.1.call-done
  83.6 4.2 %fusion.3 = bf16[193,256]{1,0:T(8,128)(2,1)S(1)} fusion(bf16[16,193,512]{2,1,0:T(8,128)(2,1)} %all-gather.8.cloned.1.call-done, bf16[16,512,256]{2,1,0:T(8,128)(2,1)} %bitcast.38), kind=kOutput, calls=%fused_computation.11 | convolution fusion | flops 809550080 | bytes 7455232 | tf_op jit(solution)/shard_map/srf,sfc->rc/dot_general | solution.py:44
  87.9 116.3 %all-gather.6.cloned.1.call-done = bf16[8,128,8192]{2,1,0:T(8,128)(2,1)} async-done(((bf16[8,128,512]{2,1,0:T(8,128)(2,1)}), bf16[8,128,8192]{2,1,0:T(8,128)(2,1)}) %all-gather.6.cloned.1.call-update) | async-done | bytes 16777232 | tf_op jit(solution)/shard_map/all_gather | solution.py:73
  204.1 11.4 %convolution_convert_fusion.2 = bf16[1024,256]{1,0:T(8,128)(2,1)S(1)} fusion(bf16[1024,8192]{1,0:T(8,128)(2,1)} %bitcast.43, bf16[8192,256]{1,0:T(8,128)(2,1)} %param.12), kind=kOutput, calls=%fused_computation.5 | convolution fusion | flops 4295229440 | bytes 21495808 | tf_op jit(solution)/shard_map/dot_general | solution.py:77
  215.6 0.1 reshape.255
  215.7 11.4 %convolution_convert_fusion.1 = bf16[1024,256]{1,0:T(8,128)(2,1)S(1)} fusion(bf16[1024,8192]{1,0:T(8,128)(2,1)} %bitcast.44, bf16[8192,256]{1,0:T(8,128)(2,1)} %param.11), kind=kOutput, calls=%fused_computation.4 | convolution fusion | flops 4295229440 | bytes 21495808 | tf_op jit(solution)/shard_map/dot_general | solution.py:76
  227.2 0.1 reshape.258
  227.3 0.3 convolution_multiply_fusion
  227.6 0.3 fusion.13
  227.9 1.0 fusion.4
  228.8 0.1 copy.35
  229.0 3.2 %convolution_convert_fusion = bf16[193,8192]{1,0:T(8,128)(2,1)S(1)} fusion(bf16[256,8192]{1,0:T(8,128)(2,1)} %param.13, bf16[256,256]{1,0:T(8,128)(2,1)S(1)} %bitcast.40), kind=kOutput, calls=%fused_computation.3 | convolution fusion | flops 811081728 | bytes 7458816 | tf_op jit(solution)/shard_map/dot_general | solution.py:82
  232.2 1.5 copy.38
  233.7 0.5 slice.13
  234.2 1.8 copy.36
  236.0 45.8 %all_to_all.20 = bf16[193,16,512]{2,0,1:T(8,128)(2,1)S(1)} all-to-all(bf16[193,16,512]{2,0,1:T(8,128)(2,1)S(1)} %copy.36), channel_id=1, replica_groups=mesh['dp'=8,'tensor'=16] {'tensor'}, dimensions={1} | all-to-all | bytes 6324224 | tf_op jit(solution)/shard_map/all_to_all | solution.py:83
  281.8 0.5 reduce_sum.45
  282.3 0.8 concatenate.7
  (8 shorter events, 0.1 us)
Async XLA Ops:
  6.5 77.0 %all-gather.8.cloned.1.call-start = ((), (), s32[]{:S(2)}) async-start(), calls=%async_computation.4 | async-start | bytes 3481600 | tf_op jit(solution)/shard_map/all_gather | solution.py:43
  25.5 54.2 %all-to-all-start.1 = ((bf16[8,4,128,512]{3,2,1,0:T(8,128)(2,1)}), bf16[8,4,128,512]{3,2,1,0:T(8,128)(2,1)}, u32[]{:S(2)}, u32[]{:S(2)}) async-start(bf16[8,4,128,512]{3,2,1,0:T(8,128)(2,1)} %bitcast.37), calls=%async_computation.1 | async-start | bytes 8388608 | tf_op jit(solution)/shard_map/all_to_all | solution.py:66
  30.1 174.0 %all-gather.6.cloned.1.call-start = ((), (), s32[]{:S(2)}) async-start(), calls=%async_computation.3 | async-start | bytes 17825792 | tf_op jit(solution)/shard_map/all_gather | solution.py:73
Sparse Core Ops, SparseCore 0:
  9.5 50.8 all-gather.7
  83.7 120.4 all-gather.5

commit v3 on v2

--- a/solution.py
+++ b/solution.py
@@ -25,6 +25,59 @@
         "chqk,ckhd->cqhd", soft, value_block, preferred_element_type=jnp.float32
     ).astype(jnp.bfloat16)
     return blended.reshape(groups * group_len, width)[:live_count]
+
+
+def last_token(query_row, tail_rows, w_key, w_value, heads_count):
+    tensor_count = lax.axis_size("tensor")
+    col_count = tail_rows.shape[-1]
+    tail = tail_rows.reshape(-1, col_count)
+    features = w_key.shape[0]
+    head_size = query_row.shape[0] // heads_count
+    exact = lax.Precision.HIGHEST
+    spread_query = jnp.einsum(
+        "fhd,hd->hf",
+        w_key.reshape(features, heads_count, head_size),
+        query_row.reshape(heads_count, head_size),
+        preferred_element_type=jnp.float32,
+    )
+    own_query = lax.all_to_all(
+        spread_query.reshape(heads_count, tensor_count, col_count),
+        "tensor",
+        split_axis=1,
+        concat_axis=0,
+        tiled=True,
+    ).reshape(-1, col_count)
+    partial_scores = jnp.einsum(
+        "hf,kf->hk", own_query, tail, precision=exact, preferred_element_type=jnp.float32
+    )
+    all_scores = lax.all_to_all(
+        jnp.broadcast_to(partial_scores[None], (tensor_count,) + partial_scores.shape),
+        "tensor",
+        split_axis=0,
+        concat_axis=0,
+        tiled=True,
+    )
+    scores = jnp.sum(all_scores, axis=0) / jnp.sqrt(jnp.float32(head_size))
+    top_score = jnp.max(scores, axis=-1, keepdims=True)
+    weights_raw = jnp.exp(scores - top_score)
+    soft = (weights_raw / jnp.sum(weights_raw, axis=-1, keepdims=True)).astype(jnp.bfloat16)
+    mixed_rows = jnp.einsum("hk,kf->hf", soft, tail, preferred_element_type=jnp.float32)
+    own_rows = lax.all_to_all(
+        mixed_rows.reshape(tensor_count, heads_count, col_count),
+        "tensor",
+        split_axis=0,
+        concat_axis=0,
+        tiled=True,
+    )
+    own_rows = jnp.transpose(own_rows, (1, 0, 2)).reshape(heads_count, features)
+    context = jnp.einsum(
+        "hf,fhd->hd",
+        own_rows,
+        w_value.reshape(features, heads_count, head_size),
+        precision=exact,
+        preferred_element_type=jnp.float32,
+    )
+    return context.astype(jnp.bfloat16).reshape(-1)
 
 
 def shards(hidden, neighbour_ids, database, w_query, w_key, w_value, w_out):
@@ -70,14 +123,24 @@
         axis=0,
         mode="clip",
     )
-    assembled = lax.all_gather(neighbour_rows, "tensor", axis=2, tiled=True).reshape(
-        per_reader * ret_len, -1
+    main_rows = per_reader - 2
+    main_parts = lax.all_gather(neighbour_rows[:main_rows], "tensor", axis=0, tiled=False)
+    w_key_parts = w_key.reshape(tensor_count, col_count, head_cols)
+    w_value_parts = w_value.reshape(tensor_count, col_count, head_cols)
+    key_rows = jnp.einsum(
+        "snkf,sfc->nkc", main_parts, w_key_parts, preferred_element_type=jnp.float32
+    ).astype(jnp.bfloat16).reshape(main_rows * ret_len, head_cols)
+    value_rows = jnp.einsum(
+        "snkf,sfc->nkc", main_parts, w_value_parts, preferred_element_type=jnp.float32
+    ).astype(jnp.bfloat16).reshape(main_rows * ret_len, head_cols)
+    main_groups = main_rows // 2
+    main_live = attend(
+        query_rows[: main_groups * group_len], key_rows, value_rows, heads_local, group_len, main_groups
     )
-    key_sum = jnp.dot(assembled, w_key, preferred_element_type=jnp.float32)
-    value_sum = jnp.dot(assembled, w_value, preferred_element_type=jnp.float32)
-    key_rows = key_sum.astype(jnp.bfloat16)
-    value_rows = value_sum.astype(jnp.bfloat16)
-    live = attend(query_rows, key_rows, value_rows, heads_local, group_len, group_count)
+    last_live = last_token(
+        query_rows[main_groups * group_len], neighbour_rows[main_rows:], w_key, w_value, heads_local
+    )
+    live = jnp.concatenate([main_live, last_live[None]], 0)
     live_rows = live.shape[0]
     partial_out = jnp.dot(live, w_out, preferred_element_type=jnp.float32).astype(jnp.bfloat16)
     spread = lax.all_to_all(

time: 290 us -> 258 us (0.89)
  waiting for transfers between devices: 166 us -> 100 us
  blocking collectives: 55.3 us -> 67.6 us
  starting transfers between devices: 4.61 us -> 16.6 us
  local copies, waits for them, and re-layouts: 17.2 us -> 25 us
    all_gather x1, waiting for transfers between devices: 116 us -> 34 us  [shards(): lax.all_gather(neighbour_rows[:main_rows], 'tensor', axis=0, tiled=False)]
    all_to_all x0 -> x2, waiting for transfers between devices: none -> 16.6 us  [the longest x1 8.44 us: last_token(): lax.all_to_all(spread_query.reshape(heads_count, tensor_count, col_count)...]
    all_to_all x0 -> x1, blocking collectives: none -> 13.1 us  [last_token(): lax.all_to_all(jnp.broadcast_to(partial_scores[None], (tensor_count,) + p...]
    all_to_all x0 -> x2, starting transfers between devices: none -> 12 us  [the longest x1 8.27 us: last_token(): lax.all_to_all(spread_query.reshape(heads_count, tensor_count, col_count)...]
    reshape x2, local copies, waits for them, and re-layouts: 0.25 us -> 6.43 us  [the longest x1 6.38 us: last_token(): w_key.reshape(features, heads_count, head_size)]
    dot_general x2 -> x6, matrix products: 22.9 us -> 23.1 us  [the longest x1 9.17 us: shards(): jnp.einsum('snkf,sfc->nkc', main_parts, w_value_parts, preferred_element_...]
  transfers between devices with their start and end apart: 3 -> 5, of which waited for: 2 -> 4; matrix products, arithmetic and copies ran while one was open for 6% -> 11% of each run, Pallas kernels for 0% -> 0%
where the time goes in v3:
time: 258 us; the launch traced here: 257 us
  waiting for transfers between devices  100 us (39%)
  blocking collectives  67.6 us (26%)
  matrix products  31.7 us (12%)
  local copies, waits for them, and re-layouts  25 us (10%)
  starting transfers between devices  16.6 us (6%)
  between operations  13.6 us (5%)
    all_to_all x1, waiting for transfers between devices, shards(): lax.all_to_all(outgoing, 'dp', split_axis=0, concat_axis=0, tiled=True)  49.5 us
    all_to_all x1, blocking collectives, shards(): lax.all_to_all(partial_out.reshape(live_rows, tensor_count, -1), 'tensor'...  45 us
    all_gather x1, waiting for transfers between devices, shards(): lax.all_gather(neighbour_rows[:main_rows], 'tensor', axis=0, tiled=False)  34 us
    all_to_all x1, blocking collectives, last_token(): lax.all_to_all(jnp.broadcast_to(partial_scores[None], (tensor_count,) + p...  13.1 us
    all_to_all x1, blocking collectives, shards(): lax.all_to_all(request_table, 'dp', split_axis=0, concat_axis=0, tiled=True)  9.49 us
    dot_general x1, matrix products, shards(): jnp.einsum('snkf,sfc->nkc', main_parts, w_value_parts, preferred_element_...  9.17 us
    dot_general x1, matrix products, shards(): jnp.einsum('snkf,sfc->nkc', main_parts, w_key_parts, preferred_element_ty...  9.17 us
    all_to_all x1, waiting for transfers between devices, last_token(): lax.all_to_all(spread_query.reshape(heads_count, tensor_count, col_count)...  8.44 us
  transfers between devices with their start and end apart: 5, of which 4 were waited for; matrix products, arithmetic and copies ran while one was open for 11% of the time, Pallas kernels for 0%

profile of v3, /device:TPU:0, one launch (start us, length us, event | category | flops | bytes accessed | tf_op | source)
XLA Modules:
  0.0 256.9 jit_solution(13808799054269181755)
XLA Ops:
  6.5 0.0 all-gather.8.cloned.1.call-start
  6.5 1.7 slice_bitcast_fusion
  8.2 0.0 all-gather.8.cloned.1.call-update
  8.2 0.8 copy.34
  9.0 0.1 reshape.325
  9.1 0.2 convert_reduce_fusion
  9.3 0.1 iota_compare_fusion.1
  9.4 0.1 select_reduce_fusion
  9.4 0.1 copy.35
  9.5 9.5 %all_to_all.44 = s32[8,1,4]{2,1,0:T(1,128)S(1)} all-to-all(s32[8,1,4]{2,1,0:T(1,128)S(1)} %copy.35), channel_id=1, replica_groups=mesh['dp'=8,'tensor'=16] {'dp'}, dimensions={0} | all-to-all | bytes 256 | tf_op jit(solution)/shard_map/all_to_all | solution.py:115
  19.0 0.6 broadcast.272
  19.6 0.7 reduce.4
  20.3 0.1 reshape.343
  20.4 5.1 %gather_fusion = bf16[32,128,512]{2,1,0:T(8,128)(2,1)} fusion(bf16[32,128,512]{2,1,0:T(8,128)(2,1)} %param.9, s32[1024]{0:T(1024)S(1)} %pad_clamp_fusion.1), kind=kCustom, calls=%fused_computation | custom fusion | bytes 8388736 | tf_op jit(solution)/shard_map/jit(_take)/gather | solution.py:116
  25.5 4.6 %all-to-all-start.1 = ((bf16[8,4,128,512]{3,2,1,0:T(8,128)(2,1)}), bf16[8,4,128,512]{3,2,1,0:T(8,128)(2,1)}, u32[]{:S(2)}, u32[]{:S(2)}) async-start(bf16[8,4,128,512]{3,2,1,0:T(8,128)(2,1)} %bitcast.94), calls=%async_computation.1 | async-start | bytes 8388608 | tf_op jit(solution)/shard_map/all_to_all | solution.py:119
  30.1 0.0 all-gather.6.cloned.1.call-start
  30.1 0.1 reshape.328
  30.3 49.5 %all-to-all-done.1 = bf16[8,4,128,512]{3,2,1,0:T(8,128)(2,1)} async-done(((bf16[8,4,128,512]{3,2,1,0:T(8,128)(2,1)}), bf16[8,4,128,512]{3,2,1,0:T(8,128)(2,1)}, u32[]{:S(2)}, u32[]{:S(2)}) %all-to-all-start.1) | async-done | bytes 4194336 | tf_op jit(solution)/shard_map/all_to_all | solution.py:119
  79.7 2.8 %gather_fusion.1 = bf16[8,128,512]{2,1,0:T(8,128)(2,1)S(1)} fusion(bf16[32,128,512]{2,1,0:T(8,128)(2,1)} %bitcast.2, s32[1024]{0:T(1024)S(1)} %pad_clamp_fusion), kind=kCustom, calls=%fused_computation.1 | custom fusion | bytes 2097184 | tf_op jit(solution)/shard_map/jit(_take)/gather | solution.py:120
  82.5 0.9 slice.25
  83.5 0.0 all-gather.6.cloned.1.call-update
  83.5 6.4 %copy.52 = bf16[8192,256]{0,1:T(8,128)(2,1)} copy(bf16[8192,256]{1,0:T(8,128)(2,1)} %param.11) | data formatting | bytes 8388608 | tf_op jit(solution)/shard_map/reshape | solution.py:39
  89.9 0.0 all-gather.8.cloned.1.call-done
  89.9 0.0 copy-start
  89.9 4.4 %fusion.8 = bf16[193,256]{1,0:T(8,128)(2,1)S(1)} fusion(bf16[16,193,512]{2,1,0:T(8,128)(2,1)} %all-gather.8.cloned.1.call-done, bf16[16,512,256]{2,1,0:T(8,128)(2,1)} %bitcast.96), kind=kOutput, calls=%fused_computation.15 | convolution fusion | flops 809550080 | bytes 7455232 | tf_op jit(solution)/shard_map/srf,sfc->rc/dot_general | solution.py:97
  94.3 0.3 copy-done
  94.5 0.7 fusion.22
  95.2 0.7 copy.48
  95.9 8.3 %all-to-all-start.2 = ((f32[2,16,512]{2,0,1:T(2,128)}), f32[2,16,512]{2,0,1:T(2,128)S(1)}, u32[]{:S(2)}, u32[]{:S(2)}) async-start(f32[2,16,512]{2,0,1:T(2,128)} %bitcast.21), calls=%async_computation.2 | async-start | bytes 131072 | tf_op jit(solution)/shard_map/all_to_all | solution.py:43
  104.2 8.4 %all-to-all-done.2 = f32[2,16,512]{2,0,1:T(2,128)S(1)} async-done(((f32[2,16,512]{2,0,1:T(2,128)}), f32[2,16,512]{2,0,1:T(2,128)S(1)}, u32[]{:S(2)}, u32[]{:S(2)}) %all-to-all-start.2) | async-done | bytes 65568 | tf_op jit(solution)/shard_map/all_to_all | solution.py:43
  112.7 0.3 fusion.27
  113.1 13.1 %all_to_all.45 = f32[16,32,256]{2,1,0:T(8,128)S(1)} all-to-all(f32[16,32,256]{2,1,0:T(8,128)S(1)} %broadcast_in_dim.7), channel_id=1, replica_groups=mesh['dp'=8,'tensor'=16] {'tensor'}, dimensions={0} | all-to-all | bytes 1048576 | tf_op jit(solution)/shard_map/all_to_all | solution.py:53
  126.2 0.1 multiply_reduce_fusion
  126.3 0.2 fusion.18
  126.5 0.1 divide_convert_fusion.2
  126.6 0.1 fusion.19
  126.8 0.7 copy.42
  127.5 3.7 %all-to-all-start.4 = ((f32[16,2,512]{2,1,0:T(2,128)}), f32[16,2,512]{2,1,0:T(2,128)S(1)}, u32[]{:S(2)}, u32[]{:S(2)}) async-start(f32[16,2,512]{2,1,0:T(2,128)} %copy.42), calls=%async_computation.4 | async-start | bytes 131072 | tf_op jit(solution)/shard_map/all_to_all | solution.py:65
  131.2 8.2 %all-to-all-done.4 = f32[16,2,512]{2,1,0:T(2,128)S(1)} async-done(((f32[16,2,512]{2,1,0:T(2,128)}), f32[16,2,512]{2,1,0:T(2,128)S(1)}, u32[]{:S(2)}, u32[]{:S(2)}) %all-to-all-start.4) | async-done | bytes 65568 | tf_op jit(solution)/shard_map/all_to_all | solution.py:65
  139.4 3.6 %fusion.1 = f32[2,1,128]{2,1,0:T(1,128)S(1)} fusion(f32[2,8192,1]{1,0,2:T(2,128)S(1)} %bitcast.104, bf16[8192,256]{1,0:T(8,128)(2,1)} %param.12), kind=kOutput, calls=%fused_computation.4 | convolution fusion | flops 25165824 | bytes 4260864 | tf_op jit(solution)/shard_map/hf,fhd->hd/dot_general | solution.py:73
  143.1 34.0 %all-gather.6.cloned.1.call-done = bf16[96,128,512]{2,1,0:T(8,128)(2,1)} async-done(((bf16[6,128,512]{2,1,0:T(8,128)(2,1)}), bf16[96,128,512]{2,1,0:T(8,128)(2,1)}) %all-gather.6.cloned.1.call-update) | async-done | bytes 12582928 | tf_op jit(solution)/shard_map/all_gather | solution.py:127
  177.0 9.2 %fusion.6 = bf16[6,128,256]{2,1,0:T(8,128)(2,1)S(1)} fusion(bf16[16,6,128,512]{3,2,1,0:T(8,128)(2,1)} %bitcast.107, bf16[16,512,256,1]{2,1,3,0:T(8,128)(2,1)} %bitcast.98), kind=kOutput, calls=%fused_computation.11 | convolution fusion | flops 3221422080 | bytes 17170432 | tf_op jit(solution)/shard_map/snkf,sfc->nkc/dot_general | solution.py:130
  186.2 0.1 reshape_reshape.7
  186.3 0.3 convolution_multiply_fusion
  186.6 0.2 fusion.26
  186.8 9.2 %fusion.5 = bf16[6,128,256]{2,1,0:T(8,128)(2,1)S(1)} fusion(bf16[16,6,128,512]{3,2,1,0:T(8,128)(2,1)} %bitcast.108, bf16[16,512,256,1]{2,1,3,0:T(8,128)(2,1)} %bitcast.109), kind=kOutput, calls=%fused_computation.10 | convolution fusion | flops 3221422080 | bytes 17170432 | tf_op jit(solution)/shard_map/snkf,sfc->nkc/dot_general | solution.py:133
  196.0 0.1 reshape_reshape.6
  196.1 0.7 fusion.9
  196.8 0.1 copy.40
  196.9 3.2 %convolution_convert_fusion = bf16[193,8192]{1,0:T(8,128)(2,1)S(1)} fusion(bf16[256,8192]{1,0:T(8,128)(2,1)} %param.13, bf16[1,256]{1,0:T(2,128)(2,1)S(1)} %bitcast.106, bf16[192,256]{1,0:T(8,128)(2,1)S(1)} %bitcast.101), kind=kOutput, calls=%fused_computation.3 | convolution fusion | flops 811279360 | bytes 7455232 | tf_op jit(solution)/shard_map/dot_general | solution.py:145
  200.2 1.5 copy.56
  201.6 0.3 slice.28
  201.9 1.8 copy.43
  203.7 45.0 %all_to_all.46 = bf16[193,16,512]{2,0,1:T(8,128)(2,1)S(1)} all-to-all(bf16[193,16,512]{2,0,1:T(8,128)(2,1)S(1)} %copy.43), channel_id=1, replica_groups=mesh['dp'=8,'tensor'=16] {'tensor'}, dimensions={1} | all-to-all | bytes 6324224 | tf_op jit(solution)/shard_map/all_to_all | solution.py:146
  248.8 0.5 reduce_sum.65
  249.3 0.8 concatenate.7
  (15 shorter events, 0.3 us)
Async XLA Ops:
  6.5 83.3 %all-gather.8.cloned.1.call-start = ((), (), s32[]{:S(2)}) async-start(), calls=%async_computation.7 | async-start | bytes 3481600 | tf_op jit(solution)/shard_map/all_gather | solution.py:96
  25.5 54.2 %all-to-all-start.1 = ((bf16[8,4,128,512]{3,2,1,0:T(8,128)(2,1)}), bf16[8,4,128,512]{3,2,1,0:T(8,128)(2,1)}, u32[]{:S(2)}, u32[]{:S(2)}) async-start(bf16[8,4,128,512]{3,2,1,0:T(8,128)(2,1)} %bitcast.94), calls=%async_computation.1 | async-start | bytes 8388608 | tf_op jit(solution)/shard_map/all_to_all | solution.py:119
  30.1 146.9 %all-gather.6.cloned.1.call-start = ((), (), s32[]{:S(2)}) async-start(), calls=%async_computation.6 | async-start | bytes 13369344 | tf_op jit(solution)/shard_map/all_gather | solution.py:127
  89.9 4.7 %copy-start = (bf16[8192,256]{0,1:T(8,128)(2,1)S(1)}, bf16[8192,256]{0,1:T(8,128)(2,1)}, u32[]{:S(2)}) copy-start(bf16[8192,256]{0,1:T(8,128)(2,1)} %copy.52) | copy-start | bytes 12582916
  95.9 16.7 %all-to-all-start.2 = ((f32[2,16,512]{2,0,1:T(2,128)}), f32[2,16,512]{2,0,1:T(2,128)S(1)}, u32[]{:S(2)}, u32[]{:S(2)}) async-start(f32[2,16,512]{2,0,1:T(2,128)} %bitcast.21), calls=%async_computation.2 | async-start | bytes 131072 | tf_op jit(solution)/shard_map/all_to_all | solution.py:43
  127.5 11.9 %all-to-all-start.4 = ((f32[16,2,512]{2,1,0:T(2,128)}), f32[16,2,512]{2,1,0:T(2,128)S(1)}, u32[]{:S(2)}, u32[]{:S(2)}) async-start(f32[16,2,512]{2,1,0:T(2,128)} %copy.42), calls=%async_computation.4 | async-start | bytes 131072 | tf_op jit(solution)/shard_map/all_to_all | solution.py:65
Sparse Core Ops, SparseCore 0:
  9.5 50.8 all-gather.7
  83.6 93.3 all-gather.5

commit v4 on v3

--- a/solution.py
+++ b/solution.py
@@ -127,12 +127,12 @@
     main_parts = lax.all_gather(neighbour_rows[:main_rows], "tensor", axis=0, tiled=False)
     w_key_parts = w_key.reshape(tensor_count, col_count, head_cols)
     w_value_parts = w_value.reshape(tensor_count, col_count, head_cols)
-    key_rows = jnp.einsum(
-        "snkf,sfc->nkc", main_parts, w_key_parts, preferred_element_type=jnp.float32
-    ).astype(jnp.bfloat16).reshape(main_rows * ret_len, head_cols)
-    value_rows = jnp.einsum(
-        "snkf,sfc->nkc", main_parts, w_value_parts, preferred_element_type=jnp.float32
-    ).astype(jnp.bfloat16).reshape(main_rows * ret_len, head_cols)
+    w_both = jnp.concatenate([w_key_parts, w_value_parts], axis=2)
+    both_rows = jnp.einsum(
+        "snkf,sfc->nkc", main_parts, w_both, preferred_element_type=jnp.float32
+    ).astype(jnp.bfloat16)
+    key_rows = both_rows[..., :head_cols].reshape(main_rows * ret_len, head_cols)
+    value_rows = both_rows[..., head_cols:].reshape(main_rows * ret_len, head_cols)
     main_groups = main_rows // 2
     main_live = attend(
         query_rows[: main_groups * group_len], key_rows, value_rows, heads_local, group_len, main_groups
@@ -142,11 +142,14 @@
     )
     live = jnp.concatenate([main_live, last_live[None]], 0)
     live_rows = live.shape[0]
-    partial_out = jnp.dot(live, w_out, preferred_element_type=jnp.float32).astype(jnp.bfloat16)
-    spread = lax.all_to_all(
-        partial_out.reshape(live_rows, tensor_count, -1), "tensor", split_axis=1, concat_axis=1, tiled=True
-    )
-    summed = jnp.sum(spread.astype(jnp.float32), axis=1).astype(jnp.bfloat16)
+    partial_out = jnp.einsum(
+        "rc,csf->srf",
+        live,
+        w_out.reshape(head_cols, tensor_count, -1),
+        preferred_element_type=jnp.float32,
+    ).astype(jnp.bfloat16)
+    spread = lax.all_to_all(partial_out, "tensor", split_axis=0, concat_axis=0, tiled=True)
+    summed = jnp.sum(spread.astype(jnp.float32), axis=0).astype(jnp.bfloat16)
     return jnp.concatenate([jnp.zeros((group_len - 1, summed.shape[1]), jnp.bfloat16), summed], 0)
 
 

time: 258 us -> 248 us (0.961)
  matrix products: 31.7 us -> 25.4 us
  local copies, waits for them, and re-layouts: 25 us -> 21.5 us
    dot_general x3 -> x2, matrix products: 21.5 us -> 15.3 us  [the longest x1 12.1 us: shards(): jnp.einsum('snkf,sfc->nkc', main_parts, w_both, preferred_element_type=jn...]
  transfers between devices with their start and end apart: 5 -> 5, of which waited for: 4 -> 4; matrix products, arithmetic and copies ran while one was open for 11% -> 12% of each run, Pallas kernels for 0% -> 0%
where the time goes in v4:
time: 248 us; the launch traced here: 247 us
  waiting for transfers between devices  100 us (40%)
  blocking collectives  67.6 us (27%)
  matrix products  25.4 us (10%)
  local copies, waits for them, and re-layouts  21.5 us (9%)
  starting transfers between devices  16.4 us (7%)
  between operations  13.6 us (5%)
    all_to_all x1, waiting for transfers between devices, shards(): lax.all_to_all(outgoing, 'dp', split_axis=0, concat_axis=0, tiled=True)  49.5 us
    all_to_all x1, blocking collectives, shards(): lax.all_to_all(partial_out, 'tensor', split_axis=0, concat_axis=0, tiled=...  45 us
    all_gather x1, waiting for transfers between devices, shards(): lax.all_gather(neighbour_rows[:main_rows], 'tensor', axis=0, tiled=False)  34 us
    all_to_all x1, blocking collectives, last_token(): lax.all_to_all(jnp.broadcast_to(partial_scores[None], (tensor_count,) + p...  13.1 us
    dot_general x1, matrix products, shards(): jnp.einsum('snkf,sfc->nkc', main_parts, w_both, preferred_element_type=jn...  12.1 us
    all_to_all x1, blocking collectives, shards(): lax.all_to_all(request_table, 'dp', split_axis=0, concat_axis=0, tiled=True)  9.49 us
    all_to_all x1, waiting for transfers between devices, last_token(): lax.all_to_all(spread_query.reshape(heads_count, tensor_count, col_count)...  8.44 us
    all_to_all x1, waiting for transfers between devices, last_token(): lax.all_to_all(mixed_rows.reshape(tensor_count, heads_count, col_count),...  8.38 us
  transfers between devices with their start and end apart: 5, of which 4 were waited for; matrix products, arithmetic and copies ran while one was open for 12% of the time, Pallas kernels for 0%

profile of v4, /device:TPU:0, one launch (start us, length us, event | category | flops | bytes accessed | tf_op | source)
XLA Modules:
  0.0 247.1 jit_solution(10541425182763091821)
XLA Ops:
  6.5 0.0 all-gather.8.cloned.1.call-start
  6.5 1.7 slice_bitcast_fusion
  8.2 0.0 all-gather.8.cloned.1.call-update
  8.2 0.8 copy.35
  9.0 0.1 reshape.325
  9.1 0.2 convert_reduce_fusion
  9.3 0.1 iota_compare_fusion.1
  9.4 0.1 select_reduce_fusion
  9.4 0.1 copy.36
  9.5 9.5 %all_to_all.44 = s32[8,1,4]{2,1,0:T(1,128)S(1)} all-to-all(s32[8,1,4]{2,1,0:T(1,128)S(1)} %copy.36), channel_id=1, replica_groups=mesh['dp'=8,'tensor'=16] {'dp'}, dimensions={0} | all-to-all | bytes 256 | tf_op jit(solution)/shard_map/all_to_all | solution.py:115
  19.0 0.6 broadcast.272
  19.6 0.7 reduce.4
  20.3 0.1 reshape.343
  20.4 5.1 %gather_fusion = bf16[32,128,512]{2,1,0:T(8,128)(2,1)} fusion(bf16[32,128,512]{2,1,0:T(8,128)(2,1)} %param.9, s32[1024]{0:T(1024)S(1)} %pad_clamp_fusion.1), kind=kCustom, calls=%fused_computation | custom fusion | bytes 8388736 | tf_op jit(solution)/shard_map/jit(_take)/gather | solution.py:116
  25.5 4.6 %all-to-all-start.1 = ((bf16[8,4,128,512]{3,2,1,0:T(8,128)(2,1)}), bf16[8,4,128,512]{3,2,1,0:T(8,128)(2,1)}, u32[]{:S(2)}, u32[]{:S(2)}) async-start(bf16[8,4,128,512]{3,2,1,0:T(8,128)(2,1)} %bitcast.90), calls=%async_computation.1 | async-start | bytes 8388608 | tf_op jit(solution)/shard_map/all_to_all | solution.py:119
  30.1 0.0 all-gather.6.cloned.1.call-start
  30.1 0.1 reshape.328
  30.3 49.5 %all-to-all-done.1 = bf16[8,4,128,512]{3,2,1,0:T(8,128)(2,1)} async-done(((bf16[8,4,128,512]{3,2,1,0:T(8,128)(2,1)}), bf16[8,4,128,512]{3,2,1,0:T(8,128)(2,1)}, u32[]{:S(2)}, u32[]{:S(2)}) %all-to-all-start.1) | async-done | bytes 4194336 | tf_op jit(solution)/shard_map/all_to_all | solution.py:119
  79.7 2.8 %gather_fusion.1 = bf16[8,128,512]{2,1,0:T(8,128)(2,1)S(1)} fusion(bf16[32,128,512]{2,1,0:T(8,128)(2,1)} %bitcast.2, s32[1024]{0:T(1024)S(1)} %pad_clamp_fusion), kind=kCustom, calls=%fused_computation.1 | custom fusion | bytes 2097184 | tf_op jit(solution)/shard_map/jit(_take)/gather | solution.py:120
  82.5 0.9 slice.33
  83.5 0.0 all-gather.6.cloned.1.call-update
  83.5 6.4 %copy.52 = bf16[8192,256]{0,1:T(8,128)(2,1)} copy(bf16[8192,256]{1,0:T(8,128)(2,1)} %param.11) | data formatting | bytes 8388608 | tf_op jit(solution)/shard_map/reshape | solution.py:39
  89.9 0.0 all-gather.8.cloned.1.call-done
  89.9 0.0 copy-start
  89.9 4.4 %fusion.14 = bf16[193,256]{1,0:T(8,128)(2,1)S(1)} fusion(bf16[16,193,512]{2,1,0:T(8,128)(2,1)} %all-gather.8.cloned.1.call-done, bf16[16,512,256]{2,1,0:T(8,128)(2,1)} %bitcast.92), kind=kOutput, calls=%fused_computation.19 | convolution fusion | flops 809550080 | bytes 7455232 | tf_op jit(solution)/shard_map/srf,sfc->rc/dot_general | solution.py:97
  94.3 0.3 copy-done
  94.5 0.7 fusion.27
  95.2 0.7 copy.48
  95.9 8.3 %all-to-all-start.2 = ((f32[2,16,512]{2,0,1:T(2,128)}), f32[2,16,512]{2,0,1:T(2,128)S(1)}, u32[]{:S(2)}, u32[]{:S(2)}) async-start(f32[2,16,512]{2,0,1:T(2,128)} %bitcast.18), calls=%async_computation.2 | async-start | bytes 131072 | tf_op jit(solution)/shard_map/all_to_all | solution.py:43
  104.2 8.4 %all-to-all-done.2 = f32[2,16,512]{2,0,1:T(2,128)S(1)} async-done(((f32[2,16,512]{2,0,1:T(2,128)}), f32[2,16,512]{2,0,1:T(2,128)S(1)}, u32[]{:S(2)}, u32[]{:S(2)}) %all-to-all-start.2) | async-done | bytes 65568 | tf_op jit(solution)/shard_map/all_to_all | solution.py:43
  112.7 0.3 fusion.34
  113.1 13.1 %all_to_all.45 = f32[16,32,256]{2,1,0:T(8,128)S(1)} all-to-all(f32[16,32,256]{2,1,0:T(8,128)S(1)} %broadcast_in_dim.7), channel_id=1, replica_groups=mesh['dp'=8,'tensor'=16] {'tensor'}, dimensions={0} | all-to-all | bytes 1048576 | tf_op jit(solution)/shard_map/all_to_all | solution.py:53
  126.2 0.1 multiply_reduce_fusion
  126.3 0.2 fusion.23
  126.5 0.1 divide_convert_fusion.2
  126.6 0.1 fusion.24
  126.8 0.7 copy.43
  127.5 3.5 %all-to-all-start.4 = ((f32[16,2,512]{2,1,0:T(2,128)}), f32[16,2,512]{2,1,0:T(2,128)S(1)}, u32[]{:S(2)}, u32[]{:S(2)}) async-start(f32[16,2,512]{2,1,0:T(2,128)} %copy.43), calls=%async_computation.4 | async-start | bytes 131072 | tf_op jit(solution)/shard_map/all_to_all | solution.py:65
  131.0 8.4 %all-to-all-done.4 = f32[16,2,512]{2,1,0:T(2,128)S(1)} async-done(((f32[16,2,512]{2,1,0:T(2,128)}), f32[16,2,512]{2,1,0:T(2,128)S(1)}, u32[]{:S(2)}, u32[]{:S(2)}) %all-to-all-start.4) | async-done | bytes 65568 | tf_op jit(solution)/shard_map/all_to_all | solution.py:65
  139.4 3.6 %fusion.7 = f32[2,1,128]{2,1,0:T(1,128)S(1)} fusion(f32[2,8192,1]{1,0,2:T(2,128)S(1)} %bitcast.100, bf16[8192,256]{1,0:T(8,128)(2,1)} %param.12), kind=kOutput, calls=%fused_computation.10 | convolution fusion | flops 25165824 | bytes 4260864 | tf_op jit(solution)/shard_map/hf,fhd->hd/dot_general | solution.py:73
  143.1 34.0 %all-gather.6.cloned.1.call-done = bf16[96,128,512]{2,1,0:T(8,128)(2,1)} async-done(((bf16[6,128,512]{2,1,0:T(8,128)(2,1)}), bf16[96,128,512]{2,1,0:T(8,128)(2,1)}) %all-gather.6.cloned.1.call-update) | async-done | bytes 12582928 | tf_op jit(solution)/shard_map/all_gather | solution.py:127
  177.0 12.1 %bitcast_convert_fusion = bf16[6,128,512]{2,1,0:T(8,128)(2,1)S(1)} fusion(bf16[16,6,128,512]{3,2,1,0:T(8,128)(2,1)} %bitcast.103, bf16[16,512,256]{2,1,0:T(8,128)(2,1)} %bitcast.104, bf16[16,512,256]{2,1,0:T(8,128)(2,1)} %bitcast.93), kind=kOutput, calls=%fused_computation.14 | convolution fusion | flops 6459621376 | bytes 21757952 | tf_op jit(solution)/shard_map/snkf,sfc->nkc/dot_general | solution.py:131
  189.1 0.1 fusion.32
  189.2 0.1 reshape_reshape.7
  189.3 0.2 convolution_multiply_fusion
  189.5 0.2 fusion.33
  189.8 0.1 reshape_reshape.6
  189.9 0.7 fusion.15
  190.6 0.1 copy.41
  190.7 3.2 %convert_bitcast_fusion = bf16[16,193,512]{2,1,0:T(8,128)(2,1)S(1)} fusion(bf16[32,16,8,512]{3,2,1,0:T(8,128)(2,1)} %bitcast.94, bf16[1,256]{1,0:T(2,128)(2,1)S(1)} %bitcast.102, bf16[192,256]{1,0:T(8,128)(2,1)S(1)} %bitcast.97), kind=kOutput, calls=%fused_computation.13 | convolution fusion | flops 811279360 | bytes 7455232 | tf_op jit(solution)/shard_map/rc,csf->srf/dot_general | solution.py:145
  194.0 45.0 %all_to_all.46 = bf16[16,193,512]{2,1,0:T(8,128)(2,1)S(1)} all-to-all(bf16[16,193,512]{2,1,0:T(8,128)(2,1)S(1)} %convert_bitcast_fusion), channel_id=1, replica_groups=mesh['dp'=8,'tensor'=16] {'tensor'}, dimensions={0} | all-to-all | bytes 6324224 | tf_op jit(solution)/shard_map/all_to_all | solution.py:151
  239.0 0.5 reduce_sum.65
  239.6 0.8 concatenate.11
  (15 shorter events, 0.3 us)
Async XLA Ops:
  6.5 83.3 %all-gather.8.cloned.1.call-start = ((), (), s32[]{:S(2)}) async-start(), calls=%async_computation.7 | async-start | bytes 3481600 | tf_op jit(solution)/shard_map/all_gather | solution.py:96
  25.5 54.2 %all-to-all-start.1 = ((bf16[8,4,128,512]{3,2,1,0:T(8,128)(2,1)}), bf16[8,4,128,512]{3,2,1,0:T(8,128)(2,1)}, u32[]{:S(2)}, u32[]{:S(2)}) async-start(bf16[8,4,128,512]{3,2,1,0:T(8,128)(2,1)} %bitcast.90), calls=%async_computation.1 | async-start | bytes 8388608 | tf_op jit(solution)/shard_map/all_to_all | solution.py:119
  30.1 146.9 %all-gather.6.cloned.1.call-start = ((), (), s32[]{:S(2)}) async-start(), calls=%async_computation.6 | async-start | bytes 13369344 | tf_op jit(solution)/shard_map/all_gather | solution.py:127
  89.9 4.7 %copy-start = (bf16[8192,256]{0,1:T(8,128)(2,1)S(1)}, bf16[8192,256]{0,1:T(8,128)(2,1)}, u32[]{:S(2)}) copy-start(bf16[8192,256]{0,1:T(8,128)(2,1)} %copy.52) | copy-start | bytes 12582916
  95.9 16.7 %all-to-all-start.2 = ((f32[2,16,512]{2,0,1:T(2,128)}), f32[2,16,512]{2,0,1:T(2,128)S(1)}, u32[]{:S(2)}, u32[]{:S(2)}) async-start(f32[2,16,512]{2,0,1:T(2,128)} %bitcast.18), calls=%async_computation.2 | async-start | bytes 131072 | tf_op jit(solution)/shard_map/all_to_all | solution.py:43
  127.5 11.9 %all-to-all-start.4 = ((f32[16,2,512]{2,1,0:T(2,128)}), f32[16,2,512]{2,1,0:T(2,128)S(1)}, u32[]{:S(2)}, u32[]{:S(2)}) async-start(f32[16,2,512]{2,1,0:T(2,128)} %copy.43), calls=%async_computation.4 | async-start | bytes 131072 | tf_op jit(solution)/shard_map/all_to_all | solution.py:65
Sparse Core Ops, SparseCore 0:
  9.5 50.8 all-gather.7
  83.6 93.3 all-gather.5

commit v5 on v4

--- a/solution.py
+++ b/solution.py
@@ -117,17 +117,15 @@
         dp_count, capacity, ret_len, col_count
     )
     arrived = lax.all_to_all(outgoing, "dp", split_axis=0, concat_axis=0, tiled=True)
-    neighbour_rows = jnp.take(
-        arrived.reshape(dp_count * capacity, ret_len, col_count),
-        owners * capacity + slot_rank,
-        axis=0,
-        mode="clip",
-    )
+    arrived_rows = arrived.reshape(dp_count * capacity, ret_len, col_count)
+    arrived_slot = owners * capacity + slot_rank
     main_rows = per_reader - 2
-    main_parts = lax.all_gather(neighbour_rows[:main_rows], "tensor", axis=0, tiled=False)
+    head_rows = jnp.take(arrived_rows, arrived_slot[:main_rows], axis=0, mode="clip")
+    tail_rows = jnp.take(arrived_rows, arrived_slot[main_rows:], axis=0, mode="clip")
+    main_parts = lax.all_gather(head_rows, "tensor", axis=0, tiled=False)
     w_key_parts = w_key.reshape(tensor_count, col_count, head_cols)
     w_value_parts = w_value.reshape(tensor_count, col_count, head_cols)
-    w_both = jnp.concatenate([w_key_parts, w_value_parts], axis=2)
+    w_both = lax.optimization_barrier(jnp.concatenate([w_key_parts, w_value_parts], axis=2))
     both_rows = jnp.einsum(
         "snkf,sfc->nkc", main_parts, w_both, preferred_element_type=jnp.float32
     ).astype(jnp.bfloat16)
@@ -138,7 +136,7 @@
         query_rows[: main_groups * group_len], key_rows, value_rows, heads_local, group_len, main_groups
     )
     last_live = last_token(
-        query_rows[main_groups * group_len], neighbour_rows[main_rows:], w_key, w_value, heads_local
+        query_rows[main_groups * group_len], tail_rows, w_key, w_value, heads_local
     )
     live = jnp.concatenate([main_live, last_live[None]], 0)
     live_rows = live.shape[0]

time: 248 us -> 248 us (level)
  waiting for transfers between devices: 100 us -> 90 us
  other arithmetic: 2.31 us -> 9.82 us
  local copies, waits for them, and re-layouts: 21.5 us -> 24.2 us
    concatenate x0 -> x1, other arithmetic: none -> 7.52 us  [shards(): jnp.concatenate([w_key_parts, w_value_parts], axis=2)]
    all_to_all x1, waiting for transfers between devices: 8.38 us -> 0.86 us  [last_token(): lax.all_to_all(mixed_rows.reshape(tensor_count, heads_count, col_count),...]
    gather x1 -> x2, local copies, waits for them, and re-layouts: 2.8 us -> 6.44 us  [the longest x1 3.69 us: shards(): jnp.take(arrived_rows, arrived_slot[:main_rows], axis=0, mode='clip')]
    all_to_all x1, waiting for transfers between devices: 8.44 us -> 5.69 us  [last_token(): lax.all_to_all(spread_query.reshape(heads_count, tensor_count, col_count)...]
  transfers between devices with their start and end apart: 5 -> 5, of which waited for: 4 -> 4; matrix products, arithmetic and copies ran while one was open for 12% -> 16% of each run, Pallas kernels for 0% -> 0%
where the time goes in v5:
time: 248 us; the launch traced here: 247 us
  waiting for transfers between devices  90 us (36%)
  blocking collectives  67.8 us (27%)
  matrix products  25.4 us (10%)
  local copies, waits for them, and re-layouts  24.2 us (10%)
  starting transfers between devices  16.4 us (7%)
  between operations  13.6 us (5%)
  other arithmetic  9.82 us (4%)
    all_to_all x1, waiting for transfers between devices, shards(): lax.all_to_all(outgoing, 'dp', split_axis=0, concat_axis=0, tiled=True)  49.6 us
    all_to_all x1, blocking collectives, shards(): lax.all_to_all(partial_out, 'tensor', split_axis=0, concat_axis=0, tiled=...  45.1 us
    all_gather x1, waiting for transfers between devices, shards(): main_parts = lax.all_gather(head_rows, 'tensor', axis=0, tiled=False)  33.8 us
    all_to_all x1, blocking collectives, last_token(): lax.all_to_all(jnp.broadcast_to(partial_scores[None], (tensor_count,) + p...  13.2 us
    dot_general x1, matrix products, shards(): jnp.einsum('snkf,sfc->nkc', main_parts, w_both, preferred_element_type=jn...  12 us
    all_to_all x1, blocking collectives, shards(): lax.all_to_all(request_table, 'dp', split_axis=0, concat_axis=0, tiled=True)  9.49 us
    all_to_all x1, starting transfers between devices, last_token(): lax.all_to_all(spread_query.reshape(heads_count, tensor_count, col_count)...  8.26 us
    concatenate x1, other arithmetic, shards(): jnp.concatenate([w_key_parts, w_value_parts], axis=2)  7.52 us
  transfers between devices with their start and end apart: 5, of which 4 were waited for; matrix products, arithmetic and copies ran while one was open for 16% of the time, Pallas kernels for 0%

profile of v5, /device:TPU:0, one launch (start us, length us, event | category | flops | bytes accessed | tf_op | source)
XLA Modules:
  0.0 247.2 jit_solution(13575457344271221068)
XLA Ops:
  6.5 0.0 all-gather.8.cloned.1.call-start
  6.5 1.7 slice_bitcast_fusion
  8.2 0.0 all-gather.8.cloned.1.call-update
  8.2 0.8 copy.32
  9.0 0.1 reshape.262
  9.1 0.2 convert_reduce_fusion
  9.3 0.1 iota_compare_fusion.1
  9.4 0.1 select_reduce_fusion
  9.4 0.1 copy.33
  9.5 9.5 %all_to_all.44 = s32[8,1,4]{2,1,0:T(1,128)S(1)} all-to-all(s32[8,1,4]{2,1,0:T(1,128)S(1)} %copy.33), channel_id=1, replica_groups=mesh['dp'=8,'tensor'=16] {'dp'}, dimensions={0} | all-to-all | bytes 256 | tf_op jit(solution)/shard_map/all_to_all | solution.py:115
  19.0 0.6 broadcast.228
  19.6 0.7 reduce.4
  20.3 0.1 reshape.279
  20.4 5.1 %gather_fusion = bf16[32,128,512]{2,1,0:T(8,128)(2,1)} fusion(bf16[32,128,512]{2,1,0:T(8,128)(2,1)} %param.9, s32[1024]{0:T(1024)S(1)} %pad_clamp_fusion.2), kind=kCustom, calls=%fused_computation | custom fusion | bytes 8388736 | tf_op jit(solution)/shard_map/jit(_take)/gather | solution.py:116
  25.5 4.6 %all-to-all-start.1 = ((bf16[8,4,128,512]{3,2,1,0:T(8,128)(2,1)}), bf16[8,4,128,512]{3,2,1,0:T(8,128)(2,1)}, u32[]{:S(2)}, u32[]{:S(2)}) async-start(bf16[8,4,128,512]{3,2,1,0:T(8,128)(2,1)} %bitcast.85), calls=%async_computation.1 | async-start | bytes 8388608 | tf_op jit(solution)/shard_map/all_to_all | solution.py:119
  30.1 0.0 all-gather.6.cloned.1.call-start
  30.2 49.6 %all-to-all-done.1 = bf16[8,4,128,512]{3,2,1,0:T(8,128)(2,1)} async-done(((bf16[8,4,128,512]{3,2,1,0:T(8,128)(2,1)}), bf16[8,4,128,512]{3,2,1,0:T(8,128)(2,1)}, u32[]{:S(2)}, u32[]{:S(2)}) %all-to-all-start.1) | async-done | bytes 4194336 | tf_op jit(solution)/shard_map/all_to_all | solution.py:119
  79.7 3.7 %gather_fusion.1 = bf16[6,128,512]{2,1,0:T(8,128)(2,1)} fusion(bf16[32,128,512]{2,1,0:T(8,128)(2,1)} %bitcast.2, s32[1024]{0:T(1024)S(1)} %pad_clamp_fusion.1), kind=kCustom, calls=%fused_computation.1 | custom fusion | bytes 1572888 | tf_op jit(solution)/shard_map/jit(_take)/gather | solution.py:123
  83.4 0.0 all-gather.6.cloned.1.call-update
  83.4 0.1 slice.27
  83.5 6.4 %copy.48 = bf16[8192,256]{0,1:T(8,128)(2,1)} copy(bf16[8192,256]{1,0:T(8,128)(2,1)} %param.11) | data formatting | bytes 8388608 | tf_op jit(solution)/shard_map/reshape | solution.py:39
  89.9 0.0 all-gather.8.cloned.1.call-done
  89.9 0.0 copy-start
  89.9 4.4 %fusion.15 = bf16[193,256]{1,0:T(8,128)(2,1)S(1)} fusion(bf16[16,193,512]{2,1,0:T(8,128)(2,1)} %all-gather.8.cloned.1.call-done, bf16[16,512,256]{2,1,0:T(8,128)(2,1)} %bitcast.88), kind=kOutput, calls=%fused_computation.19 | convolution fusion | flops 809550080 | bytes 7455232 | tf_op jit(solution)/shard_map/srf,sfc->rc/dot_general | solution.py:97
  94.3 0.3 copy-done
  94.6 0.7 fusion.28
  95.2 0.7 copy.44
  95.9 8.3 %all-to-all-start.2 = ((f32[2,16,512]{2,0,1:T(2,128)}), f32[2,16,512]{2,0,1:T(2,128)S(1)}, u32[]{:S(2)}, u32[]{:S(2)}) async-start(f32[2,16,512]{2,0,1:T(2,128)} %bitcast.16), calls=%async_computation.2 | async-start | bytes 131072 | tf_op jit(solution)/shard_map/all_to_all | solution.py:43
  104.2 2.8 %gather_fusion.2 = bf16[2,128,512]{2,1,0:T(8,128)(2,1)S(1)} fusion(bf16[32,128,512]{2,1,0:T(8,128)(2,1)} %bitcast.2, s32[1024]{0:T(1024)S(1)} %pad_clamp_fusion), kind=kCustom, calls=%fused_computation.2 | custom fusion | bytes 524296 | tf_op jit(solution)/shard_map/jit(_take)/gather | solution.py:124
  107.0 5.7 %all-to-all-done.2 = f32[2,16,512]{2,0,1:T(2,128)S(1)} async-done(((f32[2,16,512]{2,0,1:T(2,128)}), f32[2,16,512]{2,0,1:T(2,128)S(1)}, u32[]{:S(2)}, u32[]{:S(2)}) %all-to-all-start.2) | async-done | bytes 65568 | tf_op jit(solution)/shard_map/all_to_all | solution.py:43
  112.7 0.3 fusion.33
  113.1 13.2 %all_to_all.45 = f32[16,32,256]{2,1,0:T(8,128)S(1)} all-to-all(f32[16,32,256]{2,1,0:T(8,128)S(1)} %broadcast_in_dim.17), channel_id=1, replica_groups=mesh['dp'=8,'tensor'=16] {'tensor'}, dimensions={0} | all-to-all | bytes 1048576 | tf_op jit(solution)/shard_map/all_to_all | solution.py:53
  126.3 0.1 multiply_reduce_fusion
  126.4 0.2 fusion.24
  126.6 0.1 divide_convert_fusion.2
  126.8 0.1 fusion.25
  126.9 0.7 copy.39
  127.6 3.5 %all-to-all-start.4 = ((f32[16,2,512]{2,1,0:T(2,128)}), f32[16,2,512]{2,1,0:T(2,128)S(1)}, u32[]{:S(2)}, u32[]{:S(2)}) async-start(f32[16,2,512]{2,1,0:T(2,128)} %copy.39), calls=%async_computation.4 | async-start | bytes 131072 | tf_op jit(solution)/shard_map/all_to_all | solution.py:65
  131.1 7.5 %pad_maximum_fusion = bf16[16,512,512]{2,1,0:T(8,128)(2,1)} fusion(bf16[16,512,256]{2,1,0:T(8,128)(2,1)} %bitcast.90, bf16[16,512,256]{2,1,0:T(8,128)(2,1)} %bitcast.87), kind=kLoop, calls=%fused_computation.4 | loop fusion | flops 16777216 | bytes 16777216 | tf_op jit(solution)/shard_map/concatenate | solution.py:128
  138.7 0.9 all-to-all-done.4
  139.5 3.6 %fusion.6 = f32[2,1,128]{2,1,0:T(1,128)S(1)} fusion(f32[2,8192,1]{1,0,2:T(2,128)S(1)} %bitcast.96, bf16[8192,256]{1,0:T(8,128)(2,1)} %param.12), kind=kOutput, calls=%fused_computation.10 | convolution fusion | flops 25165824 | bytes 4260864 | tf_op jit(solution)/shard_map/hf,fhd->hd/dot_general | solution.py:73
  143.2 33.8 %all-gather.6.cloned.1.call-done = bf16[96,128,512]{2,1,0:T(8,128)(2,1)} async-done(((bf16[6,128,512]{2,1,0:T(8,128)(2,1)}), bf16[96,128,512]{2,1,0:T(8,128)(2,1)}) %all-gather.6.cloned.1.call-update) | async-done | bytes 12582928 | tf_op jit(solution)/shard_map/all_gather | solution.py:125
  177.0 12.0 %bitcast_convert_fusion = bf16[6,128,512]{2,1,0:T(8,128)(2,1)S(1)} fusion(bf16[16,6,128,512]{3,2,1,0:T(8,128)(2,1)} %bitcast.100, bf16[16,512,512]{2,1,0:T(8,128)(2,1)} %pad_maximum_fusion), kind=kOutput, calls=%fused_computation.14 | convolution fusion | flops 6442844160 | bytes 21757952 | tf_op jit(solution)/shard_map/snkf,sfc->nkc/dot_general | solution.py:129
  189.1 0.1 fusion.31
  189.2 0.1 reshape_reshape.7
  189.3 0.3 convolution_multiply_fusion
  189.5 0.2 fusion.32
  189.8 0.1 reshape_reshape.6
  189.9 0.7 fusion.16
  190.6 0.1 copy.37
  190.7 3.2 %convert_bitcast_fusion = bf16[16,193,512]{2,1,0:T(8,128)(2,1)S(1)} fusion(bf16[32,16,8,512]{3,2,1,0:T(8,128)(2,1)} %bitcast.89, bf16[1,256]{1,0:T(2,128)(2,1)S(1)} %bitcast.98, bf16[192,256]{1,0:T(8,128)(2,1)S(1)} %bitcast.93), kind=kOutput, calls=%fused_computation.13 | convolution fusion | flops 811279360 | bytes 7455232 | tf_op jit(solution)/shard_map/rc,csf->srf/dot_general | solution.py:143
  194.0 45.1 %all_to_all.46 = bf16[16,193,512]{2,1,0:T(8,128)(2,1)S(1)} all-to-all(bf16[16,193,512]{2,1,0:T(8,128)(2,1)S(1)} %convert_bitcast_fusion), channel_id=1, replica_groups=mesh['dp'=8,'tensor'=16] {'tensor'}, dimensions={0} | all-to-all | bytes 6324224 | tf_op jit(solution)/shard_map/all_to_all | solution.py:149
  239.0 0.5 reduce_sum.62
  239.6 0.8 concatenate.11
  (15 shorter events, 0.2 us)
Async XLA Ops:
  6.5 83.3 %all-gather.8.cloned.1.call-start = ((), (), s32[]{:S(2)}) async-start(), calls=%async_computation.7 | async-start | bytes 3481600 | tf_op jit(solution)/shard_map/all_gather | solution.py:96
  25.5 54.3 %all-to-all-start.1 = ((bf16[8,4,128,512]{3,2,1,0:T(8,128)(2,1)}), bf16[8,4,128,512]{3,2,1,0:T(8,128)(2,1)}, u32[]{:S(2)}, u32[]{:S(2)}) async-start(bf16[8,4,128,512]{3,2,1,0:T(8,128)(2,1)} %bitcast.85), calls=%async_computation.1 | async-start | bytes 8388608 | tf_op jit(solution)/shard_map/all_to_all | solution.py:119
  30.1 147.0 %all-gather.6.cloned.1.call-start = ((), (), s32[]{:S(2)}) async-start(), calls=%async_computation.6 | async-start | bytes 13369344 | tf_op jit(solution)/shard_map/all_gather | solution.py:125
  89.9 4.7 %copy-start = (bf16[8192,256]{0,1:T(8,128)(2,1)S(1)}, bf16[8192,256]{0,1:T(8,128)(2,1)}, u32[]{:S(2)}) copy-start(bf16[8192,256]{0,1:T(8,128)(2,1)} %copy.48) | copy-start | bytes 12582916
  95.9 16.7 %all-to-all-start.2 = ((f32[2,16,512]{2,0,1:T(2,128)}), f32[2,16,512]{2,0,1:T(2,128)S(1)}, u32[]{:S(2)}, u32[]{:S(2)}) async-start(f32[2,16,512]{2,0,1:T(2,128)} %bitcast.16), calls=%async_computation.2 | async-start | bytes 131072 | tf_op jit(solution)/shard_map/all_to_all | solution.py:43
  127.6 11.9 %all-to-all-start.4 = ((f32[16,2,512]{2,1,0:T(2,128)}), f32[16,2,512]{2,1,0:T(2,128)S(1)}, u32[]{:S(2)}, u32[]{:S(2)}) async-start(f32[16,2,512]{2,1,0:T(2,128)} %copy.39), calls=%async_computation.4 | async-start | bytes 131072 | tf_op jit(solution)/shard_map/all_to_all | solution.py:65
Sparse Core Ops, SparseCore 0:
  9.5 50.8 all-gather.7
  83.6 93.4 all-gather.5

commit v6 on v5

--- a/solution.py
+++ b/solution.py
@@ -122,32 +122,43 @@
     main_rows = per_reader - 2
     head_rows = jnp.take(arrived_rows, arrived_slot[:main_rows], axis=0, mode="clip")
     tail_rows = jnp.take(arrived_rows, arrived_slot[main_rows:], axis=0, mode="clip")
-    main_parts = lax.all_gather(head_rows, "tensor", axis=0, tiled=False)
     w_key_parts = w_key.reshape(tensor_count, col_count, head_cols)
     w_value_parts = w_value.reshape(tensor_count, col_count, head_cols)
     w_both = lax.optimization_barrier(jnp.concatenate([w_key_parts, w_value_parts], axis=2))
-    both_rows = jnp.einsum(
-        "snkf,sfc->nkc", main_parts, w_both, preferred_element_type=jnp.float32
-    ).astype(jnp.bfloat16)
-    key_rows = both_rows[..., :head_cols].reshape(main_rows * ret_len, head_cols)
-    value_rows = both_rows[..., head_cols:].reshape(main_rows * ret_len, head_cols)
-    main_groups = main_rows // 2
-    main_live = attend(
-        query_rows[: main_groups * group_len], key_rows, value_rows, heads_local, group_len, main_groups
+    w_out_parts = w_out.reshape(head_cols, tensor_count, -1)
+    last_live = last_token(
+        query_rows[(main_rows // 2) * group_len], tail_rows, w_key, w_value, heads_local
     )
-    last_live = last_token(
-        query_rows[main_groups * group_len], tail_rows, w_key, w_value, heads_local
-    )
-    live = jnp.concatenate([main_live, last_live[None]], 0)
-    live_rows = live.shape[0]
-    partial_out = jnp.einsum(
-        "rc,csf->srf",
-        live,
-        w_out.reshape(head_cols, tensor_count, -1),
-        preferred_element_type=jnp.float32,
-    ).astype(jnp.bfloat16)
-    spread = lax.all_to_all(partial_out, "tensor", split_axis=0, concat_axis=0, tiled=True)
-    summed = jnp.sum(spread.astype(jnp.float32), axis=0).astype(jnp.bfloat16)
+
+    def stage(rows, first_group, extra):
+        stage_rows = rows.shape[0]
+        parts = lax.all_gather(rows, "tensor", axis=0, tiled=False)
+        both_rows = jnp.einsum(
+            "snkf,sfc->nkc", parts, w_both, preferred_element_type=jnp.float32
+        ).astype(jnp.bfloat16)
+        key_rows = both_rows[..., :head_cols].reshape(stage_rows * ret_len, head_cols)
+        value_rows = both_rows[..., head_cols:].reshape(stage_rows * ret_len, head_cols)
+        groups = stage_rows // 2
+        context = attend(
+            query_rows[first_group * group_len : (first_group + groups) * group_len],
+            key_rows,
+            value_rows,
+            heads_local,
+            group_len,
+            groups,
+        )
+        if extra is not None:
+            context = jnp.concatenate([context, extra[None]], 0)
+        partial_out = jnp.einsum(
+            "rc,csf->srf", context, w_out_parts, preferred_element_type=jnp.float32
+        ).astype(jnp.bfloat16)
+        spread = lax.all_to_all(partial_out, "tensor", split_axis=0, concat_axis=0, tiled=True)
+        return jnp.sum(spread.astype(jnp.float32), axis=0).astype(jnp.bfloat16)
+
+    first_rows = ((main_rows // 2 + 1) // 2) * 2
+    second_sum = stage(head_rows[first_rows:], first_rows // 2, last_live)
+    first_sum = stage(head_rows[:first_rows], 0, None)
+    summed = jnp.concatenate([first_sum, second_sum], 0)
     return jnp.concatenate([jnp.zeros((group_len - 1, summed.shape[1]), jnp.bfloat16), summed], 0)
 
 

time: 248 us -> 283 us (1.14)
  waiting for transfers between devices: 90 us -> 139 us
  blocking collectives: 67.8 us -> 29.9 us
  starting transfers between devices: 16.4 us -> 28.5 us
  matrix products: 25.4 us -> 36.5 us
    all_to_all x1 -> x0, blocking collectives: 45.1 us -> none  [shards(): lax.all_to_all(partial_out, 'tensor', split_axis=0, concat_axis=0, tiled=...]
    all_to_all x0 -> x2, waiting for transfers between devices: none -> 31.1 us  [stage(): lax.all_to_all(partial_out, 'tensor', split_axis=0, concat_axis=0, tiled=...]
    all_gather x1 -> x2, waiting for transfers between devices: 33.8 us -> 53.5 us  [stage(): parts = lax.all_gather(rows, 'tensor', axis=0, tiled=False)]
    all_to_all x0 -> x2, starting transfers between devices: none -> 12.3 us  [stage(): lax.all_to_all(partial_out, 'tensor', split_axis=0, concat_axis=0, tiled=...]
    dot_general x2 -> x4, matrix products: 15.3 us -> 26.2 us  [the longest x2 17.8 us: stage(): jnp.einsum('snkf,sfc->nkc', parts, w_both, preferred_element_type=jnp.flo...]
    all_to_all x1, blocking collectives: 13.2 us -> 20.4 us  [last_token(): lax.all_to_all(jnp.broadcast_to(partial_scores[None], (tensor_count,) + p...]
  transfers between devices with their start and end apart: 5 -> 8, of which waited for: 4 -> 5; matrix products, arithmetic and copies ran while one was open for 16% -> 24% of each run, Pallas kernels for 0% -> 0%
where the time goes in v6:
time: 283 us; the launch traced here: 282 us
  waiting for transfers between devices  139 us (49%)
  matrix products  36.5 us (13%)
  blocking collectives  29.9 us (11%)
  starting transfers between devices  28.5 us (10%)
  local copies, waits for them, and re-layouts  23.8 us (8%)
  between operations  13.4 us (5%)
  other arithmetic  10.6 us (4%)
    all_gather x2, waiting for transfers between devices, stage(): parts = lax.all_gather(rows, 'tensor', axis=0, tiled=False)  53.5 us
    all_to_all x1, waiting for transfers between devices, shards(): lax.all_to_all(outgoing, 'dp', split_axis=0, concat_axis=0, tiled=True)  49.6 us
    all_to_all x2, waiting for transfers between devices, stage(): lax.all_to_all(partial_out, 'tensor', split_axis=0, concat_axis=0, tiled=...  31.1 us
    all_to_all x1, blocking collectives, last_token(): lax.all_to_all(jnp.broadcast_to(partial_scores[None], (tensor_count,) + p...  20.4 us
    dot_general x2, matrix products, stage(): jnp.einsum('snkf,sfc->nkc', parts, w_both, preferred_element_type=jnp.flo...  17.8 us
    all_to_all x2, starting transfers between devices, stage(): lax.all_to_all(partial_out, 'tensor', split_axis=0, concat_axis=0, tiled=...  12.3 us
    all_to_all x1, blocking collectives, shards(): lax.all_to_all(request_table, 'dp', split_axis=0, concat_axis=0, tiled=True)  9.49 us
    dot_general x2, matrix products, stage(): jnp.einsum('rc,csf->srf', context, w_out_parts, preferred_element_type=jn...  8.41 us
  transfers between devices with their start and end apart: 8, of which 5 were waited for; matrix products, arithmetic and copies ran while one was open for 24% of the time, Pallas kernels for 0%

profile of v6, /device:TPU:0, one launch (start us, length us, event | category | flops | bytes accessed | tf_op | source)
XLA Modules:
  0.0 282.0 jit_solution(11440655834155640172)
XLA Ops:
  6.5 1.7 slice_bitcast_fusion
  8.2 0.0 all-gather.12.cloned.1.call-update
  8.2 0.8 copy.47
  9.0 0.1 reshape.298
  9.1 0.2 convert_reduce_fusion
  9.3 0.1 iota_compare_fusion.1
  9.4 0.1 select_reduce_fusion
  9.5 0.1 copy.48
  9.5 9.5 %all_to_all.49 = s32[8,1,4]{2,1,0:T(1,128)S(1)} all-to-all(s32[8,1,4]{2,1,0:T(1,128)S(1)} %copy.48), channel_id=1, replica_groups=mesh['dp'=8,'tensor'=16] {'dp'}, dimensions={0} | all-to-all | bytes 256 | tf_op jit(solution)/shard_map/all_to_all | solution.py:115
  19.0 0.5 broadcast.236
  19.5 0.7 reduce.9
  20.2 0.1 reshape.319
  20.3 5.1 %gather_fusion = bf16[32,128,512]{2,1,0:T(8,128)(2,1)} fusion(bf16[32,128,512]{2,1,0:T(8,128)(2,1)} %param.9, s32[1024]{0:T(1024)S(1)} %pad_clamp_fusion.2), kind=kCustom, calls=%fused_computation | custom fusion | bytes 8388736 | tf_op jit(solution)/shard_map/jit(_take)/gather | solution.py:116
  25.4 4.6 %all-to-all-start.1 = ((bf16[8,4,128,512]{3,2,1,0:T(8,128)(2,1)}), bf16[8,4,128,512]{3,2,1,0:T(8,128)(2,1)}, u32[]{:S(2)}, u32[]{:S(2)}) async-start(bf16[8,4,128,512]{3,2,1,0:T(8,128)(2,1)} %bitcast.125), calls=%async_computation.1 | async-start | bytes 8388608 | tf_op jit(solution)/shard_map/all_to_all | solution.py:119
  30.0 0.0 all-gather.10.cloned.1.call-start
  30.1 49.6 %all-to-all-done.1 = bf16[8,4,128,512]{3,2,1,0:T(8,128)(2,1)} async-done(((bf16[8,4,128,512]{3,2,1,0:T(8,128)(2,1)}), bf16[8,4,128,512]{3,2,1,0:T(8,128)(2,1)}, u32[]{:S(2)}, u32[]{:S(2)}) %all-to-all-start.1) | async-done | bytes 4194336 | tf_op jit(solution)/shard_map/all_to_all | solution.py:119
  79.6 2.8 gather_fusion.1
  82.4 0.7 slice.59
  83.1 0.0 all-gather.10.cloned.1.call-update
  83.2 0.0 all-gather.8.cloned.1.call-start
  83.2 0.8 slice.55
  84.0 0.0 all-gather.8.cloned.1.call-update
  84.0 0.1 slice.47
  84.1 6.4 %copy.68 = bf16[8192,256]{0,1:T(8,128)(2,1)} copy(bf16[8192,256]{1,0:T(8,128)(2,1)} %param.11) | data formatting | bytes 8388608 | tf_op jit(solution)/shard_map/reshape | solution.py:39
  90.5 4.5 %fusion.38 = bf16[193,256]{1,0:T(8,128)(2,1)S(1)} fusion(bf16[16,193,512]{2,1,0:T(8,128)(2,1)} %all-gather.12.cloned.1.call-done, bf16[16,512,256]{2,1,0:T(8,128)(2,1)} %bitcast.128), kind=kOutput, calls=%fused_computation.31 | convolution fusion | flops 809550080 | bytes 7455232 | tf_op jit(solution)/shard_map/srf,sfc->rc/dot_general | solution.py:97
  95.0 0.1 copy-done
  95.1 0.7 fusion.58
  95.7 0.7 copy.64
  96.4 8.1 %all-to-all-start.3 = ((f32[2,16,512]{2,0,1:T(2,128)}), f32[2,16,512]{2,0,1:T(2,128)S(1)}, u32[]{:S(2)}, u32[]{:S(2)}) async-start(f32[2,16,512]{2,0,1:T(2,128)} %bitcast.22), calls=%async_computation.3 | async-start | bytes 131072 | tf_op jit(solution)/shard_map/all_to_all | solution.py:43
  104.5 2.8 gather_fusion.2
  107.3 4.9 %all-to-all-done.3 = f32[2,16,512]{2,0,1:T(2,128)S(1)} async-done(((f32[2,16,512]{2,0,1:T(2,128)}), f32[2,16,512]{2,0,1:T(2,128)S(1)}, u32[]{:S(2)}, u32[]{:S(2)}) %all-to-all-start.3) | async-done | bytes 65568 | tf_op jit(solution)/shard_map/all_to_all | solution.py:43
  112.2 0.3 fusion.66
  112.6 20.4 %all_to_all.50 = f32[16,32,256]{2,1,0:T(8,128)S(1)} all-to-all(f32[16,32,256]{2,1,0:T(8,128)S(1)} %broadcast_in_dim.20), channel_id=1, replica_groups=mesh['dp'=8,'tensor'=16] {'tensor'}, dimensions={0} | all-to-all | bytes 1048576 | tf_op jit(solution)/shard_map/all_to_all | solution.py:53
  133.0 0.1 multiply_reduce_fusion
  133.1 0.2 fusion.54
  133.3 0.1 divide_convert_fusion.4
  133.5 0.1 fusion.55
  133.6 0.7 copy.59
  134.3 3.5 %all-to-all-start.5 = ((f32[16,2,512]{2,1,0:T(2,128)}), f32[16,2,512]{2,1,0:T(2,128)S(1)}, u32[]{:S(2)}, u32[]{:S(2)}) async-start(f32[16,2,512]{2,1,0:T(2,128)} %copy.59), calls=%async_computation.5 | async-start | bytes 131072 | tf_op jit(solution)/shard_map/all_to_all | solution.py:65
  137.8 7.4 %pad_maximum_fusion = bf16[16,512,512]{2,1,0:T(8,128)(2,1)} fusion(bf16[16,512,256]{2,1,0:T(8,128)(2,1)} %bitcast.129, bf16[16,512,256]{2,1,0:T(8,128)(2,1)} %bitcast.127), kind=kLoop, calls=%fused_computation.5 | loop fusion | flops 16777216 | bytes 16777216 | tf_op jit(solution)/shard_map/concatenate | solution.py:127
  145.2 0.2 all-to-all-done.5
  145.4 3.5 %fusion.6 = f32[2,1,128]{2,1,0:T(1,128)S(1)} fusion(f32[2,8192,1]{1,0,2:T(2,128)S(1)} %bitcast.135, bf16[8192,256]{1,0:T(8,128)(2,1)} %param.12), kind=kOutput, calls=%fused_computation.10 | convolution fusion | flops 25165824 | bytes 4260864 | tf_op jit(solution)/shard_map/hf,fhd->hd/dot_general | solution.py:73
  149.0 0.0 all-gather.10.cloned.1.call-done
  149.0 7.5 %fusion.33 = bf16[2,128,512]{2,1,0:T(8,128)(2,1)S(1)} fusion(bf16[16,2,128,512]{3,2,1,0:T(8,128)(2,1)} %bitcast.140, bf16[16,512,512]{2,1,0:T(8,128)(2,1)} %pad_maximum_fusion), kind=kOutput, calls=%fused_computation.26 | convolution fusion | flops 2147614720 | bytes 12845056 | tf_op jit(solution)/shard_map/snkf,sfc->nkc/dot_general | solution.py:136
  156.6 0.2 convolution_multiply_fusion.1
  156.8 0.2 fusion.64
  157.0 0.3 fusion.41
  157.4 4.1 %fusion.20 = bf16[16,65,512]{2,1,0:T(8,128)(2,1)} fusion(bf16[32,16,8,512]{3,2,1,0:T(8,128)(2,1)} %bitcast.123, bf16[1,256]{1,0:T(2,128)(2,1)S(1)} %bitcast.137, bf16[64,256]{1,0:T(8,128)(2,1)S(1)} %bitcast.133), kind=kOutput, calls=%fused_computation.21 | convolution fusion | flops 273228800 | bytes 5292544 | tf_op jit(solution)/shard_map/rc,csf->srf/dot_general | solution.py:152
  161.5 7.0 %all-to-all-start.6 = ((bf16[16,65,512]{2,1,0:T(8,128)(2,1)}), bf16[16,65,512]{2,1,0:T(8,128)(2,1)S(1)}, u32[]{:S(2)}, u32[]{:S(2)}) async-start(bf16[16,65,512]{2,1,0:T(8,128)(2,1)} %fusion.20), calls=%async_computation.6 | async-start | bytes 2359296 | tf_op jit(solution)/shard_map/all_to_all | solution.py:155
  168.5 53.5 %all-gather.8.cloned.1.call-done = bf16[64,128,512]{2,1,0:T(8,128)(2,1)} async-done(((bf16[4,128,512]{2,1,0:T(8,128)(2,1)}), bf16[64,128,512]{2,1,0:T(8,128)(2,1)}) %all-gather.8.cloned.1.call-update) | async-done | bytes 8388624 | tf_op jit(solution)/shard_map/all_gather | solution.py:135
  222.0 10.2 %fusion.26 = bf16[4,128,512]{2,1,0:T(8,128)(2,1)S(1)} fusion(bf16[16,4,128,512]{3,2,1,0:T(8,128)(2,1)} %bitcast.139, bf16[16,512,512]{2,1,0:T(8,128)(2,1)} %pad_maximum_fusion), kind=kOutput, calls=%fused_computation.23 | convolution fusion | flops 4295229440 | bytes 17301504 | tf_op jit(solution)/shard_map/snkf,sfc->nkc/dot_general | solution.py:136
  232.3 0.1 reshape_reshape.9
  232.4 0.1 reshape_reshape.8
  232.4 0.2 convolution_multiply_fusion
  232.7 0.2 fusion.65
  232.9 0.5 fusion.40
  233.4 0.1 copy.52
  233.5 4.3 %convert_bitcast_fusion = bf16[16,128,512]{2,1,0:T(8,128)(2,1)} fusion(bf16[128,256,1]{1,0,2:T(8,128)(2,1)S(1)} %reshape.353, bf16[32,16,8,512]{3,2,1,0:T(8,128)(2,1)} %bitcast.124), kind=kOutput, calls=%fused_computation.19 | convolution fusion | flops 537919488 | bytes 6356992 | tf_op jit(solution)/shard_map/rc,csf->srf/dot_general | solution.py:152
  237.8 0.0 all-to-all-done.6
  237.8 5.3 %all-to-all-start.2 = ((bf16[16,128,512]{2,1,0:T(8,128)(2,1)}), bf16[16,128,512]{2,1,0:T(8,128)(2,1)S(1)}, u32[]{:S(2)}, u32[]{:S(2)}) async-start(bf16[16,128,512]{2,1,0:T(8,128)(2,1)} %convert_bitcast_fusion), calls=%async_computation.2 | async-start | bytes 4194304 | tf_op jit(solution)/shard_map/all_to_all | solution.py:155
  243.1 0.2 reduce_sum.85
  243.3 31.1 %all-to-all-done.2 = bf16[16,128,512]{2,1,0:T(8,128)(2,1)S(1)} async-done(((bf16[16,128,512]{2,1,0:T(8,128)(2,1)}), bf16[16,128,512]{2,1,0:T(8,128)(2,1)S(1)}, u32[]{:S(2)}, u32[]{:S(2)}) %all-to-all-start.2) | async-done | bytes 2097184 | tf_op jit(solution)/shard_map/all_to_all | solution.py:155
  274.4 0.3 reduce_sum.81
  274.7 0.8 pad_maximum_fusion.1
  (26 shorter events, 0.5 us)
Async XLA Ops:
  6.5 83.9 %all-gather.12.cloned.1.call-start = ((), (), s32[]{:S(2)}) async-start(), calls=%async_computation.9 | async-start | bytes 3481600 | tf_op jit(solution)/shard_map/all_gather | solution.py:96
  25.4 54.3 %all-to-all-start.1 = ((bf16[8,4,128,512]{3,2,1,0:T(8,128)(2,1)}), bf16[8,4,128,512]{3,2,1,0:T(8,128)(2,1)}, u32[]{:S(2)}, u32[]{:S(2)}) async-start(bf16[8,4,128,512]{3,2,1,0:T(8,128)(2,1)} %bitcast.125), calls=%async_computation.1 | async-start | bytes 8388608 | tf_op jit(solution)/shard_map/all_to_all | solution.py:119
  30.0 119.0 %all-gather.10.cloned.1.call-start = ((), (), s32[]{:S(2)}) async-start(), calls=%async_computation.8 | async-start | bytes 4456448 | tf_op jit(solution)/shard_map/all_gather | solution.py:135
  83.2 138.9 %all-gather.8.cloned.1.call-start = ((), (), s32[]{:S(2)}) async-start(), calls=%async_computation.7 | async-start | bytes 8912896 | tf_op jit(solution)/shard_map/all_gather | solution.py:135
  90.5 4.6 %copy-start = (bf16[8192,256]{0,1:T(8,128)(2,1)S(1)}, bf16[8192,256]{0,1:T(8,128)(2,1)}, u32[]{:S(2)}) copy-start(bf16[8192,256]{0,1:T(8,128)(2,1)} %copy.68) | copy-start | bytes 12582916
  96.4 15.7 %all-to-all-start.3 = ((f32[2,16,512]{2,0,1:T(2,128)}), f32[2,16,512]{2,0,1:T(2,128)S(1)}, u32[]{:S(2)}, u32[]{:S(2)}) async-start(f32[2,16,512]{2,0,1:T(2,128)} %bitcast.22), calls=%async_computation.3 | async-start | bytes 131072 | tf_op jit(solution)/shard_map/all_to_all | solution.py:43
  134.3 11.1 %all-to-all-start.5 = ((f32[16,2,512]{2,1,0:T(2,128)}), f32[16,2,512]{2,1,0:T(2,128)S(1)}, u32[]{:S(2)}, u32[]{:S(2)}) async-start(f32[16,2,512]{2,1,0:T(2,128)} %copy.59), calls=%async_computation.5 | async-start | bytes 131072 | tf_op jit(solution)/shard_map/all_to_all | solution.py:65
  161.5 76.3 %all-to-all-start.6 = ((bf16[16,65,512]{2,1,0:T(8,128)(2,1)}), bf16[16,65,512]{2,1,0:T(8,128)(2,1)S(1)}, u32[]{:S(2)}, u32[]{:S(2)}) async-start(bf16[16,65,512]{2,1,0:T(8,128)(2,1)} %fusion.20), calls=%async_computation.6 | async-start | bytes 2359296 | tf_op jit(solution)/shard_map/all_to_all | solution.py:155
  237.8 36.6 %all-to-all-start.2 = ((bf16[16,128,512]{2,1,0:T(8,128)(2,1)}), bf16[16,128,512]{2,1,0:T(8,128)(2,1)S(1)}, u32[]{:S(2)}, u32[]{:S(2)}) async-start(bf16[16,128,512]{2,1,0:T(8,128)(2,1)} %convert_bitcast_fusion), calls=%async_computation.2 | async-start | bytes 4194304 | tf_op jit(solution)/shard_map/all_to_all | solution.py:155
Sparse Core Ops, SparseCore 0:
  9.5 50.9 all-gather.11
  83.3 57.7 all-gather.9
  143.2 78.7 all-gather.7

commit v7 on v5

--- a/solution.py
+++ b/solution.py
@@ -2,6 +2,8 @@
 import jax.numpy as jnp
 from jax import lax
 from jax.sharding import PartitionSpec as P
+from jax.experimental import pallas as pl
+from jax.experimental.pallas import tpu as pltpu
 
 HD = 128
 
@@ -80,6 +82,28 @@
     return context.astype(jnp.bfloat16).reshape(-1)
 
 
+def project_kernel(parts_ref, weight_ref, out_ref):
+    total = jnp.dot(parts_ref[0, 0], weight_ref[0], preferred_element_type=jnp.float32)
+    for part in range(1, parts_ref.shape[0]):
+        total += jnp.dot(parts_ref[part, 0], weight_ref[part], preferred_element_type=jnp.float32)
+    out_ref[0] = total.astype(out_ref.dtype)
+
+
+def project(parts, weight):
+    part_count, rows, ret_len, col_count = parts.shape
+    out_cols = weight.shape[2]
+    return pl.pallas_call(
+        project_kernel,
+        out_shape=jax.ShapeDtypeStruct((rows, ret_len, out_cols), jnp.bfloat16),
+        grid=(rows,),
+        in_specs=[
+            pl.BlockSpec((part_count, 1, ret_len, col_count), lambda n: (0, n, 0, 0)),
+            pl.BlockSpec(memory_space=pltpu.VMEM),
+        ],
+        out_specs=pl.BlockSpec((1, ret_len, out_cols), lambda n: (n, 0, 0)),
+    )(parts, weight)
+
+
 def shards(hidden, neighbour_ids, database, w_query, w_key, w_value, w_out):
     dp_count = lax.axis_size("dp")
     tok_rows = hidden.shape[0]
@@ -126,9 +150,7 @@
     w_key_parts = w_key.reshape(tensor_count, col_count, head_cols)
     w_value_parts = w_value.reshape(tensor_count, col_count, head_cols)
     w_both = lax.optimization_barrier(jnp.concatenate([w_key_parts, w_value_parts], axis=2))
-    both_rows = jnp.einsum(
-        "snkf,sfc->nkc", main_parts, w_both, preferred_element_type=jnp.float32
-    ).astype(jnp.bfloat16)
+    both_rows = project(main_parts, w_both)
     key_rows = both_rows[..., :head_cols].reshape(main_rows * ret_len, head_cols)
     value_rows = both_rows[..., head_cols:].reshape(main_rows * ret_len, head_cols)
     main_groups = main_rows // 2

time: 248 us -> 250 us (level)
  Pallas kernels: 0 us -> 13.2 us
  matrix products: 25.4 us -> 13.3 us
    pallas_call x0 -> x1, Pallas kernels: none -> 13.2 us  [project(): pl.pallas_call(project_kernel, out_shape=jax.ShapeDtypeStruct((rows, ret_...]
    dot_general x1 -> x0, matrix products: 12 us -> none  [shards(): jnp.einsum('snkf,sfc->nkc', main_parts, w_both, preferred_element_type=jn...]
where the time goes in v7:
time: 250 us; the launch traced here: 249 us
  waiting for transfers between devices  90 us (36%)
  blocking collectives  67.8 us (27%)
  local copies, waits for them, and re-layouts  25.3 us (10%)
  starting transfers between devices  16.4 us (7%)
  between operations  13.6 us (5%)
  matrix products  13.3 us (5%)
  Pallas kernels  13.2 us (5%)
  other arithmetic  9.82 us (4%)
    all_to_all x1, waiting for transfers between devices, shards(): lax.all_to_all(outgoing, 'dp', split_axis=0, concat_axis=0, tiled=True)  49.6 us
    all_to_all x1, blocking collectives, shards(): lax.all_to_all(partial_out, 'tensor', split_axis=0, concat_axis=0, tiled=...  45.1 us
    all_gather x1, waiting for transfers between devices, shards(): main_parts = lax.all_gather(head_rows, 'tensor', axis=0, tiled=False)  33.8 us
    all_to_all x1, blocking collectives, last_token(): lax.all_to_all(jnp.broadcast_to(partial_scores[None], (tensor_count,) + p...  13.2 us
    pallas_call x1, Pallas kernels, project(): pl.pallas_call(project_kernel, out_shape=jax.ShapeDtypeStruct((rows, ret_...  13.2 us
    all_to_all x1, blocking collectives, shards(): lax.all_to_all(request_table, 'dp', split_axis=0, concat_axis=0, tiled=True)  9.49 us
    all_to_all x1, starting transfers between devices, last_token(): lax.all_to_all(spread_query.reshape(heads_count, tensor_count, col_count)...  8.26 us
    concatenate x1, other arithmetic, shards(): jnp.concatenate([w_key_parts, w_value_parts], axis=2)  7.52 us
  transfers between devices with their start and end apart: 5, of which 4 were waited for; matrix products, arithmetic and copies ran while one was open for 16% of the time, Pallas kernels for 0%

profile of v7, /device:TPU:0, one launch (start us, length us, event | category | flops | bytes accessed | tf_op | source)
XLA Modules:
  0.0 249.4 jit_solution(5891610126671848295)
XLA Ops:
  6.5 0.0 all-gather.8.cloned.1.call-start
  6.5 1.7 slice_bitcast_fusion
  8.2 0.0 all-gather.8.cloned.1.call-update
  8.2 0.8 copy.31
  9.0 0.1 reshape.262
  9.1 0.2 convert_reduce_fusion
  9.3 0.1 iota_compare_fusion.1
  9.4 0.1 select_reduce_fusion
  9.4 0.1 copy.32
  9.5 9.5 %all_to_all.44 = s32[8,1,4]{2,1,0:T(1,128)S(1)} all-to-all(s32[8,1,4]{2,1,0:T(1,128)S(1)} %copy.32), channel_id=1, replica_groups=mesh['dp'=8,'tensor'=16] {'dp'}, dimensions={0} | all-to-all | bytes 256 | tf_op jit(solution)/shard_map/all_to_all | solution.py:139
  19.0 0.6 broadcast.228
  19.6 0.7 reduce.4
  20.3 0.1 reshape.279
  20.4 5.1 %gather_fusion = bf16[32,128,512]{2,1,0:T(8,128)(2,1)} fusion(bf16[32,128,512]{2,1,0:T(8,128)(2,1)} %param.9, s32[1024]{0:T(1024)S(1)} %pad_clamp_fusion.2), kind=kCustom, calls=%fused_computation | custom fusion | bytes 8388736 | tf_op jit(solution)/shard_map/jit(_take)/gather | solution.py:140
  25.5 4.6 %all-to-all-start.1 = ((bf16[8,4,128,512]{3,2,1,0:T(8,128)(2,1)}), bf16[8,4,128,512]{3,2,1,0:T(8,128)(2,1)}, u32[]{:S(2)}, u32[]{:S(2)}) async-start(bf16[8,4,128,512]{3,2,1,0:T(8,128)(2,1)} %bitcast.75), calls=%async_computation.1 | async-start | bytes 8388608 | tf_op jit(solution)/shard_map/all_to_all | solution.py:143
  30.1 0.0 all-gather.6.cloned.1.call-start
  30.2 49.6 %all-to-all-done.1 = bf16[8,4,128,512]{3,2,1,0:T(8,128)(2,1)} async-done(((bf16[8,4,128,512]{3,2,1,0:T(8,128)(2,1)}), bf16[8,4,128,512]{3,2,1,0:T(8,128)(2,1)}, u32[]{:S(2)}, u32[]{:S(2)}) %all-to-all-start.1) | async-done | bytes 4194336 | tf_op jit(solution)/shard_map/all_to_all | solution.py:143
  79.7 3.7 %gather_fusion.1 = bf16[6,128,512]{2,1,0:T(8,128)(2,1)} fusion(bf16[32,128,512]{2,1,0:T(8,128)(2,1)} %bitcast.2, s32[1024]{0:T(1024)S(1)} %pad_clamp_fusion.1), kind=kCustom, calls=%fused_computation.1 | custom fusion | bytes 1572888 | tf_op jit(solution)/shard_map/jit(_take)/gather | solution.py:147
  83.4 0.0 all-gather.6.cloned.1.call-update
  83.4 0.1 slice.27
  83.5 6.4 %copy.46 = bf16[8192,256]{0,1:T(8,128)(2,1)} copy(bf16[8192,256]{1,0:T(8,128)(2,1)} %param.11) | data formatting | bytes 8388608 | tf_op jit(solution)/shard_map/reshape | solution.py:41
  89.9 0.0 all-gather.8.cloned.1.call-done
  89.9 0.0 copy-start
  89.9 4.4 %fusion.11 = bf16[193,256]{1,0:T(8,128)(2,1)S(1)} fusion(bf16[16,193,512]{2,1,0:T(8,128)(2,1)} %all-gather.8.cloned.1.call-done, bf16[16,512,256]{2,1,0:T(8,128)(2,1)} %bitcast.78), kind=kOutput, calls=%fused_computation.16 | convolution fusion | flops 809550080 | bytes 7455232 | tf_op jit(solution)/shard_map/srf,sfc->rc/dot_general | solution.py:121
  94.3 0.3 copy-done
  94.6 0.7 fusion.24
  95.2 0.7 copy.42
  95.9 8.3 %all-to-all-start.2 = ((f32[2,16,512]{2,0,1:T(2,128)}), f32[2,16,512]{2,0,1:T(2,128)S(1)}, u32[]{:S(2)}, u32[]{:S(2)}) async-start(f32[2,16,512]{2,0,1:T(2,128)} %bitcast.13), calls=%async_computation.2 | async-start | bytes 131072 | tf_op jit(solution)/shard_map/all_to_all | solution.py:45
  104.2 2.8 %gather_fusion.2 = bf16[2,128,512]{2,1,0:T(8,128)(2,1)S(1)} fusion(bf16[32,128,512]{2,1,0:T(8,128)(2,1)} %bitcast.2, s32[1024]{0:T(1024)S(1)} %pad_clamp_fusion), kind=kCustom, calls=%fused_computation.2 | custom fusion | bytes 524296 | tf_op jit(solution)/shard_map/jit(_take)/gather | solution.py:148
  107.0 5.7 %all-to-all-done.2 = f32[2,16,512]{2,0,1:T(2,128)S(1)} async-done(((f32[2,16,512]{2,0,1:T(2,128)}), f32[2,16,512]{2,0,1:T(2,128)S(1)}, u32[]{:S(2)}, u32[]{:S(2)}) %all-to-all-start.2) | async-done | bytes 65568 | tf_op jit(solution)/shard_map/all_to_all | solution.py:45
  112.7 0.3 fusion.29
  113.1 13.2 %all_to_all.45 = f32[16,32,256]{2,1,0:T(8,128)S(1)} all-to-all(f32[16,32,256]{2,1,0:T(8,128)S(1)} %broadcast_in_dim.17), channel_id=1, replica_groups=mesh['dp'=8,'tensor'=16] {'tensor'}, dimensions={0} | all-to-all | bytes 1048576 | tf_op jit(solution)/shard_map/all_to_all | solution.py:55
  126.3 0.1 multiply_reduce_fusion
  126.4 0.2 fusion.20
  126.6 0.1 divide_convert_fusion.2
  126.8 0.1 fusion.21
  126.9 0.7 copy.38
  127.6 3.5 %all-to-all-start.4 = ((f32[16,2,512]{2,1,0:T(2,128)}), f32[16,2,512]{2,1,0:T(2,128)S(1)}, u32[]{:S(2)}, u32[]{:S(2)}) async-start(f32[16,2,512]{2,1,0:T(2,128)} %copy.38), calls=%async_computation.4 | async-start | bytes 131072 | tf_op jit(solution)/shard_map/all_to_all | solution.py:67
  131.1 7.5 %pad_maximum_fusion.weight_ref = bf16[16,512,512]{2,1,0:T(8,128)(2,1)} fusion(bf16[16,512,256]{2,1,0:T(8,128)(2,1)} %bitcast.81, bf16[16,512,256]{2,1,0:T(8,128)(2,1)} %bitcast.77), kind=kLoop, calls=%fused_computation.4 | loop fusion | flops 16777216 | bytes 16777216 | tf_op jit(solution)/shard_map/concatenate | solution.py:152
  138.7 0.9 all-to-all-done.4
  139.5 3.6 %fusion.4 = f32[2,1,128]{2,1,0:T(1,128)S(1)} fusion(f32[2,8192,1]{1,0,2:T(2,128)S(1)} %bitcast.87, bf16[8192,256]{1,0:T(8,128)(2,1)} %param.12), kind=kOutput, calls=%fused_computation.8 | convolution fusion | flops 25165824 | bytes 4260864 | tf_op jit(solution)/shard_map/hf,fhd->hd/dot_general | solution.py:75
  143.2 33.8 %all-gather.6.cloned.1.call-done = bf16[96,128,512]{2,1,0:T(8,128)(2,1)} async-done(((bf16[6,128,512]{2,1,0:T(8,128)(2,1)}), bf16[96,128,512]{2,1,0:T(8,128)(2,1)}) %all-gather.6.cloned.1.call-update) | async-done | bytes 12582928 | tf_op jit(solution)/shard_map/all_gather | solution.py:149
  177.0 13.2 %shard_map.73 = bf16[6,128,512]{2,1,0:T(8,128)(2,1)} custom-call(bf16[16,6,128,512]{3,2,1,0:T(8,128)(2,1)} %bitcast.79, bf16[16,512,512]{2,1,0:T(8,128)(2,1)} %pad_maximum_fusion.weight_ref), custom_call_target="tpu_custom_call" | custom-call | tf_op jit(solution)/shard_map/pallas_call | solution.py:95
  190.2 1.2 fusion.27
  191.4 0.1 reshape_reshape.7
  191.5 0.3 convolution_multiply_fusion
  191.7 0.2 fusion.28
  192.0 0.1 reshape_reshape.6
  192.1 0.7 fusion.12
  192.8 0.1 copy.36
  192.9 3.2 %convert_bitcast_fusion = bf16[16,193,512]{2,1,0:T(8,128)(2,1)S(1)} fusion(bf16[32,16,8,512]{3,2,1,0:T(8,128)(2,1)} %bitcast.80, bf16[1,256]{1,0:T(2,128)(2,1)S(1)} %bitcast.89, bf16[192,256]{1,0:T(8,128)(2,1)S(1)} %bitcast.84), kind=kOutput, calls=%fused_computation.11 | convolution fusion | flops 811279360 | bytes 7455232 | tf_op jit(solution)/shard_map/rc,csf->srf/dot_general | solution.py:165
  196.2 45.1 %all_to_all.46 = bf16[16,193,512]{2,1,0:T(8,128)(2,1)S(1)} all-to-all(bf16[16,193,512]{2,1,0:T(8,128)(2,1)S(1)} %convert_bitcast_fusion), channel_id=1, replica_groups=mesh['dp'=8,'tensor'=16] {'tensor'}, dimensions={0} | all-to-all | bytes 6324224 | tf_op jit(solution)/shard_map/all_to_all | solution.py:171
  241.2 0.5 reduce_sum.62
  241.8 0.8 concatenate.11
  (15 shorter events, 0.2 us)
Async XLA Ops:
  6.5 83.3 %all-gather.8.cloned.1.call-start = ((), (), s32[]{:S(2)}) async-start(), calls=%async_computation.7 | async-start | bytes 3481600 | tf_op jit(solution)/shard_map/all_gather | solution.py:120
  25.5 54.3 %all-to-all-start.1 = ((bf16[8,4,128,512]{3,2,1,0:T(8,128)(2,1)}), bf16[8,4,128,512]{3,2,1,0:T(8,128)(2,1)}, u32[]{:S(2)}, u32[]{:S(2)}) async-start(bf16[8,4,128,512]{3,2,1,0:T(8,128)(2,1)} %bitcast.75), calls=%async_computation.1 | async-start | bytes 8388608 | tf_op jit(solution)/shard_map/all_to_all | solution.py:143
  30.1 147.0 %all-gather.6.cloned.1.call-start = ((), (), s32[]{:S(2)}) async-start(), calls=%async_computation.6 | async-start | bytes 13369344 | tf_op jit(solution)/shard_map/all_gather | solution.py:149
  89.9 4.7 %copy-start = (bf16[8192,256]{0,1:T(8,128)(2,1)S(1)}, bf16[8192,256]{0,1:T(8,128)(2,1)}, u32[]{:S(2)}) copy-start(bf16[8192,256]{0,1:T(8,128)(2,1)} %copy.46) | copy-start | bytes 12582916
  95.9 16.7 %all-to-all-start.2 = ((f32[2,16,512]{2,0,1:T(2,128)}), f32[2,16,512]{2,0,1:T(2,128)S(1)}, u32[]{:S(2)}, u32[]{:S(2)}) async-start(f32[2,16,512]{2,0,1:T(2,128)} %bitcast.13), calls=%async_computation.2 | async-start | bytes 131072 | tf_op jit(solution)/shard_map/all_to_all | solution.py:45
  127.6 11.9 %all-to-all-start.4 = ((f32[16,2,512]{2,1,0:T(2,128)}), f32[16,2,512]{2,1,0:T(2,128)S(1)}, u32[]{:S(2)}, u32[]{:S(2)}) async-start(f32[16,2,512]{2,1,0:T(2,128)} %copy.38), calls=%async_computation.4 | async-start | bytes 131072 | tf_op jit(solution)/shard_map/all_to_all | solution.py:67
Sparse Core Ops, SparseCore 0:
  9.5 50.8 all-gather.7
  83.6 93.4 all-gather.5

commit v8 on v5

--- a/solution.py
+++ b/solution.py
@@ -93,10 +93,10 @@
     heads_local = head_cols // HD
     tensor_count = lax.axis_size("tensor")
     group_len = tok_rows // group_count
-    hidden_parts = lax.all_gather(hidden[group_len - 1 :], "tensor", axis=0, tiled=False)
+    hidden_parts = lax.all_gather(hidden, "tensor", axis=0, tiled=False)
     query_sum = jnp.einsum(
         "srf,sfc->rc",
-        hidden_parts,
+        hidden_parts[:, group_len - 1 :],
         w_query.reshape(tensor_count, -1, head_cols),
         preferred_element_type=jnp.float32,
     )

time: 248 us -> 247 us (level)
  no operation moved by 1% of the time
where the time goes in v8:
time: 247 us; the launch traced here: 246 us
  waiting for transfers between devices  90.7 us (37%)
  blocking collectives  67.7 us (27%)
  matrix products  25.3 us (10%)
  local copies, waits for them, and re-layouts  22.4 us (9%)
  starting transfers between devices  16.6 us (7%)
  between operations  13.6 us (6%)
  other arithmetic  9.79 us (4%)
    all_to_all x1, waiting for transfers between devices, shards(): lax.all_to_all(outgoing, 'dp', split_axis=0, concat_axis=0, tiled=True)  49.6 us
    all_to_all x1, blocking collectives, shards(): lax.all_to_all(partial_out, 'tensor', split_axis=0, concat_axis=0, tiled=...  45.1 us
    all_gather x1, waiting for transfers between devices, shards(): main_parts = lax.all_gather(head_rows, 'tensor', axis=0, tiled=False)  33.9 us
    all_to_all x1, blocking collectives, last_token(): lax.all_to_all(jnp.broadcast_to(partial_scores[None], (tensor_count,) + p...  13.2 us
    dot_general x1, matrix products, shards(): jnp.einsum('snkf,sfc->nkc', main_parts, w_both, preferred_element_type=jn...  12 us
    all_to_all x1, blocking collectives, shards(): lax.all_to_all(request_table, 'dp', split_axis=0, concat_axis=0, tiled=True)  9.49 us
    all_to_all x1, starting transfers between devices, last_token(): lax.all_to_all(spread_query.reshape(heads_count, tensor_count, col_count)...  8.48 us
    concatenate x1, other arithmetic, shards(): jnp.concatenate([w_key_parts, w_value_parts], axis=2)  7.53 us
  transfers between devices with their start and end apart: 5, of which 4 were waited for; matrix products, arithmetic and copies ran while one was open for 16% of the time, Pallas kernels for 0%

profile of v8, /device:TPU:0, one launch (start us, length us, event | category | flops | bytes accessed | tf_op | source)
XLA Modules:
  0.0 246.2 jit_solution(1433890594481959822)
XLA Ops:
  6.5 0.0 all-gather.7.cloned.1.call-start
  6.5 0.7 all-gather.7.cloned.1.call-update
  7.3 0.8 copy.32
  8.0 0.1 reshape.262
  8.1 0.2 convert_reduce_fusion
  8.3 0.1 iota_compare_fusion.1
  8.4 0.1 select_reduce_fusion
  8.5 0.1 copy.33
  8.6 9.5 %all_to_all.44 = s32[8,1,4]{2,1,0:T(1,128)S(1)} all-to-all(s32[8,1,4]{2,1,0:T(1,128)S(1)} %copy.33), channel_id=1, replica_groups=mesh['dp'=8,'tensor'=16] {'dp'}, dimensions={0} | all-to-all | bytes 256 | tf_op jit(solution)/shard_map/all_to_all | solution.py:115
  18.1 0.5 broadcast.228
  18.6 0.7 reduce.4
  19.2 0.1 reshape.279
  19.3 5.0 %gather_fusion = bf16[32,128,512]{2,1,0:T(8,128)(2,1)} fusion(bf16[32,128,512]{2,1,0:T(8,128)(2,1)} %param.9, s32[1024]{0:T(1024)S(1)} %pad_clamp_fusion.2), kind=kCustom, calls=%fused_computation | custom fusion | bytes 8388736 | tf_op jit(solution)/shard_map/jit(_take)/gather | solution.py:116
  24.3 4.6 %all-to-all-start.1 = ((bf16[8,4,128,512]{3,2,1,0:T(8,128)(2,1)}), bf16[8,4,128,512]{3,2,1,0:T(8,128)(2,1)}, u32[]{:S(2)}, u32[]{:S(2)}) async-start(bf16[8,4,128,512]{3,2,1,0:T(8,128)(2,1)} %bitcast.83), calls=%async_computation.1 | async-start | bytes 8388608 | tf_op jit(solution)/shard_map/all_to_all | solution.py:119
  28.9 0.0 all-gather.5.cloned.1.call-start
  29.0 49.6 %all-to-all-done.1 = bf16[8,4,128,512]{3,2,1,0:T(8,128)(2,1)} async-done(((bf16[8,4,128,512]{3,2,1,0:T(8,128)(2,1)}), bf16[8,4,128,512]{3,2,1,0:T(8,128)(2,1)}, u32[]{:S(2)}, u32[]{:S(2)}) %all-to-all-start.1) | async-done | bytes 4194336 | tf_op jit(solution)/shard_map/all_to_all | solution.py:119
  78.5 3.7 %gather_fusion.1 = bf16[6,128,512]{2,1,0:T(8,128)(2,1)} fusion(bf16[32,128,512]{2,1,0:T(8,128)(2,1)} %bitcast.2, s32[1024]{0:T(1024)S(1)} %pad_clamp_fusion.1), kind=kCustom, calls=%fused_computation.1 | custom fusion | bytes 1572888 | tf_op jit(solution)/shard_map/jit(_take)/gather | solution.py:123
  82.3 0.0 all-gather.5.cloned.1.call-update
  82.3 0.1 slice.27
  82.4 6.4 %copy.48 = bf16[8192,256]{0,1:T(8,128)(2,1)} copy(bf16[8192,256]{1,0:T(8,128)(2,1)} %param.11) | data formatting | bytes 8388608 | tf_op jit(solution)/shard_map/reshape | solution.py:39
  88.7 0.0 all-gather.7.cloned.1.call-done
  88.7 0.0 copy-start
  88.7 4.4 %fusion.20 = bf16[193,256]{1,0:T(8,128)(2,1)S(1)} fusion(bf16[16,512,256]{2,1,0:T(8,128)(2,1)} %bitcast.98, bf16[16,256,512]{2,1,0:T(8,128)(2,1)} %bitcast.99), kind=kOutput, calls=%fused_computation.21 | convolution fusion | flops 809550080 | bytes 7569920 | tf_op jit(solution)/shard_map/srf,sfc->rc/dot_general | solution.py:97
  93.1 0.3 copy-done
  93.4 0.7 fusion.35
  94.0 0.7 copy.44
  94.7 8.5 %all-to-all-start.2 = ((f32[2,16,512]{2,0,1:T(2,128)}), f32[2,16,512]{2,0,1:T(2,128)S(1)}, u32[]{:S(2)}, u32[]{:S(2)}) async-start(f32[2,16,512]{2,0,1:T(2,128)} %bitcast.16), calls=%async_computation.2 | async-start | bytes 131072 | tf_op jit(solution)/shard_map/all_to_all | solution.py:43
  103.2 2.8 %gather_fusion.2 = bf16[2,128,512]{2,1,0:T(8,128)(2,1)S(1)} fusion(bf16[32,128,512]{2,1,0:T(8,128)(2,1)} %bitcast.2, s32[1024]{0:T(1024)S(1)} %pad_clamp_fusion), kind=kCustom, calls=%fused_computation.2 | custom fusion | bytes 524296 | tf_op jit(solution)/shard_map/jit(_take)/gather | solution.py:124
  106.0 5.7 %all-to-all-done.2 = f32[2,16,512]{2,0,1:T(2,128)S(1)} async-done(((f32[2,16,512]{2,0,1:T(2,128)}), f32[2,16,512]{2,0,1:T(2,128)S(1)}, u32[]{:S(2)}, u32[]{:S(2)}) %all-to-all-start.2) | async-done | bytes 65568 | tf_op jit(solution)/shard_map/all_to_all | solution.py:43
  111.7 0.3 fusion.40
  112.1 13.2 %all_to_all.45 = f32[16,32,256]{2,1,0:T(8,128)S(1)} all-to-all(f32[16,32,256]{2,1,0:T(8,128)S(1)} %broadcast_in_dim.17), channel_id=1, replica_groups=mesh['dp'=8,'tensor'=16] {'tensor'}, dimensions={0} | all-to-all | bytes 1048576 | tf_op jit(solution)/shard_map/all_to_all | solution.py:53
  125.3 0.1 multiply_reduce_fusion
  125.4 0.2 fusion.31
  125.6 0.1 divide_convert_fusion.2
  125.8 0.1 fusion.32
  125.9 0.7 copy.39
  126.6 3.5 %all-to-all-start.4 = ((f32[16,2,512]{2,1,0:T(2,128)}), f32[16,2,512]{2,1,0:T(2,128)S(1)}, u32[]{:S(2)}, u32[]{:S(2)}) async-start(f32[16,2,512]{2,1,0:T(2,128)} %copy.39), calls=%async_computation.4 | async-start | bytes 131072 | tf_op jit(solution)/shard_map/all_to_all | solution.py:65
  130.1 7.5 %pad_maximum_fusion = bf16[16,512,512]{2,1,0:T(8,128)(2,1)} fusion(bf16[16,512,256]{2,1,0:T(8,128)(2,1)} %bitcast.87, bf16[16,512,256]{2,1,0:T(8,128)(2,1)} %bitcast.85), kind=kLoop, calls=%fused_computation.4 | loop fusion | flops 16777216 | bytes 16777216 | tf_op jit(solution)/shard_map/concatenate | solution.py:128
  137.7 0.9 all-to-all-done.4
  138.5 3.6 %fusion.6 = f32[2,1,128]{2,1,0:T(1,128)S(1)} fusion(f32[2,8192,1]{1,0,2:T(2,128)S(1)} %bitcast.93, bf16[8192,256]{1,0:T(8,128)(2,1)} %param.12), kind=kOutput, calls=%fused_computation.10 | convolution fusion | flops 25165824 | bytes 4260864 | tf_op jit(solution)/shard_map/hf,fhd->hd/dot_general | solution.py:73
  142.2 33.9 %all-gather.5.cloned.1.call-done = bf16[96,128,512]{2,1,0:T(8,128)(2,1)} async-done(((bf16[6,128,512]{2,1,0:T(8,128)(2,1)}), bf16[96,128,512]{2,1,0:T(8,128)(2,1)}) %all-gather.5.cloned.1.call-update) | async-done | bytes 12582928 | tf_op jit(solution)/shard_map/all_gather | solution.py:125
  176.1 12.0 %bitcast_convert_fusion = bf16[6,128,512]{2,1,0:T(8,128)(2,1)S(1)} fusion(bf16[16,6,128,512]{3,2,1,0:T(8,128)(2,1)} %bitcast.97, bf16[16,512,512]{2,1,0:T(8,128)(2,1)} %pad_maximum_fusion), kind=kOutput, calls=%fused_computation.16 | convolution fusion | flops 6442844160 | bytes 21757952 | tf_op jit(solution)/shard_map/snkf,sfc->nkc/dot_general | solution.py:129
  188.1 0.1 fusion.38
  188.2 0.1 reshape_reshape.7
  188.3 0.2 convolution_multiply_fusion
  188.6 0.2 fusion.39
  188.8 0.1 reshape_reshape.6
  188.9 0.7 fusion.23
  189.6 0.1 copy.37
  189.8 3.2 %convert_bitcast_fusion = bf16[16,193,512]{2,1,0:T(8,128)(2,1)S(1)} fusion(bf16[32,16,8,512]{3,2,1,0:T(8,128)(2,1)} %bitcast.86, bf16[1,256]{1,0:T(2,128)(2,1)S(1)} %bitcast.95, bf16[192,256]{1,0:T(8,128)(2,1)S(1)} %bitcast.90), kind=kOutput, calls=%fused_computation.15 | convolution fusion | flops 811279360 | bytes 7455232 | tf_op jit(solution)/shard_map/rc,csf->srf/dot_general | solution.py:143
  193.0 45.1 %all_to_all.46 = bf16[16,193,512]{2,1,0:T(8,128)(2,1)S(1)} all-to-all(bf16[16,193,512]{2,1,0:T(8,128)(2,1)S(1)} %convert_bitcast_fusion), channel_id=1, replica_groups=mesh['dp'=8,'tensor'=16] {'tensor'}, dimensions={0} | all-to-all | bytes 6324224 | tf_op jit(solution)/shard_map/all_to_all | solution.py:149
  238.0 0.5 reduce_sum.62
  238.6 0.8 concatenate.11
  (15 shorter events, 0.3 us)
Async XLA Ops:
  6.5 82.2 %all-gather.7.cloned.1.call-start = ((), (), s32[]{:S(2)}) async-start(), calls=%async_computation.7 | async-start | bytes 4456448 | tf_op jit(solution)/shard_map/all_gather | solution.py:96
  24.3 54.2 %all-to-all-start.1 = ((bf16[8,4,128,512]{3,2,1,0:T(8,128)(2,1)}), bf16[8,4,128,512]{3,2,1,0:T(8,128)(2,1)}, u32[]{:S(2)}, u32[]{:S(2)}) async-start(bf16[8,4,128,512]{3,2,1,0:T(8,128)(2,1)} %bitcast.83), calls=%async_computation.1 | async-start | bytes 8388608 | tf_op jit(solution)/shard_map/all_to_all | solution.py:119
  28.9 147.2 %all-gather.5.cloned.1.call-start = ((), (), s32[]{:S(2)}) async-start(), calls=%async_computation.6 | async-start | bytes 13369344 | tf_op jit(solution)/shard_map/all_gather | solution.py:125
  88.7 4.6 %copy-start = (bf16[8192,256]{0,1:T(8,128)(2,1)S(1)}, bf16[8192,256]{0,1:T(8,128)(2,1)}, u32[]{:S(2)}) copy-start(bf16[8192,256]{0,1:T(8,128)(2,1)} %copy.48) | copy-start | bytes 12582916
  94.7 17.0 %all-to-all-start.2 = ((f32[2,16,512]{2,0,1:T(2,128)}), f32[2,16,512]{2,0,1:T(2,128)S(1)}, u32[]{:S(2)}, u32[]{:S(2)}) async-start(f32[2,16,512]{2,0,1:T(2,128)} %bitcast.16), calls=%async_computation.2 | async-start | bytes 131072 | tf_op jit(solution)/shard_map/all_to_all | solution.py:43
  126.6 11.9 %all-to-all-start.4 = ((f32[16,2,512]{2,1,0:T(2,128)}), f32[16,2,512]{2,1,0:T(2,128)S(1)}, u32[]{:S(2)}, u32[]{:S(2)}) async-start(f32[16,2,512]{2,1,0:T(2,128)} %copy.39), calls=%async_computation.4 | async-start | bytes 131072 | tf_op jit(solution)/shard_map/all_to_all | solution.py:65
Sparse Core Ops, SparseCore 0:
  9.5 53.9 all-gather.6
  82.4 93.5 all-gather.4

commit v9 on v8

--- a/solution.py
+++ b/solution.py
@@ -138,16 +138,19 @@
     last_live = last_token(
         query_rows[main_groups * group_len], tail_rows, w_key, w_value, heads_local
     )
-    live = jnp.concatenate([main_live, last_live[None]], 0)
-    live_rows = live.shape[0]
+    w_out_parts = w_out.reshape(head_cols, tensor_count, -1)
+    last_partial = jnp.einsum(
+        "c,csf->sf", last_live, w_out_parts, preferred_element_type=jnp.float32
+    ).astype(jnp.bfloat16)
+    last_spread = lax.all_to_all(last_partial, "tensor", split_axis=0, concat_axis=0, tiled=True)
+    last_sum = jnp.sum(last_spread.astype(jnp.float32), axis=0).astype(jnp.bfloat16)
     partial_out = jnp.einsum(
-        "rc,csf->srf",
-        live,
-        w_out.reshape(head_cols, tensor_count, -1),
-        preferred_element_type=jnp.float32,
+        "rc,csf->srf", main_live, w_out_parts, preferred_element_type=jnp.float32
     ).astype(jnp.bfloat16)
     spread = lax.all_to_all(partial_out, "tensor", split_axis=0, concat_axis=0, tiled=True)
-    summed = jnp.sum(spread.astype(jnp.float32), axis=0).astype(jnp.bfloat16)
+    summed = jnp.concatenate(
+        [jnp.sum(spread.astype(jnp.float32), axis=0).astype(jnp.bfloat16), last_sum[None]], 0
+    )
     return jnp.concatenate([jnp.zeros((group_len - 1, summed.shape[1]), jnp.bfloat16), summed], 0)
 
 

time: 247 us -> 256 us (1.036)
  blocking collectives: 67.7 us -> 22.7 us
  waiting for transfers between devices: 90.7 us -> 130 us
  starting transfers between devices: 16.6 us -> 27 us
    all_to_all x0 -> x2, waiting for transfers between devices: none -> 48 us  [the longest x1 48 us: shards(): lax.all_to_all(partial_out, 'tensor', split_axis=0, concat_axis=0, tiled=...]
    all_to_all x1 -> x0, blocking collectives: 45.1 us -> none  [shards(): lax.all_to_all(partial_out, 'tensor', split_axis=0, concat_axis=0, tiled=...]
    all_to_all x0 -> x2, starting transfers between devices: none -> 10.4 us  [the longest x1 6.35 us: shards(): lax.all_to_all(last_partial, 'tensor', split_axis=0, concat_axis=0, tiled...]
    all_gather x1, waiting for transfers between devices: 33.9 us -> 25.1 us  [shards(): main_parts = lax.all_gather(head_rows, 'tensor', axis=0, tiled=False)]
    dot_general x1 -> x2, matrix products: 3.21 us -> 5.5 us  [the longest x1 4.85 us: shards(): jnp.einsum('rc,csf->srf', main_live, w_out_parts, preferred_element_type=...]
  transfers between devices with their start and end apart: 5 -> 7, of which waited for: 4 -> 5; matrix products, arithmetic and copies ran while one was open for 16% -> 24% of each run, Pallas kernels for 0% -> 0%
where the time goes in v9:
time: 256 us; the launch traced here: 255 us
  waiting for transfers between devices  130 us (51%)
  matrix products  27.8 us (11%)
  starting transfers between devices  27 us (11%)
  local copies, waits for them, and re-layouts  22.9 us (9%)
  blocking collectives  22.7 us (9%)
  between operations  13.7 us (5%)
  other arithmetic  11.2 us (4%)
    all_to_all x1, waiting for transfers between devices, shards(): lax.all_to_all(outgoing, 'dp', split_axis=0, concat_axis=0, tiled=True)  49.6 us
    all_to_all x1, waiting for transfers between devices, shards(): lax.all_to_all(partial_out, 'tensor', split_axis=0, concat_axis=0, tiled=...  48 us
    all_gather x1, waiting for transfers between devices, shards(): main_parts = lax.all_gather(head_rows, 'tensor', axis=0, tiled=False)  25.1 us
    all_to_all x1, blocking collectives, last_token(): lax.all_to_all(jnp.broadcast_to(partial_scores[None], (tensor_count,) + p...  13.2 us
    dot_general x1, matrix products, shards(): jnp.einsum('snkf,sfc->nkc', main_parts, w_both, preferred_element_type=jn...  12 us
    all_to_all x1, blocking collectives, shards(): lax.all_to_all(request_table, 'dp', split_axis=0, concat_axis=0, tiled=True)  9.49 us
    all_to_all x1, starting transfers between devices, last_token(): lax.all_to_all(spread_query.reshape(heads_count, tensor_count, col_count)...  8.48 us
    concatenate x1, other arithmetic, shards(): jnp.concatenate([w_key_parts, w_value_parts], axis=2)  7.53 us
  transfers between devices with their start and end apart: 7, of which 5 were waited for; matrix products, arithmetic and copies ran while one was open for 24% of the time, Pallas kernels for 0%

profile of v9, /device:TPU:0, one launch (start us, length us, event | category | flops | bytes accessed | tf_op | source)
XLA Modules:
  0.0 255.1 jit_solution(15640302116454193684)
XLA Ops:
  6.5 0.0 all-gather.7.cloned.1.call-start
  6.5 0.7 all-gather.7.cloned.1.call-update
  7.3 0.8 copy.42
  8.0 0.1 reshape.267
  8.1 0.2 convert_reduce_fusion
  8.3 0.1 iota_compare_fusion.1
  8.4 0.1 select_reduce_fusion
  8.5 0.1 copy.43
  8.6 9.5 %all_to_all.53 = s32[8,1,4]{2,1,0:T(1,128)S(1)} all-to-all(s32[8,1,4]{2,1,0:T(1,128)S(1)} %copy.43), channel_id=1, replica_groups=mesh['dp'=8,'tensor'=16] {'dp'}, dimensions={0} | all-to-all | bytes 256 | tf_op jit(solution)/shard_map/all_to_all | solution.py:115
  18.1 0.5 broadcast.228
  18.6 0.7 reduce.6
  19.2 0.1 reshape.285
  19.3 5.0 %gather_fusion = bf16[32,128,512]{2,1,0:T(8,128)(2,1)} fusion(bf16[32,128,512]{2,1,0:T(8,128)(2,1)} %param.9, s32[1024]{0:T(1024)S(1)} %pad_clamp_fusion.2), kind=kCustom, calls=%fused_computation | custom fusion | bytes 8388736 | tf_op jit(solution)/shard_map/jit(_take)/gather | solution.py:116
  24.3 4.6 %all-to-all-start.1 = ((bf16[8,4,128,512]{3,2,1,0:T(8,128)(2,1)}), bf16[8,4,128,512]{3,2,1,0:T(8,128)(2,1)}, u32[]{:S(2)}, u32[]{:S(2)}) async-start(bf16[8,4,128,512]{3,2,1,0:T(8,128)(2,1)} %bitcast.85), calls=%async_computation.1 | async-start | bytes 8388608 | tf_op jit(solution)/shard_map/all_to_all | solution.py:119
  28.9 0.0 all-gather.5.cloned.1.call-start
  29.0 49.6 %all-to-all-done.1 = bf16[8,4,128,512]{3,2,1,0:T(8,128)(2,1)} async-done(((bf16[8,4,128,512]{3,2,1,0:T(8,128)(2,1)}), bf16[8,4,128,512]{3,2,1,0:T(8,128)(2,1)}, u32[]{:S(2)}, u32[]{:S(2)}) %all-to-all-start.1) | async-done | bytes 4194336 | tf_op jit(solution)/shard_map/all_to_all | solution.py:119
  78.5 3.7 %gather_fusion.1 = bf16[6,128,512]{2,1,0:T(8,128)(2,1)} fusion(bf16[32,128,512]{2,1,0:T(8,128)(2,1)} %bitcast.2, s32[1024]{0:T(1024)S(1)} %pad_clamp_fusion.1), kind=kCustom, calls=%fused_computation.1 | custom fusion | bytes 1572888 | tf_op jit(solution)/shard_map/jit(_take)/gather | solution.py:123
  82.3 0.0 all-gather.5.cloned.1.call-update
  82.3 0.1 slice.27
  82.4 6.4 %copy.60 = bf16[8192,256]{0,1:T(8,128)(2,1)} copy(bf16[8192,256]{1,0:T(8,128)(2,1)} %param.11) | data formatting | bytes 8388608 | tf_op jit(solution)/shard_map/reshape | solution.py:39
  88.7 0.0 all-gather.7.cloned.1.call-done
  88.7 0.0 copy-start.1
  88.7 4.4 %fusion.23 = bf16[193,256]{1,0:T(8,128)(2,1)S(1)} fusion(bf16[16,512,256]{2,1,0:T(8,128)(2,1)} %bitcast.97, bf16[16,256,512]{2,1,0:T(8,128)(2,1)} %bitcast.98), kind=kOutput, calls=%fused_computation.24 | convolution fusion | flops 809550080 | bytes 7569920 | tf_op jit(solution)/shard_map/srf,sfc->rc/dot_general | solution.py:97
  93.1 0.3 copy-done.1
  93.4 0.7 fusion.37
  94.0 0.7 copy.55
  94.7 8.5 %all-to-all-start.3 = ((f32[2,16,512]{2,0,1:T(2,128)}), f32[2,16,512]{2,0,1:T(2,128)S(1)}, u32[]{:S(2)}, u32[]{:S(2)}) async-start(f32[2,16,512]{2,0,1:T(2,128)} %bitcast.17), calls=%async_computation.3 | async-start | bytes 131072 | tf_op jit(solution)/shard_map/all_to_all | solution.py:43
  103.2 2.8 %gather_fusion.2 = bf16[2,128,512]{2,1,0:T(8,128)(2,1)S(1)} fusion(bf16[32,128,512]{2,1,0:T(8,128)(2,1)} %bitcast.2, s32[1024]{0:T(1024)S(1)} %pad_clamp_fusion), kind=kCustom, calls=%fused_computation.2 | custom fusion | bytes 524296 | tf_op jit(solution)/shard_map/jit(_take)/gather | solution.py:124
  106.0 5.7 %all-to-all-done.3 = f32[2,16,512]{2,0,1:T(2,128)S(1)} async-done(((f32[2,16,512]{2,0,1:T(2,128)}), f32[2,16,512]{2,0,1:T(2,128)S(1)}, u32[]{:S(2)}, u32[]{:S(2)}) %all-to-all-start.3) | async-done | bytes 65568 | tf_op jit(solution)/shard_map/all_to_all | solution.py:43
  111.7 0.3 fusion.41
  112.1 13.2 %all_to_all.54 = f32[16,32,256]{2,1,0:T(8,128)S(1)} all-to-all(f32[16,32,256]{2,1,0:T(8,128)S(1)} %broadcast_in_dim.22), channel_id=1, replica_groups=mesh['dp'=8,'tensor'=16] {'tensor'}, dimensions={0} | all-to-all | bytes 1048576 | tf_op jit(solution)/shard_map/all_to_all | solution.py:53
  125.3 0.1 multiply_reduce_fusion
  125.4 0.2 fusion.32
  125.6 0.1 divide_convert_fusion.2
  125.8 0.1 fusion.34
  125.9 0.7 copy.50
  126.6 3.5 %all-to-all-start.5 = ((f32[16,2,512]{2,1,0:T(2,128)}), f32[16,2,512]{2,1,0:T(2,128)S(1)}, u32[]{:S(2)}, u32[]{:S(2)}) async-start(f32[16,2,512]{2,1,0:T(2,128)} %copy.50), calls=%async_computation.5 | async-start | bytes 131072 | tf_op jit(solution)/shard_map/all_to_all | solution.py:65
  130.1 7.5 %pad_maximum_fusion = bf16[16,512,512]{2,1,0:T(8,128)(2,1)} fusion(bf16[16,512,256]{2,1,0:T(8,128)(2,1)} %bitcast.88, bf16[16,512,256]{2,1,0:T(8,128)(2,1)} %bitcast.87), kind=kLoop, calls=%fused_computation.4 | loop fusion | flops 16777216 | bytes 16777216 | tf_op jit(solution)/shard_map/concatenate | solution.py:128
  137.7 0.9 all-to-all-done.5
  138.5 0.0 copy-start
  138.5 3.8 %fusion.3 = f32[2,1,128]{2,1,0:T(1,128)S(1)} fusion(f32[2,8192,1]{1,0,2:T(2,128)S(1)} %bitcast.93, bf16[8192,256]{1,0:T(8,128)(2,1)} %param.12), kind=kOutput, calls=%fused_computation.7 | convolution fusion | flops 25165824 | bytes 4260864 | tf_op jit(solution)/shard_map/hf,fhd->hd/dot_general | solution.py:73
  142.4 0.0 copy-done
  142.4 0.7 fusion.6
  143.0 0.5 broadcast.229
  143.5 0.7 reduce.7
  144.2 0.6 reshape.334
  144.8 6.3 %all-to-all-start.6 = ((bf16[16,2,256]{2,1,0:T(2,128)(2,1)}), bf16[16,2,256]{2,1,0:T(2,128)(2,1)S(1)}, u32[]{:S(2)}, u32[]{:S(2)}) async-start(bf16[16,2,256]{2,1,0:T(2,128)(2,1)} %reshape.334), calls=%async_computation.6 | async-start | bytes 32768 | tf_op jit(solution)/shard_map/all_to_all | solution.py:145
  151.2 25.1 %all-gather.5.cloned.1.call-done = bf16[96,128,512]{2,1,0:T(8,128)(2,1)} async-done(((bf16[6,128,512]{2,1,0:T(8,128)(2,1)}), bf16[96,128,512]{2,1,0:T(8,128)(2,1)}) %all-gather.5.cloned.1.call-update) | async-done | bytes 12582928 | tf_op jit(solution)/shard_map/all_gather | solution.py:125
  176.2 12.0 %bitcast_convert_fusion = bf16[6,128,512]{2,1,0:T(8,128)(2,1)S(1)} fusion(bf16[16,6,128,512]{3,2,1,0:T(8,128)(2,1)} %bitcast.96, bf16[16,512,512]{2,1,0:T(8,128)(2,1)} %pad_maximum_fusion), kind=kOutput, calls=%fused_computation.19 | convolution fusion | flops 6442844160 | bytes 21757952 | tf_op jit(solution)/shard_map/snkf,sfc->nkc/dot_general | solution.py:129
  188.3 0.1 fusion.39
  188.4 0.1 reshape_reshape.7
  188.5 0.2 convolution_multiply_fusion
  188.7 0.2 fusion.40
  189.0 0.1 reshape_reshape.6
  189.1 0.7 fusion.26
  189.8 0.1 copy.47
  189.9 0.1 reshape.315
  190.0 4.9 %convert_bitcast_fusion = bf16[16,192,512]{2,1,0:T(8,128)(2,1)} fusion(bf16[192,256,1]{1,0,2:T(8,128)(2,1)S(1)} %reshape.315, bf16[32,16,8,512]{3,2,1,0:T(8,128)(2,1)} %bitcast.83), kind=kOutput, calls=%fused_computation.18 | convolution fusion | flops 806879232 | bytes 7438336 | tf_op jit(solution)/shard_map/rc,csf->srf/dot_general | solution.py:147
  194.8 0.0 all-to-all-done.6
  194.8 4.1 %all-to-all-start.2 = ((bf16[16,192,512]{2,1,0:T(8,128)(2,1)}), bf16[16,192,512]{2,1,0:T(8,128)(2,1)S(1)}, u32[]{:S(2)}, u32[]{:S(2)}) async-start(bf16[16,192,512]{2,1,0:T(8,128)(2,1)} %convert_bitcast_fusion), calls=%async_computation.2 | async-start | bytes 6291456 | tf_op jit(solution)/shard_map/all_to_all | solution.py:150
  199.0 0.1 reduce_sum.75
  199.0 48.0 %all-to-all-done.2 = bf16[16,192,512]{2,1,0:T(8,128)(2,1)S(1)} async-done(((bf16[16,192,512]{2,1,0:T(8,128)(2,1)}), bf16[16,192,512]{2,1,0:T(8,128)(2,1)S(1)}, u32[]{:S(2)}, u32[]{:S(2)}) %all-to-all-start.2) | async-done | bytes 3145760 | tf_op jit(solution)/shard_map/all_to_all | solution.py:150
  247.0 0.5 reduce_sum.72
  247.4 0.8 pad_maximum_fusion.1
  (19 shorter events, 0.3 us)
Async XLA Ops:
  6.5 82.2 %all-gather.7.cloned.1.call-start = ((), (), s32[]{:S(2)}) async-start(), calls=%async_computation.8 | async-start | bytes 4456448 | tf_op jit(solution)/shard_map/all_gather | solution.py:96
  24.3 54.2 %all-to-all-start.1 = ((bf16[8,4,128,512]{3,2,1,0:T(8,128)(2,1)}), bf16[8,4,128,512]{3,2,1,0:T(8,128)(2,1)}, u32[]{:S(2)}, u32[]{:S(2)}) async-start(bf16[8,4,128,512]{3,2,1,0:T(8,128)(2,1)} %bitcast.85), calls=%async_computation.1 | async-start | bytes 8388608 | tf_op jit(solution)/shard_map/all_to_all | solution.py:119
  28.9 147.4 %all-gather.5.cloned.1.call-start = ((), (), s32[]{:S(2)}) async-start(), calls=%async_computation.7 | async-start | bytes 13369344 | tf_op jit(solution)/shard_map/all_gather | solution.py:125
  88.7 4.6 %copy-start.1 = (bf16[8192,256]{0,1:T(8,128)(2,1)S(1)}, bf16[8192,256]{0,1:T(8,128)(2,1)}, u32[]{:S(2)}) copy-start(bf16[8192,256]{0,1:T(8,128)(2,1)} %copy.60) | copy-start | bytes 12582916
  94.7 17.0 %all-to-all-start.3 = ((f32[2,16,512]{2,0,1:T(2,128)}), f32[2,16,512]{2,0,1:T(2,128)S(1)}, u32[]{:S(2)}, u32[]{:S(2)}) async-start(f32[2,16,512]{2,0,1:T(2,128)} %bitcast.17), calls=%async_computation.3 | async-start | bytes 131072 | tf_op jit(solution)/shard_map/all_to_all | solution.py:43
  126.6 11.9 %all-to-all-start.5 = ((f32[16,2,512]{2,1,0:T(2,128)}), f32[16,2,512]{2,1,0:T(2,128)S(1)}, u32[]{:S(2)}, u32[]{:S(2)}) async-start(f32[16,2,512]{2,1,0:T(2,128)} %copy.50), calls=%async_computation.5 | async-start | bytes 131072 | tf_op jit(solution)/shard_map/all_to_all | solution.py:65
  138.5 3.8 %copy-start = (bf16[256,8192]{1,0:T(8,128)(2,1)S(1)}, bf16[256,8192]{1,0:T(8,128)(2,1)}, u32[]{:S(2)}) copy-start(bf16[256,8192]{1,0:T(8,128)(2,1)} %param.13) | copy-start | bytes 12582916
  144.8 50.0 %all-to-all-start.6 = ((bf16[16,2,256]{2,1,0:T(2,128)(2,1)}), bf16[16,2,256]{2,1,0:T(2,128)(2,1)S(1)}, u32[]{:S(2)}, u32[]{:S(2)}) async-start(bf16[16,2,256]{2,1,0:T(2,128)(2,1)} %reshape.334), calls=%async_computation.6 | async-start | bytes 32768 | tf_op jit(solution)/shard_map/all_to_all | solution.py:145
  194.8 52.1 %all-to-all-start.2 = ((bf16[16,192,512]{2,1,0:T(8,128)(2,1)}), bf16[16,192,512]{2,1,0:T(8,128)(2,1)S(1)}, u32[]{:S(2)}, u32[]{:S(2)}) async-start(bf16[16,192,512]{2,1,0:T(8,128)(2,1)} %convert_bitcast_fusion), calls=%async_computation.2 | async-start | bytes 6291456 | tf_op jit(solution)/shard_map/all_to_all | solution.py:150
Sparse Core Ops, SparseCore 0:
  9.5 53.9 all-gather.6
  82.4 93.7 all-gather.4

commit v10 on v8

--- a/solution.py
+++ b/solution.py
@@ -2,6 +2,8 @@
 import jax.numpy as jnp
 from jax import lax
 from jax.sharding import PartitionSpec as P
+from jax.experimental import pallas as pl
+from jax.experimental.pallas import tpu as pltpu
 
 HD = 128
 
@@ -80,6 +82,29 @@
     return context.astype(jnp.bfloat16).reshape(-1)
 
 
+def pick_kernel(index_ref, source_ref, out_ref, sems):
+    last = source_ref.shape[0] - 1
+    copies = []
+    for n in range(out_ref.shape[0]):
+        row = jnp.minimum(jnp.maximum(index_ref[n], 0), last)
+        copies.append(pltpu.make_async_copy(source_ref.at[row], out_ref.at[n], sems.at[n]))
+    for copy in copies:
+        copy.start()
+    for copy in copies:
+        copy.wait()
+
+
+def pick(source, index):
+    count = index.shape[0]
+    return pl.pallas_call(
+        pick_kernel,
+        out_shape=jax.ShapeDtypeStruct((count,) + source.shape[1:], source.dtype),
+        in_specs=[pl.BlockSpec(memory_space=pltpu.SMEM), pl.BlockSpec(memory_space=pl.ANY)],
+        out_specs=pl.BlockSpec(memory_space=pl.ANY),
+        scratch_shapes=[pltpu.SemaphoreType.DMA((count,))],
+    )(index, source)
+
+
 def shards(hidden, neighbour_ids, database, w_query, w_key, w_value, w_out):
     dp_count = lax.axis_size("dp")
     tok_rows = hidden.shape[0]
@@ -113,14 +138,14 @@
     )
     request_table = jnp.sum(slot_hit.astype(jnp.int32) * local_index[:, None, None], 0)
     requested = lax.all_to_all(request_table, "dp", split_axis=0, concat_axis=0, tiled=True)
-    outgoing = jnp.take(database, requested.reshape(-1), axis=0, mode="clip").reshape(
+    outgoing = pick(database, requested.reshape(-1)).reshape(
         dp_count, capacity, ret_len, col_count
     )
     arrived = lax.all_to_all(outgoing, "dp", split_axis=0, concat_axis=0, tiled=True)
     arrived_rows = arrived.reshape(dp_count * capacity, ret_len, col_count)
     arrived_slot = owners * capacity + slot_rank
     main_rows = per_reader - 2
-    head_rows = jnp.take(arrived_rows, arrived_slot[:main_rows], axis=0, mode="clip")
+    head_rows = pick(arrived_rows, arrived_slot[:main_rows])
     tail_rows = jnp.take(arrived_rows, arrived_slot[main_rows:], axis=0, mode="clip")
     main_parts = lax.all_gather(head_rows, "tensor", axis=0, tiled=False)
     w_key_parts = w_key.reshape(tensor_count, col_count, head_cols)

time: 247 us -> 393 us (1.59)
  Pallas kernels: 0 us -> 155 us
  local copies, waits for them, and re-layouts: 22.4 us -> 14.2 us
    pallas_call x0 -> x2, Pallas kernels: none -> 155 us  [pick(): pl.pallas_call(pick_kernel, out_shape=jax.ShapeDtypeStruct((count,) + sou...]
    gather x2 -> x0, local copies, waits for them, and re-layouts: 8.72 us -> none  [the longest x1 4.98 us: shards(): jnp.take(database, requested.reshape(-1), axis=0, mode='clip')]
  transfers between devices with their start and end apart: 5 -> 5, of which waited for: 4 -> 4; matrix products, arithmetic and copies ran while one was open for 16% -> 8% of each run, Pallas kernels for 0% -> 39%
where the time goes in v10:
time: 393 us
  Pallas kernels  155 us (39%)
  waiting for transfers between devices  90.2 us (23%)
  blocking collectives  67.8 us (17%)
  matrix products  25.4 us (6%)
  starting transfers between devices  16.5 us (4%)
  local copies, waits for them, and re-layouts  14.2 us (4%)
  between operations  13.6 us (3%)
  other arithmetic  10.3 us (3%)
    pallas_call x2, Pallas kernels, pick(): pl.pallas_call(pick_kernel, out_shape=jax.ShapeDtypeStruct((count,) + sou...  155 us
    all_to_all x1, waiting for transfers between devices, shards(): lax.all_to_all(outgoing, 'dp', split_axis=0, concat_axis=0, tiled=True)  49.1 us
    all_to_all x1, blocking collectives, shards(): lax.all_to_all(partial_out, 'tensor', split_axis=0, concat_axis=0, tiled=...  45.1 us
    all_gather x1, waiting for transfers between devices, shards(): main_parts = lax.all_gather(head_rows, 'tensor', axis=0, tiled=False)  33.8 us
    all_to_all x1, blocking collectives, last_token(): lax.all_to_all(jnp.broadcast_to(partial_scores[None], (tensor_count,) + p...  13.2 us
    dot_general x1, matrix products, shards(): jnp.einsum('snkf,sfc->nkc', main_parts, w_both, preferred_element_type=jn...  12 us
    all_to_all x1, blocking collectives, shards(): lax.all_to_all(request_table, 'dp', split_axis=0, concat_axis=0, tiled=True)  9.49 us
    all_to_all x1, starting transfers between devices, last_token(): lax.all_to_all(spread_query.reshape(heads_count, tensor_count, col_count)...  8.34 us
  transfers between devices with their start and end apart: 5, of which 4 were waited for; matrix products, arithmetic and copies ran while one was open for 8% of the time, Pallas kernels for 39%

profile of v10, /device:TPU:0, one launch (start us, length us, event | category | flops | bytes accessed | tf_op | source)
XLA Modules:
  0.0 392.7 jit_solution(4861343356335616392)
XLA Ops:
  6.5 0.0 all-gather.7.cloned.1.call-start
  6.5 0.7 all-gather.7.cloned.1.call-update
  7.3 0.8 copy.33
  8.0 0.1 reshape.263
  8.1 0.2 convert_reduce_fusion
  8.3 0.1 iota_compare_fusion
  8.4 0.1 select_reduce_fusion
  8.5 0.1 copy.34
  8.6 9.5 %all_to_all.44 = s32[8,1,4]{2,1,0:T(1,128)S(1)} all-to-all(s32[8,1,4]{2,1,0:T(1,128)S(1)} %copy.34), channel_id=1, replica_groups=mesh['dp'=8,'tensor'=16] {'dp'}, dimensions={0} | all-to-all | bytes 256 | tf_op jit(solution)/shard_map/all_to_all | solution.py:140
  18.1 0.5 broadcast.220
  18.6 0.7 reduce.4
  19.2 0.6 reshape.264.index_ref
  19.8 129.1 %shard_map.73 = bf16[32,128,512]{2,1,0:T(8,128)(2,1)} custom-call(s32[32]{0:T(128)} %reshape.264.index_ref, bf16[32,128,512]{2,1,0:T(8,128)(2,1)} %source_ref.1), custom_call_target="tpu_custom_call" | custom-call | tf_op jit(solution)/shard_map/pallas_call | solution.py:99
  149.0 4.6 %all-to-all-start.1 = ((bf16[8,4,128,512]{3,2,1,0:T(8,128)(2,1)}), bf16[8,4,128,512]{3,2,1,0:T(8,128)(2,1)}, u32[]{:S(2)}, u32[]{:S(2)}) async-start(bf16[8,4,128,512]{3,2,1,0:T(8,128)(2,1)} %bitcast.83), calls=%async_computation.1 | async-start | bytes 8388608 | tf_op jit(solution)/shard_map/all_to_all | solution.py:144
  153.6 0.0 all-gather.5.cloned.1.call-start
  153.6 0.5 multiply_add_fusion
  154.1 0.0 copy-start.1
  154.1 49.1 %all-to-all-done.1 = bf16[8,4,128,512]{3,2,1,0:T(8,128)(2,1)} async-done(((bf16[8,4,128,512]{3,2,1,0:T(8,128)(2,1)}), bf16[8,4,128,512]{3,2,1,0:T(8,128)(2,1)}, u32[]{:S(2)}, u32[]{:S(2)}) %all-to-all-start.1) | async-done | bytes 4194336 | tf_op jit(solution)/shard_map/all_to_all | solution.py:144
  203.2 25.6 %shard_map.74 = bf16[6,128,512]{2,1,0:T(8,128)(2,1)} custom-call(s32[6]{0:T(128)} %bitcast.96, bf16[32,128,512]{2,1,0:T(8,128)(2,1)} %bitcast.2.source_ref), custom_call_target="tpu_custom_call" | custom-call | tf_op jit(solution)/shard_map/pallas_call | solution.py:99
  228.8 0.0 all-gather.5.cloned.1.call-update
  228.9 0.0 copy-done.1
  228.9 0.1 slice.27
  229.0 6.4 %copy.49 = bf16[8192,256]{0,1:T(8,128)(2,1)} copy(bf16[8192,256]{1,0:T(8,128)(2,1)} %param.11) | data formatting | bytes 8388608 | tf_op jit(solution)/shard_map/reshape | solution.py:41
  235.3 0.0 all-gather.7.cloned.1.call-done
  235.3 0.0 copy-start
  235.3 4.4 %fusion.20 = bf16[193,256]{1,0:T(8,128)(2,1)S(1)} fusion(bf16[16,512,256]{2,1,0:T(8,128)(2,1)} %bitcast.98, bf16[16,256,512]{2,1,0:T(8,128)(2,1)} %bitcast.99), kind=kOutput, calls=%fused_computation.19 | convolution fusion | flops 809550080 | bytes 7569920 | tf_op jit(solution)/shard_map/srf,sfc->rc/dot_general | solution.py:122
  239.7 0.3 copy-done
  240.0 0.7 fusion.35
  240.7 0.7 copy.45
  241.3 8.3 %all-to-all-start.2 = ((f32[2,16,512]{2,0,1:T(2,128)}), f32[2,16,512]{2,0,1:T(2,128)S(1)}, u32[]{:S(2)}, u32[]{:S(2)}) async-start(f32[2,16,512]{2,0,1:T(2,128)} %bitcast.16), calls=%async_computation.2 | async-start | bytes 131072 | tf_op jit(solution)/shard_map/all_to_all | solution.py:45
  249.7 2.8 gather_fusion
  252.5 5.7 %all-to-all-done.2 = f32[2,16,512]{2,0,1:T(2,128)S(1)} async-done(((f32[2,16,512]{2,0,1:T(2,128)}), f32[2,16,512]{2,0,1:T(2,128)S(1)}, u32[]{:S(2)}, u32[]{:S(2)}) %all-to-all-start.2) | async-done | bytes 65568 | tf_op jit(solution)/shard_map/all_to_all | solution.py:45
  258.2 0.3 fusion.40
  258.6 13.2 %all_to_all.45 = f32[16,32,256]{2,1,0:T(8,128)S(1)} all-to-all(f32[16,32,256]{2,1,0:T(8,128)S(1)} %broadcast_in_dim.6), channel_id=1, replica_groups=mesh['dp'=8,'tensor'=16] {'tensor'}, dimensions={0} | all-to-all | bytes 1048576 | tf_op jit(solution)/shard_map/all_to_all | solution.py:55
  271.8 0.1 multiply_reduce_fusion
  271.9 0.2 fusion.31
  272.1 0.1 divide_convert_fusion.2
  272.3 0.1 fusion.32
  272.4 0.7 copy.40
  273.1 3.5 all-to-all-start.4
  276.6 7.5 %pad_maximum_fusion = bf16[16,512,512]{2,1,0:T(8,128)(2,1)} fusion(bf16[16,512,256]{2,1,0:T(8,128)(2,1)} %bitcast.87, bf16[16,512,256]{2,1,0:T(8,128)(2,1)} %bitcast.85), kind=kLoop, calls=%fused_computation.2 | loop fusion | flops 16777216 | bytes 16777216 | tf_op jit(solution)/shard_map/concatenate | solution.py:153
  284.2 0.9 all-to-all-done.4
  285.0 3.6 fusion.6
  288.7 33.8 %all-gather.5.cloned.1.call-done = bf16[96,128,512]{2,1,0:T(8,128)(2,1)} async-done(((bf16[6,128,512]{2,1,0:T(8,128)(2,1)}), bf16[96,128,512]{2,1,0:T(8,128)(2,1)}) %all-gather.5.cloned.1.call-update) | async-done | bytes 12582928 | tf_op jit(solution)/shard_map/all_gather | solution.py:150
  322.5 12.0 %bitcast_convert_fusion = bf16[6,128,512]{2,1,0:T(8,128)(2,1)S(1)} fusion(bf16[16,6,128,512]{3,2,1,0:T(8,128)(2,1)} %bitcast.97, bf16[16,512,512]{2,1,0:T(8,128)(2,1)} %pad_maximum_fusion), kind=kOutput, calls=%fused_computation.14 | convolution fusion | flops 6442844160 | bytes 21757952 | tf_op jit(solution)/shard_map/snkf,sfc->nkc/dot_general | solution.py:154
  334.6 0.1 fusion.38
  334.7 0.1 reshape_reshape.7
  334.8 0.3 convolution_multiply_fusion
  335.0 0.2 fusion.39
  335.3 0.1 reshape_reshape.6
  335.4 0.7 fusion.23
  336.1 0.1 copy.38
  336.2 3.2 convert_bitcast_fusion
  339.5 45.1 %all_to_all.46 = bf16[16,193,512]{2,1,0:T(8,128)(2,1)S(1)} all-to-all(bf16[16,193,512]{2,1,0:T(8,128)(2,1)S(1)} %convert_bitcast_fusion), channel_id=1, replica_groups=mesh['dp'=8,'tensor'=16] {'tensor'}, dimensions={0} | all-to-all | bytes 6324224 | tf_op jit(solution)/shard_map/all_to_all | solution.py:174
  384.5 0.5 reduce_sum.62
  385.1 0.8 concatenate.11
  (12 shorter events, 0.2 us)
Async XLA Ops:
  6.5 228.8 %all-gather.7.cloned.1.call-start = ((), (), s32[]{:S(2)}) async-start(), calls=%async_computation.7 | async-start | bytes 4456448 | tf_op jit(solution)/shard_map/all_gather | solution.py:121
  149.0 54.2 %all-to-all-start.1 = ((bf16[8,4,128,512]{3,2,1,0:T(8,128)(2,1)}), bf16[8,4,128,512]{3,2,1,0:T(8,128)(2,1)}, u32[]{:S(2)}, u32[]{:S(2)}) async-start(bf16[8,4,128,512]{3,2,1,0:T(8,128)(2,1)} %bitcast.83), calls=%async_computation.1 | async-start | bytes 8388608 | tf_op jit(solution)/shard_map/all_to_all | solution.py:144
  153.6 169.0 %all-gather.5.cloned.1.call-start = ((), (), s32[]{:S(2)}) async-start(), calls=%async_computation.6 | async-start | bytes 13369344 | tf_op jit(solution)/shard_map/all_gather | solution.py:150
  154.1 74.8 %copy-start.1 = (s32[8]{0:T(128)S(1)}, s32[8]{0:T(128)}, u32[]{:S(2)}) copy-start(s32[8]{0:T(128)} %multiply_add_fusion) | copy-start | bytes 100
  235.3 4.7 %copy-start = (bf16[8192,256]{0,1:T(8,128)(2,1)S(1)}, bf16[8192,256]{0,1:T(8,128)(2,1)}, u32[]{:S(2)}) copy-start(bf16[8192,256]{0,1:T(8,128)(2,1)} %copy.49) | copy-start | bytes 12582916
  241.3 16.8 %all-to-all-start.2 = ((f32[2,16,512]{2,0,1:T(2,128)}), f32[2,16,512]{2,0,1:T(2,128)S(1)}, u32[]{:S(2)}, u32[]{:S(2)}) async-start(f32[2,16,512]{2,0,1:T(2,128)} %bitcast.16), calls=%async_computation.2 | async-start | bytes 131072 | tf_op jit(solution)/shard_map/all_to_all | solution.py:45
  273.1 11.9 %all-to-all-start.4 = ((f32[16,2,512]{2,1,0:T(2,128)}), f32[16,2,512]{2,1,0:T(2,128)S(1)}, u32[]{:S(2)}, u32[]{:S(2)}) async-start(f32[16,2,512]{2,1,0:T(2,128)} %copy.40), calls=%async_computation.4 | async-start | bytes 131072 | tf_op jit(solution)/shard_map/all_to_all | solution.py:67
Sparse Core Ops, SparseCore 0:
  9.5 53.9 all-gather.6
  229.0 93.5 all-gather.4

commit v11 on v8

--- a/solution.py
+++ b/solution.py
@@ -50,17 +50,24 @@
     partial_scores = jnp.einsum(
         "hf,kf->hk", own_query, tail, precision=exact, preferred_element_type=jnp.float32
     )
-    all_scores = lax.all_to_all(
-        jnp.broadcast_to(partial_scores[None], (tensor_count,) + partial_scores.shape),
+    own_scores = lax.all_to_all(
+        partial_scores.reshape(tensor_count, heads_count, -1),
         "tensor",
         split_axis=0,
         concat_axis=0,
         tiled=True,
     )
-    scores = jnp.sum(all_scores, axis=0) / jnp.sqrt(jnp.float32(head_size))
+    scores = jnp.sum(own_scores, axis=0) / jnp.sqrt(jnp.float32(head_size))
     top_score = jnp.max(scores, axis=-1, keepdims=True)
     weights_raw = jnp.exp(scores - top_score)
-    soft = (weights_raw / jnp.sum(weights_raw, axis=-1, keepdims=True)).astype(jnp.bfloat16)
+    own_soft = (weights_raw / jnp.sum(weights_raw, axis=-1, keepdims=True)).astype(jnp.bfloat16)
+    soft = lax.all_to_all(
+        jnp.broadcast_to(own_soft[None], (tensor_count,) + own_soft.shape),
+        "tensor",
+        split_axis=0,
+        concat_axis=0,
+        tiled=True,
+    ).reshape(tensor_count * heads_count, -1)
     mixed_rows = jnp.einsum("hk,kf->hf", soft, tail, preferred_element_type=jnp.float32)
     own_rows = lax.all_to_all(
         mixed_rows.reshape(tensor_count, heads_count, col_count),

time: 247 us -> 246 us (level)
  waiting for transfers between devices: 90.7 us -> 81.2 us
  blocking collectives: 67.7 us -> 76.8 us
    all_gather x1, waiting for transfers between devices: 33.9 us -> 24.3 us  [shards(): main_parts = lax.all_gather(head_rows, 'tensor', axis=0, tiled=False)]
    all_to_all x1 -> x2, blocking collectives: 13.2 us -> 21.4 us  [the longest x1 10.8 us: last_token(): lax.all_to_all(jnp.broadcast_to(own_soft[None], (tensor_count,) + own_sof...]
where the time goes in v11:
time: 246 us
  waiting for transfers between devices  81.2 us (33%)
  blocking collectives  76.8 us (31%)
  matrix products  25.3 us (10%)
  local copies, waits for them, and re-layouts  22.3 us (9%)
  starting transfers between devices  16.6 us (7%)
  between operations  13.6 us (6%)
  other arithmetic  9.66 us (4%)
    all_to_all x1, waiting for transfers between devices, shards(): lax.all_to_all(outgoing, 'dp', split_axis=0, concat_axis=0, tiled=True)  49.6 us
    all_to_all x1, blocking collectives, shards(): lax.all_to_all(partial_out, 'tensor', split_axis=0, concat_axis=0, tiled=...  46 us
    all_gather x1, waiting for transfers between devices, shards(): main_parts = lax.all_gather(head_rows, 'tensor', axis=0, tiled=False)  24.3 us
    dot_general x1, matrix products, shards(): jnp.einsum('snkf,sfc->nkc', main_parts, w_both, preferred_element_type=jn...  12 us
    all_to_all x1, blocking collectives, last_token(): lax.all_to_all(jnp.broadcast_to(own_soft[None], (tensor_count,) + own_sof...  10.8 us
    all_to_all x1, blocking collectives, last_token(): lax.all_to_all(partial_scores.reshape(tensor_count, heads_count, -1), 'te...  10.6 us
    all_to_all x1, blocking collectives, shards(): lax.all_to_all(request_table, 'dp', split_axis=0, concat_axis=0, tiled=True)  9.49 us
    all_to_all x1, starting transfers between devices, last_token(): lax.all_to_all(spread_query.reshape(heads_count, tensor_count, col_count)...  8.48 us
  transfers between devices with their start and end apart: 5, of which 4 were waited for; matrix products, arithmetic and copies ran while one was open for 16% of the time, Pallas kernels for 0%

profile of v11, /device:TPU:0, one launch (start us, length us, event | category | flops | bytes accessed | tf_op | source)
XLA Modules:
  0.0 245.6 jit_solution(8849488270839154782)
XLA Ops:
  6.5 0.0 all-gather.7.cloned.1.call-start
  6.5 0.7 all-gather.7.cloned.1.call-update
  7.3 0.8 copy.33
  8.0 0.1 reshape.237
  8.1 0.2 convert_reduce_fusion
  8.3 0.1 iota_compare_fusion.1
  8.4 0.1 select_reduce_fusion
  8.5 0.1 copy.34
  8.6 9.5 %all_to_all.49 = s32[8,1,4]{2,1,0:T(1,128)S(1)} all-to-all(s32[8,1,4]{2,1,0:T(1,128)S(1)} %copy.34), channel_id=1, replica_groups=mesh['dp'=8,'tensor'=16] {'dp'}, dimensions={0} | all-to-all | bytes 256 | tf_op jit(solution)/shard_map/all_to_all | solution.py:122
  18.1 0.5 broadcast.201
  18.6 0.7 reduce.4
  19.2 0.1 reshape.253
  19.3 5.0 %gather_fusion = bf16[32,128,512]{2,1,0:T(8,128)(2,1)} fusion(bf16[32,128,512]{2,1,0:T(8,128)(2,1)} %param.9, s32[1024]{0:T(1024)S(1)} %pad_clamp_fusion.2), kind=kCustom, calls=%fused_computation | custom fusion | bytes 8388736 | tf_op jit(solution)/shard_map/jit(_take)/gather | solution.py:123
  24.3 4.6 %all-to-all-start.1 = ((bf16[8,4,128,512]{3,2,1,0:T(8,128)(2,1)}), bf16[8,4,128,512]{3,2,1,0:T(8,128)(2,1)}, u32[]{:S(2)}, u32[]{:S(2)}) async-start(bf16[8,4,128,512]{3,2,1,0:T(8,128)(2,1)} %bitcast.84), calls=%async_computation.1 | async-start | bytes 8388608 | tf_op jit(solution)/shard_map/all_to_all | solution.py:126
  28.9 0.0 all-gather.5.cloned.1.call-start
  29.0 49.6 %all-to-all-done.1 = bf16[8,4,128,512]{3,2,1,0:T(8,128)(2,1)} async-done(((bf16[8,4,128,512]{3,2,1,0:T(8,128)(2,1)}), bf16[8,4,128,512]{3,2,1,0:T(8,128)(2,1)}, u32[]{:S(2)}, u32[]{:S(2)}) %all-to-all-start.1) | async-done | bytes 4194336 | tf_op jit(solution)/shard_map/all_to_all | solution.py:126
  78.5 3.7 %gather_fusion.1 = bf16[6,128,512]{2,1,0:T(8,128)(2,1)} fusion(bf16[32,128,512]{2,1,0:T(8,128)(2,1)} %bitcast.2, s32[1024]{0:T(1024)S(1)} %pad_clamp_fusion.1), kind=kCustom, calls=%fused_computation.1 | custom fusion | bytes 1572888 | tf_op jit(solution)/shard_map/jit(_take)/gather | solution.py:130
  82.3 0.0 all-gather.5.cloned.1.call-update
  82.3 0.1 slice.27
  82.4 6.4 %copy.51 = bf16[8192,256]{0,1:T(8,128)(2,1)} copy(bf16[8192,256]{1,0:T(8,128)(2,1)} %param.11) | data formatting | bytes 8388608 | tf_op jit(solution)/shard_map/reshape | solution.py:39
  88.7 0.0 all-gather.7.cloned.1.call-done
  88.7 0.0 copy-start
  88.7 4.4 %fusion.20 = bf16[193,256]{1,0:T(8,128)(2,1)S(1)} fusion(bf16[16,512,256]{2,1,0:T(8,128)(2,1)} %bitcast.98, bf16[16,256,512]{2,1,0:T(8,128)(2,1)} %bitcast.99), kind=kOutput, calls=%fused_computation.21 | convolution fusion | flops 809550080 | bytes 7569920 | tf_op jit(solution)/shard_map/srf,sfc->rc/dot_general | solution.py:104
  93.1 0.3 copy-done
  93.4 0.7 fusion.37
  94.0 0.7 copy.47
  94.7 8.5 %all-to-all-start.2 = ((f32[2,16,512]{2,0,1:T(2,128)}), f32[2,16,512]{2,0,1:T(2,128)S(1)}, u32[]{:S(2)}, u32[]{:S(2)}) async-start(f32[2,16,512]{2,0,1:T(2,128)} %bitcast.16), calls=%async_computation.2 | async-start | bytes 131072 | tf_op jit(solution)/shard_map/all_to_all | solution.py:43
  103.2 2.8 %gather_fusion.2 = bf16[2,128,512]{2,1,0:T(8,128)(2,1)S(1)} fusion(bf16[32,128,512]{2,1,0:T(8,128)(2,1)} %bitcast.2, s32[1024]{0:T(1024)S(1)} %pad_clamp_fusion), kind=kCustom, calls=%fused_computation.2 | custom fusion | bytes 524296 | tf_op jit(solution)/shard_map/jit(_take)/gather | solution.py:131
  106.0 5.7 %all-to-all-done.2 = f32[2,16,512]{2,0,1:T(2,128)S(1)} async-done(((f32[2,16,512]{2,0,1:T(2,128)}), f32[2,16,512]{2,0,1:T(2,128)S(1)}, u32[]{:S(2)}, u32[]{:S(2)}) %all-to-all-start.2) | async-done | bytes 65568 | tf_op jit(solution)/shard_map/all_to_all | solution.py:43
  111.7 0.3 fusion.30
  112.1 10.6 %all_to_all.50 = f32[16,2,256]{2,1,0:T(2,128)S(1)} all-to-all(f32[16,2,256]{2,1,0:T(2,128)S(1)} %copy.40), channel_id=1, replica_groups=mesh['dp'=8,'tensor'=16] {'tensor'}, dimensions={0} | all-to-all | bytes 65536 | tf_op jit(solution)/shard_map/all_to_all | solution.py:53
  122.7 0.1 multiply_reduce_fusion
  122.8 0.2 fusion.40
  123.0 0.1 divide_convert_fusion.2
  123.1 10.8 %all_to_all.51 = bf16[16,2,256]{2,1,0:T(2,128)(2,1)S(1)} all-to-all(bf16[16,2,256]{2,1,0:T(2,128)(2,1)S(1)} %broadcast_in_dim.17), channel_id=1, replica_groups=mesh['dp'=8,'tensor'=16] {'tensor'}, dimensions={0} | all-to-all | bytes 32768 | tf_op jit(solution)/shard_map/all_to_all | solution.py:64
  133.9 0.1 fusion.34
  134.0 0.7 copy.42
  134.7 3.5 %all-to-all-start.5 = ((f32[16,2,512]{2,1,0:T(2,128)}), f32[16,2,512]{2,1,0:T(2,128)S(1)}, u32[]{:S(2)}, u32[]{:S(2)}) async-start(f32[16,2,512]{2,1,0:T(2,128)} %copy.42), calls=%async_computation.5 | async-start | bytes 131072 | tf_op jit(solution)/shard_map/all_to_all | solution.py:72
  138.2 7.4 %pad_maximum_fusion = bf16[16,512,512]{2,1,0:T(8,128)(2,1)} fusion(bf16[16,512,256]{2,1,0:T(8,128)(2,1)} %bitcast.88, bf16[16,512,256]{2,1,0:T(8,128)(2,1)} %bitcast.86), kind=kLoop, calls=%fused_computation.4 | loop fusion | flops 16777216 | bytes 16777216 | tf_op jit(solution)/shard_map/concatenate | solution.py:135
  145.7 1.0 all-to-all-done.5
  146.7 3.6 %fusion.6 = f32[2,1,128]{2,1,0:T(1,128)S(1)} fusion(f32[2,8192,1]{1,0,2:T(2,128)S(1)} %bitcast.93, bf16[8192,256]{1,0:T(8,128)(2,1)} %param.12), kind=kOutput, calls=%fused_computation.10 | convolution fusion | flops 25165824 | bytes 4260864 | tf_op jit(solution)/shard_map/hf,fhd->hd/dot_general | solution.py:80
  150.3 24.3 %all-gather.5.cloned.1.call-done = bf16[96,128,512]{2,1,0:T(8,128)(2,1)} async-done(((bf16[6,128,512]{2,1,0:T(8,128)(2,1)}), bf16[96,128,512]{2,1,0:T(8,128)(2,1)}) %all-gather.5.cloned.1.call-update) | async-done | bytes 12582928 | tf_op jit(solution)/shard_map/all_gather | solution.py:132
  174.6 12.0 %bitcast_convert_fusion = bf16[6,128,512]{2,1,0:T(8,128)(2,1)S(1)} fusion(bf16[16,6,128,512]{3,2,1,0:T(8,128)(2,1)} %bitcast.97, bf16[16,512,512]{2,1,0:T(8,128)(2,1)} %pad_maximum_fusion), kind=kOutput, calls=%fused_computation.16 | convolution fusion | flops 6442844160 | bytes 21757952 | tf_op jit(solution)/shard_map/snkf,sfc->nkc/dot_general | solution.py:136
  186.6 0.1 fusion.41
  186.7 0.1 reshape_reshape.7
  186.8 0.2 convolution_multiply_fusion
  187.1 0.2 fusion.42
  187.3 0.1 reshape_reshape.6
  187.4 0.7 fusion.23
  188.1 0.1 copy.38
  188.3 3.2 %convert_bitcast_fusion = bf16[16,193,512]{2,1,0:T(8,128)(2,1)S(1)} fusion(bf16[32,16,8,512]{3,2,1,0:T(8,128)(2,1)} %bitcast.87, bf16[1,256]{1,0:T(2,128)(2,1)S(1)} %bitcast.95, bf16[192,256]{1,0:T(8,128)(2,1)S(1)} %bitcast.91), kind=kOutput, calls=%fused_computation.15 | convolution fusion | flops 811279360 | bytes 7455232 | tf_op jit(solution)/shard_map/rc,csf->srf/dot_general | solution.py:150
  191.5 46.0 %all_to_all.52 = bf16[16,193,512]{2,1,0:T(8,128)(2,1)S(1)} all-to-all(bf16[16,193,512]{2,1,0:T(8,128)(2,1)S(1)} %convert_bitcast_fusion), channel_id=1, replica_groups=mesh['dp'=8,'tensor'=16] {'tensor'}, dimensions={0} | all-to-all | bytes 6324224 | tf_op jit(solution)/shard_map/all_to_all | solution.py:156
  237.4 0.5 reduce_sum.62
  238.0 0.8 concatenate.11
  (14 shorter events, 0.2 us)
Async XLA Ops:
  6.5 82.2 %all-gather.7.cloned.1.call-start = ((), (), s32[]{:S(2)}) async-start(), calls=%async_computation.8 | async-start | bytes 4456448 | tf_op jit(solution)/shard_map/all_gather | solution.py:103
  24.3 54.2 %all-to-all-start.1 = ((bf16[8,4,128,512]{3,2,1,0:T(8,128)(2,1)}), bf16[8,4,128,512]{3,2,1,0:T(8,128)(2,1)}, u32[]{:S(2)}, u32[]{:S(2)}) async-start(bf16[8,4,128,512]{3,2,1,0:T(8,128)(2,1)} %bitcast.84), calls=%async_computation.1 | async-start | bytes 8388608 | tf_op jit(solution)/shard_map/all_to_all | solution.py:126
  28.9 145.7 %all-gather.5.cloned.1.call-start = ((), (), s32[]{:S(2)}) async-start(), calls=%async_computation.7 | async-start | bytes 13369344 | tf_op jit(solution)/shard_map/all_gather | solution.py:132
  88.7 4.6 %copy-start = (bf16[8192,256]{0,1:T(8,128)(2,1)S(1)}, bf16[8192,256]{0,1:T(8,128)(2,1)}, u32[]{:S(2)}) copy-start(bf16[8192,256]{0,1:T(8,128)(2,1)} %copy.51) | copy-start | bytes 12582916
  94.7 17.0 %all-to-all-start.2 = ((f32[2,16,512]{2,0,1:T(2,128)}), f32[2,16,512]{2,0,1:T(2,128)S(1)}, u32[]{:S(2)}, u32[]{:S(2)}) async-start(f32[2,16,512]{2,0,1:T(2,128)} %bitcast.16), calls=%async_computation.2 | async-start | bytes 131072 | tf_op jit(solution)/shard_map/all_to_all | solution.py:43
  134.7 11.9 %all-to-all-start.5 = ((f32[16,2,512]{2,1,0:T(2,128)}), f32[16,2,512]{2,1,0:T(2,128)S(1)}, u32[]{:S(2)}, u32[]{:S(2)}) async-start(f32[16,2,512]{2,1,0:T(2,128)} %copy.42), calls=%async_computation.5 | async-start | bytes 131072 | tf_op jit(solution)/shard_map/all_to_all | solution.py:72
Sparse Core Ops, SparseCore 0:
  9.5 53.9 all-gather.6
  82.4 92.1 all-gather.4

commit v12 on v8

--- a/solution.py
+++ b/solution.py
@@ -2,6 +2,8 @@
 import jax.numpy as jnp
 from jax import lax
 from jax.sharding import PartitionSpec as P
+from jax.experimental import pallas as pl
+from jax.experimental.pallas import tpu as pltpu
 
 HD = 128
 
@@ -80,6 +82,26 @@
     return context.astype(jnp.bfloat16).reshape(-1)
 
 
+def copy_kernel(index_ref, source_ref, out_ref):
+    out_ref[...] = source_ref[...]
+
+
+def pick(source, index):
+    count = index.shape[0]
+    block = (1,) + source.shape[1:]
+    tail = (0,) * (source.ndim - 1)
+    return pl.pallas_call(
+        copy_kernel,
+        out_shape=jax.ShapeDtypeStruct((count,) + source.shape[1:], source.dtype),
+        grid_spec=pltpu.PrefetchScalarGridSpec(
+            num_scalar_prefetch=1,
+            grid=(count,),
+            in_specs=[pl.BlockSpec(block, lambda n, rows: (rows[n],) + tail)],
+            out_specs=pl.BlockSpec(block, lambda n, rows: (n,) + tail),
+        ),
+    )(jnp.clip(index, 0, source.shape[0] - 1), source)
+
+
 def shards(hidden, neighbour_ids, database, w_query, w_key, w_value, w_out):
     dp_count = lax.axis_size("dp")
     tok_rows = hidden.shape[0]
@@ -120,7 +142,7 @@
     arrived_rows = arrived.reshape(dp_count * capacity, ret_len, col_count)
     arrived_slot = owners * capacity + slot_rank
     main_rows = per_reader - 2
-    head_rows = jnp.take(arrived_rows, arrived_slot[:main_rows], axis=0, mode="clip")
+    head_rows = pick(arrived_rows, arrived_slot[:main_rows])
     tail_rows = jnp.take(arrived_rows, arrived_slot[main_rows:], axis=0, mode="clip")
     main_parts = lax.all_gather(head_rows, "tensor", axis=0, tiled=False)
     w_key_parts = w_key.reshape(tensor_count, col_count, head_cols)

time: 247 us -> 248 us (level)
  Pallas kernels: 0 us -> 4.85 us
  local copies, waits for them, and re-layouts: 22.4 us -> 18.6 us
    pallas_call x0 -> x1, Pallas kernels: none -> 4.85 us  [pick(): pl.pallas_call(copy_kernel, out_shape=jax.ShapeDtypeStruct((count,) + sou...]
    gather x1 -> x0, local copies, waits for them, and re-layouts: 3.74 us -> none  [shards(): jnp.take(arrived_rows, arrived_slot[:main_rows], axis=0, mode='clip')]
  transfers between devices with their start and end apart: 5 -> 5, of which waited for: 4 -> 4; matrix products, arithmetic and copies ran while one was open for 16% -> 15% of each run, Pallas kernels for 0% -> 2%
where the time goes in v12:
time: 248 us; the launch traced here: 247 us
  waiting for transfers between devices  90.2 us (36%)
  blocking collectives  67.7 us (27%)
  matrix products  25.4 us (10%)
  local copies, waits for them, and re-layouts  18.6 us (8%)
  starting transfers between devices  16.6 us (7%)
  between operations  13.6 us (5%)
  other arithmetic  10.3 us (4%)
  Pallas kernels  4.85 us (2%)
    all_to_all x1, waiting for transfers between devices, shards(): lax.all_to_all(outgoing, 'dp', split_axis=0, concat_axis=0, tiled=True)  49.1 us
    all_to_all x1, blocking collectives, shards(): lax.all_to_all(partial_out, 'tensor', split_axis=0, concat_axis=0, tiled=...  45.1 us
    all_gather x1, waiting for transfers between devices, shards(): main_parts = lax.all_gather(head_rows, 'tensor', axis=0, tiled=False)  33.9 us
    all_to_all x1, blocking collectives, last_token(): lax.all_to_all(jnp.broadcast_to(partial_scores[None], (tensor_count,) + p...  13.2 us
    dot_general x1, matrix products, shards(): jnp.einsum('snkf,sfc->nkc', main_parts, w_both, preferred_element_type=jn...  12 us
    all_to_all x1, blocking collectives, shards(): lax.all_to_all(request_table, 'dp', split_axis=0, concat_axis=0, tiled=True)  9.49 us
    all_to_all x1, starting transfers between devices, last_token(): lax.all_to_all(spread_query.reshape(heads_count, tensor_count, col_count)...  8.48 us
    concatenate x1, other arithmetic, shards(): jnp.concatenate([w_key_parts, w_value_parts], axis=2)  7.53 us
  transfers between devices with their start and end apart: 5, of which 4 were waited for; matrix products, arithmetic and copies ran while one was open for 15% of the time, Pallas kernels for 2%

profile of v12, /device:TPU:0, one launch (start us, length us, event | category | flops | bytes accessed | tf_op | source)
XLA Modules:
  0.0 247.3 jit_solution(3075391770691495555)
XLA Ops:
  6.5 0.0 all-gather.7.cloned.1.call-start
  6.5 0.7 all-gather.7.cloned.1.call-update
  7.3 0.8 copy.33
  8.0 0.1 reshape.262
  8.1 0.2 convert_reduce_fusion
  8.3 0.1 iota_compare_fusion
  8.4 0.1 select_reduce_fusion
  8.5 0.1 copy.34
  8.6 9.5 %all_to_all.44 = s32[8,1,4]{2,1,0:T(1,128)S(1)} all-to-all(s32[8,1,4]{2,1,0:T(1,128)S(1)} %copy.34), channel_id=1, replica_groups=mesh['dp'=8,'tensor'=16] {'dp'}, dimensions={0} | all-to-all | bytes 256 | tf_op jit(solution)/shard_map/all_to_all | solution.py:137
  18.1 0.5 broadcast.224
  18.6 0.7 reduce.4
  19.2 0.1 reshape.279
  19.3 5.0 %gather_fusion = bf16[32,128,512]{2,1,0:T(8,128)(2,1)} fusion(bf16[32,128,512]{2,1,0:T(8,128)(2,1)} %param.9, s32[1024]{0:T(1024)S(1)} %pad_clamp_fusion.1), kind=kCustom, calls=%fused_computation | custom fusion | bytes 8388736 | tf_op jit(solution)/shard_map/jit(_take)/gather | solution.py:138
  24.3 4.6 %all-to-all-start.1 = ((bf16[8,4,128,512]{3,2,1,0:T(8,128)(2,1)}), bf16[8,4,128,512]{3,2,1,0:T(8,128)(2,1)}, u32[]{:S(2)}, u32[]{:S(2)}) async-start(bf16[8,4,128,512]{3,2,1,0:T(8,128)(2,1)} %bitcast.82), calls=%async_computation.1 | async-start | bytes 8388608 | tf_op jit(solution)/shard_map/all_to_all | solution.py:141
  28.9 0.0 all-gather.5.cloned.1.call-start
  29.0 0.5 slice_clamp_fusion.index_ref
  29.5 49.1 %all-to-all-done.1 = bf16[8,4,128,512]{3,2,1,0:T(8,128)(2,1)} async-done(((bf16[8,4,128,512]{3,2,1,0:T(8,128)(2,1)}), bf16[8,4,128,512]{3,2,1,0:T(8,128)(2,1)}, u32[]{:S(2)}, u32[]{:S(2)}) %all-to-all-start.1) | async-done | bytes 4194336 | tf_op jit(solution)/shard_map/all_to_all | solution.py:141
  78.5 4.8 %shard_map.73 = bf16[6,128,512]{2,1,0:T(8,128)(2,1)} custom-call(s32[6]{0:T(128)} %slice_clamp_fusion.index_ref, bf16[32,128,512]{2,1,0:T(8,128)(2,1)} %bitcast.2.source_ref), custom_call_target="tpu_custom_call" | custom-call | tf_op jit(solution)/shard_map/pallas_call | solution.py:93
  83.4 0.0 all-gather.5.cloned.1.call-update
  83.4 0.1 slice.27
  83.5 6.4 %copy.49 = bf16[8192,256]{0,1:T(8,128)(2,1)} copy(bf16[8192,256]{1,0:T(8,128)(2,1)} %param.11) | data formatting | bytes 8388608 | tf_op jit(solution)/shard_map/reshape | solution.py:41
  89.8 0.0 all-gather.7.cloned.1.call-done
  89.8 0.0 copy-start
  89.8 4.4 %fusion.20 = bf16[193,256]{1,0:T(8,128)(2,1)S(1)} fusion(bf16[16,512,256]{2,1,0:T(8,128)(2,1)} %bitcast.96, bf16[16,256,512]{2,1,0:T(8,128)(2,1)} %bitcast.97), kind=kOutput, calls=%fused_computation.20 | convolution fusion | flops 809550080 | bytes 7569920 | tf_op jit(solution)/shard_map/srf,sfc->rc/dot_general | solution.py:119
  94.2 0.3 copy-done
  94.5 0.7 fusion.35
  95.1 0.7 copy.45
  95.8 8.5 %all-to-all-start.2 = ((f32[2,16,512]{2,0,1:T(2,128)}), f32[2,16,512]{2,0,1:T(2,128)S(1)}, u32[]{:S(2)}, u32[]{:S(2)}) async-start(f32[2,16,512]{2,0,1:T(2,128)} %bitcast.16), calls=%async_computation.2 | async-start | bytes 131072 | tf_op jit(solution)/shard_map/all_to_all | solution.py:45
  104.3 2.8 %gather_fusion.1 = bf16[2,128,512]{2,1,0:T(8,128)(2,1)S(1)} fusion(bf16[32,128,512]{2,1,0:T(8,128)(2,1)} %bitcast.2.source_ref, s32[1024]{0:T(1024)S(1)} %pad_clamp_fusion), kind=kCustom, calls=%fused_computation.1 | custom fusion | bytes 524296 | tf_op jit(solution)/shard_map/jit(_take)/gather | solution.py:146
  107.1 5.7 %all-to-all-done.2 = f32[2,16,512]{2,0,1:T(2,128)S(1)} async-done(((f32[2,16,512]{2,0,1:T(2,128)}), f32[2,16,512]{2,0,1:T(2,128)S(1)}, u32[]{:S(2)}, u32[]{:S(2)}) %all-to-all-start.2) | async-done | bytes 65568 | tf_op jit(solution)/shard_map/all_to_all | solution.py:45
  112.8 0.3 fusion.40
  113.2 13.2 %all_to_all.45 = f32[16,32,256]{2,1,0:T(8,128)S(1)} all-to-all(f32[16,32,256]{2,1,0:T(8,128)S(1)} %broadcast_in_dim.10), channel_id=1, replica_groups=mesh['dp'=8,'tensor'=16] {'tensor'}, dimensions={0} | all-to-all | bytes 1048576 | tf_op jit(solution)/shard_map/all_to_all | solution.py:55
  126.4 0.1 multiply_reduce_fusion
  126.6 0.2 fusion.31
  126.7 0.1 divide_convert_fusion.2
  126.9 0.1 fusion.32
  127.0 0.7 copy.40
  127.7 3.5 %all-to-all-start.4 = ((f32[16,2,512]{2,1,0:T(2,128)}), f32[16,2,512]{2,1,0:T(2,128)S(1)}, u32[]{:S(2)}, u32[]{:S(2)}) async-start(f32[16,2,512]{2,1,0:T(2,128)} %copy.40), calls=%async_computation.4 | async-start | bytes 131072 | tf_op jit(solution)/shard_map/all_to_all | solution.py:67
  131.2 7.5 %pad_maximum_fusion = bf16[16,512,512]{2,1,0:T(8,128)(2,1)} fusion(bf16[16,512,256]{2,1,0:T(8,128)(2,1)} %bitcast.86, bf16[16,512,256]{2,1,0:T(8,128)(2,1)} %bitcast.84), kind=kLoop, calls=%fused_computation.3 | loop fusion | flops 16777216 | bytes 16777216 | tf_op jit(solution)/shard_map/concatenate | solution.py:150
  138.8 0.9 all-to-all-done.4
  139.6 3.6 %fusion.6 = f32[2,1,128]{2,1,0:T(1,128)S(1)} fusion(f32[2,8192,1]{1,0,2:T(2,128)S(1)} %bitcast.92, bf16[8192,256]{1,0:T(8,128)(2,1)} %param.12), kind=kOutput, calls=%fused_computation.9 | convolution fusion | flops 25165824 | bytes 4260864 | tf_op jit(solution)/shard_map/hf,fhd->hd/dot_general | solution.py:75
  143.3 33.9 %all-gather.5.cloned.1.call-done = bf16[96,128,512]{2,1,0:T(8,128)(2,1)} async-done(((bf16[6,128,512]{2,1,0:T(8,128)(2,1)}), bf16[96,128,512]{2,1,0:T(8,128)(2,1)}) %all-gather.5.cloned.1.call-update) | async-done | bytes 12582928 | tf_op jit(solution)/shard_map/all_gather | solution.py:147
  177.2 12.0 %bitcast_convert_fusion = bf16[6,128,512]{2,1,0:T(8,128)(2,1)S(1)} fusion(bf16[16,6,128,512]{3,2,1,0:T(8,128)(2,1)} %bitcast.95, bf16[16,512,512]{2,1,0:T(8,128)(2,1)} %pad_maximum_fusion), kind=kOutput, calls=%fused_computation.15 | convolution fusion | flops 6442844160 | bytes 21757952 | tf_op jit(solution)/shard_map/snkf,sfc->nkc/dot_general | solution.py:151
  189.2 0.1 fusion.38
  189.3 0.1 reshape_reshape.7
  189.4 0.3 convolution_multiply_fusion
  189.7 0.2 fusion.39
  189.9 0.1 reshape_reshape.6
  190.0 0.7 fusion.23
  190.7 0.1 copy.38
  190.9 3.2 %convert_bitcast_fusion = bf16[16,193,512]{2,1,0:T(8,128)(2,1)S(1)} fusion(bf16[32,16,8,512]{3,2,1,0:T(8,128)(2,1)} %bitcast.85, bf16[1,256]{1,0:T(2,128)(2,1)S(1)} %bitcast.94, bf16[192,256]{1,0:T(8,128)(2,1)S(1)} %bitcast.89), kind=kOutput, calls=%fused_computation.14 | convolution fusion | flops 811279360 | bytes 7455232 | tf_op jit(solution)/shard_map/rc,csf->srf/dot_general | solution.py:165
  194.1 45.1 %all_to_all.46 = bf16[16,193,512]{2,1,0:T(8,128)(2,1)S(1)} all-to-all(bf16[16,193,512]{2,1,0:T(8,128)(2,1)S(1)} %convert_bitcast_fusion), channel_id=1, replica_groups=mesh['dp'=8,'tensor'=16] {'tensor'}, dimensions={0} | all-to-all | bytes 6324224 | tf_op jit(solution)/shard_map/all_to_all | solution.py:171
  239.1 0.5 reduce_sum.62
  239.7 0.8 concatenate.11
  (14 shorter events, 0.2 us)
Async XLA Ops:
  6.5 83.3 %all-gather.7.cloned.1.call-start = ((), (), s32[]{:S(2)}) async-start(), calls=%async_computation.7 | async-start | bytes 4456448 | tf_op jit(solution)/shard_map/all_gather | solution.py:118
  24.3 54.2 %all-to-all-start.1 = ((bf16[8,4,128,512]{3,2,1,0:T(8,128)(2,1)}), bf16[8,4,128,512]{3,2,1,0:T(8,128)(2,1)}, u32[]{:S(2)}, u32[]{:S(2)}) async-start(bf16[8,4,128,512]{3,2,1,0:T(8,128)(2,1)} %bitcast.82), calls=%async_computation.1 | async-start | bytes 8388608 | tf_op jit(solution)/shard_map/all_to_all | solution.py:141
  28.9 148.3 %all-gather.5.cloned.1.call-start = ((), (), s32[]{:S(2)}) async-start(), calls=%async_computation.6 | async-start | bytes 13369344 | tf_op jit(solution)/shard_map/all_gather | solution.py:147
  89.8 4.6 %copy-start = (bf16[8192,256]{0,1:T(8,128)(2,1)S(1)}, bf16[8192,256]{0,1:T(8,128)(2,1)}, u32[]{:S(2)}) copy-start(bf16[8192,256]{0,1:T(8,128)(2,1)} %copy.49) | copy-start | bytes 12582916
  95.8 17.0 %all-to-all-start.2 = ((f32[2,16,512]{2,0,1:T(2,128)}), f32[2,16,512]{2,0,1:T(2,128)S(1)}, u32[]{:S(2)}, u32[]{:S(2)}) async-start(f32[2,16,512]{2,0,1:T(2,128)} %bitcast.16), calls=%async_computation.2 | async-start | bytes 131072 | tf_op jit(solution)/shard_map/all_to_all | solution.py:45
  127.7 11.9 %all-to-all-start.4 = ((f32[16,2,512]{2,1,0:T(2,128)}), f32[16,2,512]{2,1,0:T(2,128)S(1)}, u32[]{:S(2)}, u32[]{:S(2)}) async-start(f32[16,2,512]{2,1,0:T(2,128)} %copy.40), calls=%async_computation.4 | async-start | bytes 131072 | tf_op jit(solution)/shard_map/all_to_all | solution.py:67
Sparse Core Ops, SparseCore 0:
  9.5 53.9 all-gather.6
  83.5 93.5 all-gather.4

commit v13 on v8

--- a/solution.py
+++ b/solution.py
@@ -139,7 +139,6 @@
         query_rows[main_groups * group_len], tail_rows, w_key, w_value, heads_local
     )
     live = jnp.concatenate([main_live, last_live[None]], 0)
-    live_rows = live.shape[0]
     partial_out = jnp.einsum(
         "rc,csf->srf",
         live,
@@ -148,7 +147,9 @@
     ).astype(jnp.bfloat16)
     spread = lax.all_to_all(partial_out, "tensor", split_axis=0, concat_axis=0, tiled=True)
     summed = jnp.sum(spread.astype(jnp.float32), axis=0).astype(jnp.bfloat16)
-    return jnp.concatenate([jnp.zeros((group_len - 1, summed.shape[1]), jnp.bfloat16), summed], 0)
+    return lax.dynamic_update_slice(
+        jnp.zeros((tok_rows, summed.shape[1]), jnp.bfloat16), summed, (group_len - 1, 0)
+    )
 
 
 def solution(mesh):
@@ -161,6 +162,7 @@
         P(None, "tensor"),
         P("tensor", None),
     )
+
     return jax.shard_map(
         shards, mesh=mesh, in_specs=placed, out_specs=P("dp", "tensor"), check_vma=False
     )

time: 247 us -> 247 us (level)
  no operation moved by 1% of the time
where the time goes in v13:
time: 247 us; the launch traced here: 246 us
  waiting for transfers between devices  90.7 us (37%)
  blocking collectives  67.7 us (27%)
  matrix products  25.3 us (10%)
  local copies, waits for them, and re-layouts  22.4 us (9%)
  starting transfers between devices  16.6 us (7%)
  between operations  13.6 us (6%)
  other arithmetic  9.79 us (4%)
    all_to_all x1, waiting for transfers between devices, shards(): lax.all_to_all(outgoing, 'dp', split_axis=0, concat_axis=0, tiled=True)  49.6 us
    all_to_all x1, blocking collectives, shards(): lax.all_to_all(partial_out, 'tensor', split_axis=0, concat_axis=0, tiled=...  45.1 us
    all_gather x1, waiting for transfers between devices, shards(): main_parts = lax.all_gather(head_rows, 'tensor', axis=0, tiled=False)  33.9 us
    all_to_all x1, blocking collectives, last_token(): lax.all_to_all(jnp.broadcast_to(partial_scores[None], (tensor_count,) + p...  13.2 us
    dot_general x1, matrix products, shards(): jnp.einsum('snkf,sfc->nkc', main_parts, w_both, preferred_element_type=jn...  12 us
    all_to_all x1, blocking collectives, shards(): lax.all_to_all(request_table, 'dp', split_axis=0, concat_axis=0, tiled=True)  9.49 us
    all_to_all x1, starting transfers between devices, last_token(): lax.all_to_all(spread_query.reshape(heads_count, tensor_count, col_count)...  8.48 us
    concatenate x1, other arithmetic, shards(): jnp.concatenate([w_key_parts, w_value_parts], axis=2)  7.53 us
  transfers between devices with their start and end apart: 5, of which 4 were waited for; matrix products, arithmetic and copies ran while one was open for 16% of the time, Pallas kernels for 0%

profile of v13, /device:TPU:0, one launch (start us, length us, event | category | flops | bytes accessed | tf_op | source)
XLA Modules:
  0.0 246.2 jit_solution(1433890594481959822)
XLA Ops:
  6.5 0.0 all-gather.7.cloned.1.call-start
  6.5 0.7 all-gather.7.cloned.1.call-update
  7.3 0.8 copy.32
  8.0 0.1 reshape.262
  8.1 0.2 convert_reduce_fusion
  8.3 0.1 iota_compare_fusion.1
  8.4 0.1 select_reduce_fusion
  8.5 0.1 copy.33
  8.6 9.5 %all_to_all.44 = s32[8,1,4]{2,1,0:T(1,128)S(1)} all-to-all(s32[8,1,4]{2,1,0:T(1,128)S(1)} %copy.33), channel_id=1, replica_groups=mesh['dp'=8,'tensor'=16] {'dp'}, dimensions={0} | all-to-all | bytes 256 | tf_op jit(solution)/shard_map/all_to_all | solution.py:115
  18.1 0.5 broadcast.228
  18.6 0.7 reduce.4
  19.2 0.1 reshape.279
  19.3 5.0 %gather_fusion = bf16[32,128,512]{2,1,0:T(8,128)(2,1)} fusion(bf16[32,128,512]{2,1,0:T(8,128)(2,1)} %param.9, s32[1024]{0:T(1024)S(1)} %pad_clamp_fusion.2), kind=kCustom, calls=%fused_computation | custom fusion | bytes 8388736 | tf_op jit(solution)/shard_map/jit(_take)/gather | solution.py:116
  24.3 4.6 %all-to-all-start.1 = ((bf16[8,4,128,512]{3,2,1,0:T(8,128)(2,1)}), bf16[8,4,128,512]{3,2,1,0:T(8,128)(2,1)}, u32[]{:S(2)}, u32[]{:S(2)}) async-start(bf16[8,4,128,512]{3,2,1,0:T(8,128)(2,1)} %bitcast.83), calls=%async_computation.1 | async-start | bytes 8388608 | tf_op jit(solution)/shard_map/all_to_all | solution.py:119
  28.9 0.0 all-gather.5.cloned.1.call-start
  29.0 49.6 %all-to-all-done.1 = bf16[8,4,128,512]{3,2,1,0:T(8,128)(2,1)} async-done(((bf16[8,4,128,512]{3,2,1,0:T(8,128)(2,1)}), bf16[8,4,128,512]{3,2,1,0:T(8,128)(2,1)}, u32[]{:S(2)}, u32[]{:S(2)}) %all-to-all-start.1) | async-done | bytes 4194336 | tf_op jit(solution)/shard_map/all_to_all | solution.py:119
  78.5 3.7 %gather_fusion.1 = bf16[6,128,512]{2,1,0:T(8,128)(2,1)} fusion(bf16[32,128,512]{2,1,0:T(8,128)(2,1)} %bitcast.2, s32[1024]{0:T(1024)S(1)} %pad_clamp_fusion.1), kind=kCustom, calls=%fused_computation.1 | custom fusion | bytes 1572888 | tf_op jit(solution)/shard_map/jit(_take)/gather | solution.py:123
  82.3 0.0 all-gather.5.cloned.1.call-update
  82.3 0.1 slice.27
  82.4 6.4 %copy.48 = bf16[8192,256]{0,1:T(8,128)(2,1)} copy(bf16[8192,256]{1,0:T(8,128)(2,1)} %param.11) | data formatting | bytes 8388608 | tf_op jit(solution)/shard_map/reshape | solution.py:39
  88.7 0.0 all-gather.7.cloned.1.call-done
  88.7 0.0 copy-start
  88.7 4.4 %fusion.20 = bf16[193,256]{1,0:T(8,128)(2,1)S(1)} fusion(bf16[16,512,256]{2,1,0:T(8,128)(2,1)} %bitcast.98, bf16[16,256,512]{2,1,0:T(8,128)(2,1)} %bitcast.99), kind=kOutput, calls=%fused_computation.21 | convolution fusion | flops 809550080 | bytes 7569920 | tf_op jit(solution)/shard_map/srf,sfc->rc/dot_general | solution.py:97
  93.1 0.3 copy-done
  93.4 0.7 fusion.35
  94.0 0.7 copy.44
  94.7 8.5 %all-to-all-start.2 = ((f32[2,16,512]{2,0,1:T(2,128)}), f32[2,16,512]{2,0,1:T(2,128)S(1)}, u32[]{:S(2)}, u32[]{:S(2)}) async-start(f32[2,16,512]{2,0,1:T(2,128)} %bitcast.16), calls=%async_computation.2 | async-start | bytes 131072 | tf_op jit(solution)/shard_map/all_to_all | solution.py:43
  103.2 2.8 %gather_fusion.2 = bf16[2,128,512]{2,1,0:T(8,128)(2,1)S(1)} fusion(bf16[32,128,512]{2,1,0:T(8,128)(2,1)} %bitcast.2, s32[1024]{0:T(1024)S(1)} %pad_clamp_fusion), kind=kCustom, calls=%fused_computation.2 | custom fusion | bytes 524296 | tf_op jit(solution)/shard_map/jit(_take)/gather | solution.py:124
  106.0 5.7 %all-to-all-done.2 = f32[2,16,512]{2,0,1:T(2,128)S(1)} async-done(((f32[2,16,512]{2,0,1:T(2,128)}), f32[2,16,512]{2,0,1:T(2,128)S(1)}, u32[]{:S(2)}, u32[]{:S(2)}) %all-to-all-start.2) | async-done | bytes 65568 | tf_op jit(solution)/shard_map/all_to_all | solution.py:43
  111.7 0.3 fusion.40
  112.1 13.2 %all_to_all.45 = f32[16,32,256]{2,1,0:T(8,128)S(1)} all-to-all(f32[16,32,256]{2,1,0:T(8,128)S(1)} %broadcast_in_dim.17), channel_id=1, replica_groups=mesh['dp'=8,'tensor'=16] {'tensor'}, dimensions={0} | all-to-all | bytes 1048576 | tf_op jit(solution)/shard_map/all_to_all | solution.py:53
  125.3 0.1 multiply_reduce_fusion
  125.4 0.2 fusion.31
  125.6 0.1 divide_convert_fusion.2
  125.8 0.1 fusion.32
  125.9 0.7 copy.39
  126.6 3.5 %all-to-all-start.4 = ((f32[16,2,512]{2,1,0:T(2,128)}), f32[16,2,512]{2,1,0:T(2,128)S(1)}, u32[]{:S(2)}, u32[]{:S(2)}) async-start(f32[16,2,512]{2,1,0:T(2,128)} %copy.39), calls=%async_computation.4 | async-start | bytes 131072 | tf_op jit(solution)/shard_map/all_to_all | solution.py:65
  130.1 7.5 %pad_maximum_fusion = bf16[16,512,512]{2,1,0:T(8,128)(2,1)} fusion(bf16[16,512,256]{2,1,0:T(8,128)(2,1)} %bitcast.87, bf16[16,512,256]{2,1,0:T(8,128)(2,1)} %bitcast.85), kind=kLoop, calls=%fused_computation.4 | loop fusion | flops 16777216 | bytes 16777216 | tf_op jit(solution)/shard_map/concatenate | solution.py:128
  137.7 0.9 all-to-all-done.4
  138.5 3.6 %fusion.6 = f32[2,1,128]{2,1,0:T(1,128)S(1)} fusion(f32[2,8192,1]{1,0,2:T(2,128)S(1)} %bitcast.93, bf16[8192,256]{1,0:T(8,128)(2,1)} %param.12), kind=kOutput, calls=%fused_computation.10 | convolution fusion | flops 25165824 | bytes 4260864 | tf_op jit(solution)/shard_map/hf,fhd->hd/dot_general | solution.py:73
  142.2 33.9 %all-gather.5.cloned.1.call-done = bf16[96,128,512]{2,1,0:T(8,128)(2,1)} async-done(((bf16[6,128,512]{2,1,0:T(8,128)(2,1)}), bf16[96,128,512]{2,1,0:T(8,128)(2,1)}) %all-gather.5.cloned.1.call-update) | async-done | bytes 12582928 | tf_op jit(solution)/shard_map/all_gather | solution.py:125
  176.1 12.0 %bitcast_convert_fusion = bf16[6,128,512]{2,1,0:T(8,128)(2,1)S(1)} fusion(bf16[16,6,128,512]{3,2,1,0:T(8,128)(2,1)} %bitcast.97, bf16[16,512,512]{2,1,0:T(8,128)(2,1)} %pad_maximum_fusion), kind=kOutput, calls=%fused_computation.16 | convolution fusion | flops 6442844160 | bytes 21757952 | tf_op jit(solution)/shard_map/snkf,sfc->nkc/dot_general | solution.py:129
  188.1 0.1 fusion.38
  188.2 0.1 reshape_reshape.7
  188.3 0.2 convolution_multiply_fusion
  188.6 0.2 fusion.39
  188.8 0.1 reshape_reshape.6
  188.9 0.7 fusion.23
  189.6 0.1 copy.37
  189.8 3.2 %convert_bitcast_fusion = bf16[16,193,512]{2,1,0:T(8,128)(2,1)S(1)} fusion(bf16[32,16,8,512]{3,2,1,0:T(8,128)(2,1)} %bitcast.86, bf16[1,256]{1,0:T(2,128)(2,1)S(1)} %bitcast.95, bf16[192,256]{1,0:T(8,128)(2,1)S(1)} %bitcast.90), kind=kOutput, calls=%fused_computation.15 | convolution fusion | flops 811279360 | bytes 7455232 | tf_op jit(solution)/shard_map/rc,csf->srf/dot_general | solution.py:142
  193.0 45.1 %all_to_all.46 = bf16[16,193,512]{2,1,0:T(8,128)(2,1)S(1)} all-to-all(bf16[16,193,512]{2,1,0:T(8,128)(2,1)S(1)} %convert_bitcast_fusion), channel_id=1, replica_groups=mesh['dp'=8,'tensor'=16] {'tensor'}, dimensions={0} | all-to-all | bytes 6324224 | tf_op jit(solution)/shard_map/all_to_all | solution.py:148
  238.0 0.5 reduce_sum.62
  238.6 0.8 dynamic_update_slice.3
  (15 shorter events, 0.3 us)
Async XLA Ops:
  6.5 82.2 %all-gather.7.cloned.1.call-start = ((), (), s32[]{:S(2)}) async-start(), calls=%async_computation.7 | async-start | bytes 4456448 | tf_op jit(solution)/shard_map/all_gather | solution.py:96
  24.3 54.2 %all-to-all-start.1 = ((bf16[8,4,128,512]{3,2,1,0:T(8,128)(2,1)}), bf16[8,4,128,512]{3,2,1,0:T(8,128)(2,1)}, u32[]{:S(2)}, u32[]{:S(2)}) async-start(bf16[8,4,128,512]{3,2,1,0:T(8,128)(2,1)} %bitcast.83), calls=%async_computation.1 | async-start | bytes 8388608 | tf_op jit(solution)/shard_map/all_to_all | solution.py:119
  28.9 147.2 %all-gather.5.cloned.1.call-start = ((), (), s32[]{:S(2)}) async-start(), calls=%async_computation.6 | async-start | bytes 13369344 | tf_op jit(solution)/shard_map/all_gather | solution.py:125
  88.7 4.6 %copy-start = (bf16[8192,256]{0,1:T(8,128)(2,1)S(1)}, bf16[8192,256]{0,1:T(8,128)(2,1)}, u32[]{:S(2)}) copy-start(bf16[8192,256]{0,1:T(8,128)(2,1)} %copy.48) | copy-start | bytes 12582916
  94.7 17.0 %all-to-all-start.2 = ((f32[2,16,512]{2,0,1:T(2,128)}), f32[2,16,512]{2,0,1:T(2,128)S(1)}, u32[]{:S(2)}, u32[]{:S(2)}) async-start(f32[2,16,512]{2,0,1:T(2,128)} %bitcast.16), calls=%async_computation.2 | async-start | bytes 131072 | tf_op jit(solution)/shard_map/all_to_all | solution.py:43
  126.6 11.9 %all-to-all-start.4 = ((f32[16,2,512]{2,1,0:T(2,128)}), f32[16,2,512]{2,1,0:T(2,128)S(1)}, u32[]{:S(2)}, u32[]{:S(2)}) async-start(f32[16,2,512]{2,1,0:T(2,128)} %copy.39), calls=%async_computation.4 | async-start | bytes 131072 | tf_op jit(solution)/shard_map/all_to_all | solution.py:65
Sparse Core Ops, SparseCore 0:
  9.5 53.9 all-gather.6
  82.4 93.5 all-gather.4

commit v14 on v8

--- a/solution.py
+++ b/solution.py
@@ -80,6 +80,12 @@
     return context.astype(jnp.bfloat16).reshape(-1)
 
 
+def pick(source, index):
+    return jnp.stack(
+        [lax.dynamic_index_in_dim(source, index[n], 0, keepdims=False) for n in range(index.shape[0])], 0
+    )
+
+
 def shards(hidden, neighbour_ids, database, w_query, w_key, w_value, w_out):
     dp_count = lax.axis_size("dp")
     tok_rows = hidden.shape[0]
@@ -120,7 +126,7 @@
     arrived_rows = arrived.reshape(dp_count * capacity, ret_len, col_count)
     arrived_slot = owners * capacity + slot_rank
     main_rows = per_reader - 2
-    head_rows = jnp.take(arrived_rows, arrived_slot[:main_rows], axis=0, mode="clip")
+    head_rows = pick(arrived_rows, arrived_slot[:main_rows])
     tail_rows = jnp.take(arrived_rows, arrived_slot[main_rows:], axis=0, mode="clip")
     main_parts = lax.all_gather(head_rows, "tensor", axis=0, tiled=False)
     w_key_parts = w_key.reshape(tensor_count, col_count, head_cols)

time: 247 us -> 250 us (1.012)
  waiting for transfers between devices: 90.7 us -> 79 us
  between operations: 13.6 us -> 24.7 us
  local copies, waits for them, and re-layouts: 22.4 us -> 25.8 us
    all_to_all x1, waiting for transfers between devices: 49.6 us -> 37.8 us  [shards(): lax.all_to_all(outgoing, 'dp', split_axis=0, concat_axis=0, tiled=True)]
    unnamed x5 -> x12, local copies, waits for them, and re-layouts: 1.07 us -> 6.59 us
    gather x1 -> x0, local copies, waits for them, and re-layouts: 3.74 us -> none  [shards(): jnp.take(arrived_rows, arrived_slot[:main_rows], axis=0, mode='clip')]
  transfers between devices with their start and end apart: 5 -> 5, of which waited for: 4 -> 4; matrix products, arithmetic and copies ran while one was open for 16% -> 17% of each run, Pallas kernels for 0% -> 0%
where the time goes in v14:
time: 250 us; the launch traced here: 249 us
  waiting for transfers between devices  79 us (32%)
  blocking collectives  67.7 us (27%)
  local copies, waits for them, and re-layouts  25.8 us (10%)
  matrix products  25.4 us (10%)
  between operations  24.7 us (10%)
  starting transfers between devices  16.6 us (7%)
  other arithmetic  9.78 us (4%)
    all_to_all x1, blocking collectives, shards(): lax.all_to_all(partial_out, 'tensor', split_axis=0, concat_axis=0, tiled=...  45.1 us
    all_to_all x1, waiting for transfers between devices, shards(): lax.all_to_all(outgoing, 'dp', split_axis=0, concat_axis=0, tiled=True)  37.8 us
    all_gather x1, waiting for transfers between devices, shards(): main_parts = lax.all_gather(head_rows, 'tensor', axis=0, tiled=False)  33.9 us
    all_to_all x1, blocking collectives, last_token(): lax.all_to_all(jnp.broadcast_to(partial_scores[None], (tensor_count,) + p...  13.2 us
    dot_general x1, matrix products, shards(): jnp.einsum('snkf,sfc->nkc', main_parts, w_both, preferred_element_type=jn...  12 us
    all_to_all x1, blocking collectives, shards(): lax.all_to_all(request_table, 'dp', split_axis=0, concat_axis=0, tiled=True)  9.49 us
    all_to_all x1, starting transfers between devices, last_token(): lax.all_to_all(spread_query.reshape(heads_count, tensor_count, col_count)...  8.48 us
    concatenate x1, other arithmetic, shards(): jnp.concatenate([w_key_parts, w_value_parts], axis=2)  7.53 us
  transfers between devices with their start and end apart: 5, of which 4 were waited for; matrix products, arithmetic and copies ran while one was open for 17% of the time, Pallas kernels for 0%

profile of v14, /device:TPU:0, one launch (start us, length us, event | category | flops | bytes accessed | tf_op | source)
XLA Modules:
  0.0 248.9 jit_solution(12210289831689209234)
XLA Ops:
  6.5 0.0 all-gather.7.cloned.1.call-start
  6.5 0.7 all-gather.7.cloned.1.call-update
  7.3 0.8 copy.32
  8.0 0.1 reshape.262
  8.1 0.2 convert_reduce_fusion
  8.3 0.1 iota_compare_fusion.1
  8.4 0.1 select_reduce_fusion
  8.5 0.1 copy.33
  8.6 9.5 %all_to_all.44 = s32[8,1,4]{2,1,0:T(1,128)S(1)} all-to-all(s32[8,1,4]{2,1,0:T(1,128)S(1)} %copy.33), channel_id=1, replica_groups=mesh['dp'=8,'tensor'=16] {'dp'}, dimensions={0} | all-to-all | bytes 256 | tf_op jit(solution)/shard_map/all_to_all | solution.py:121
  18.1 0.5 broadcast.224
  18.6 0.7 reduce.4
  19.2 0.1 reshape.279
  19.3 5.0 %gather_fusion = bf16[32,128,512]{2,1,0:T(8,128)(2,1)} fusion(bf16[32,128,512]{2,1,0:T(8,128)(2,1)} %param.9, s32[1024]{0:T(1024)S(1)} %pad_clamp_fusion.1), kind=kCustom, calls=%fused_computation | custom fusion | bytes 8388736 | tf_op jit(solution)/shard_map/jit(_take)/gather | solution.py:122
  24.3 4.6 %all-to-all-start.1 = ((bf16[8,4,128,512]{3,2,1,0:T(8,128)(2,1)}), bf16[8,4,128,512]{3,2,1,0:T(8,128)(2,1)}, u32[]{:S(2)}, u32[]{:S(2)}) async-start(bf16[8,4,128,512]{3,2,1,0:T(8,128)(2,1)} %bitcast.88), calls=%async_computation.1 | async-start | bytes 8388608 | tf_op jit(solution)/shard_map/all_to_all | solution.py:125
  28.9 0.0 all-gather.5.cloned.1.call-start
  29.0 0.7 fusion.39
  40.7 37.8 %all-to-all-done.1 = bf16[8,4,128,512]{3,2,1,0:T(8,128)(2,1)} async-done(((bf16[8,4,128,512]{3,2,1,0:T(8,128)(2,1)}), bf16[8,4,128,512]{3,2,1,0:T(8,128)(2,1)}, u32[]{:S(2)}, u32[]{:S(2)}) %all-to-all-start.1) | async-done | bytes 4194336 | tf_op jit(solution)/shard_map/all_to_all | solution.py:125
  78.5 0.9 dynamic-slice_dynamic-update-slice_fusion.5
  79.5 0.9 dynamic-slice_dynamic-update-slice_fusion.4
  80.4 0.9 dynamic-slice_dynamic-update-slice_fusion.3
  81.3 0.9 dynamic-slice_dynamic-update-slice_fusion.2
  82.2 0.9 dynamic-slice_dynamic-update-slice_fusion.1
  83.1 0.9 dynamic-slice_dynamic-update-slice_fusion
  84.1 0.0 copy-start.1
  84.1 0.9 copy-done.1
  85.0 0.0 all-gather.5.cloned.1.call-update
  85.0 0.1 slice.54
  85.1 6.4 %copy.48 = bf16[8192,256]{0,1:T(8,128)(2,1)} copy(bf16[8192,256]{1,0:T(8,128)(2,1)} %param.11) | data formatting | bytes 8388608 | tf_op jit(solution)/shard_map/reshape | solution.py:39
  91.5 0.0 all-gather.7.cloned.1.call-done
  91.5 0.0 copy-start
  91.5 4.4 %fusion.20 = bf16[193,256]{1,0:T(8,128)(2,1)S(1)} fusion(bf16[16,512,256]{2,1,0:T(8,128)(2,1)} %bitcast.102, bf16[16,256,512]{2,1,0:T(8,128)(2,1)} %bitcast.103), kind=kOutput, calls=%fused_computation.20 | convolution fusion | flops 809550080 | bytes 7569920 | tf_op jit(solution)/shard_map/srf,sfc->rc/dot_general | solution.py:103
  95.8 0.3 copy-done
  96.1 0.7 fusion.35
  96.8 0.7 copy.44
  97.4 8.5 %all-to-all-start.2 = ((f32[2,16,512]{2,0,1:T(2,128)}), f32[2,16,512]{2,0,1:T(2,128)S(1)}, u32[]{:S(2)}, u32[]{:S(2)}) async-start(f32[2,16,512]{2,0,1:T(2,128)} %bitcast.22), calls=%async_computation.2 | async-start | bytes 131072 | tf_op jit(solution)/shard_map/all_to_all | solution.py:43
  106.0 2.8 %gather_fusion.1 = bf16[2,128,512]{2,1,0:T(8,128)(2,1)S(1)} fusion(bf16[32,128,512]{2,1,0:T(8,128)(2,1)} %bitcast.2, s32[1024]{0:T(1024)S(1)} %pad_clamp_fusion), kind=kCustom, calls=%fused_computation.1 | custom fusion | bytes 524296 | tf_op jit(solution)/shard_map/jit(_take)/gather | solution.py:130
  108.7 5.7 %all-to-all-done.2 = f32[2,16,512]{2,0,1:T(2,128)S(1)} async-done(((f32[2,16,512]{2,0,1:T(2,128)}), f32[2,16,512]{2,0,1:T(2,128)S(1)}, u32[]{:S(2)}, u32[]{:S(2)}) %all-to-all-start.2) | async-done | bytes 65568 | tf_op jit(solution)/shard_map/all_to_all | solution.py:43
  114.5 0.3 fusion.41
  114.9 13.2 %all_to_all.45 = f32[16,32,256]{2,1,0:T(8,128)S(1)} all-to-all(f32[16,32,256]{2,1,0:T(8,128)S(1)} %broadcast_in_dim.10), channel_id=1, replica_groups=mesh['dp'=8,'tensor'=16] {'tensor'}, dimensions={0} | all-to-all | bytes 1048576 | tf_op jit(solution)/shard_map/all_to_all | solution.py:53
  128.1 0.1 multiply_reduce_fusion
  128.2 0.2 fusion.31
  128.4 0.1 divide_convert_fusion.2
  128.5 0.1 fusion.32
  128.6 0.7 copy.39
  129.3 3.5 %all-to-all-start.4 = ((f32[16,2,512]{2,1,0:T(2,128)}), f32[16,2,512]{2,1,0:T(2,128)S(1)}, u32[]{:S(2)}, u32[]{:S(2)}) async-start(f32[16,2,512]{2,1,0:T(2,128)} %copy.39), calls=%async_computation.4 | async-start | bytes 131072 | tf_op jit(solution)/shard_map/all_to_all | solution.py:65
  132.8 7.5 %pad_maximum_fusion = bf16[16,512,512]{2,1,0:T(8,128)(2,1)} fusion(bf16[16,512,256]{2,1,0:T(8,128)(2,1)} %bitcast.92, bf16[16,512,256]{2,1,0:T(8,128)(2,1)} %bitcast.90), kind=kLoop, calls=%fused_computation.3 | loop fusion | flops 16777216 | bytes 16777216 | tf_op jit(solution)/shard_map/concatenate | solution.py:134
  140.4 0.9 all-to-all-done.4
  141.3 3.6 %fusion.6 = f32[2,1,128]{2,1,0:T(1,128)S(1)} fusion(f32[2,8192,1]{1,0,2:T(2,128)S(1)} %bitcast.98, bf16[8192,256]{1,0:T(8,128)(2,1)} %param.12), kind=kOutput, calls=%fused_computation.9 | convolution fusion | flops 25165824 | bytes 4260864 | tf_op jit(solution)/shard_map/hf,fhd->hd/dot_general | solution.py:73
  144.9 33.9 %all-gather.5.cloned.1.call-done = bf16[96,128,512]{2,1,0:T(8,128)(2,1)} async-done(((bf16[6,128,512]{2,1,0:T(8,128)(2,1)}), bf16[96,128,512]{2,1,0:T(8,128)(2,1)}) %all-gather.5.cloned.1.call-update) | async-done | bytes 12582928 | tf_op jit(solution)/shard_map/all_gather | solution.py:131
  178.8 12.0 %bitcast_convert_fusion = bf16[6,128,512]{2,1,0:T(8,128)(2,1)S(1)} fusion(bf16[16,6,128,512]{3,2,1,0:T(8,128)(2,1)} %bitcast.101, bf16[16,512,512]{2,1,0:T(8,128)(2,1)} %pad_maximum_fusion), kind=kOutput, calls=%fused_computation.15 | convolution fusion | flops 6442844160 | bytes 21757952 | tf_op jit(solution)/shard_map/snkf,sfc->nkc/dot_general | solution.py:135
  190.8 0.1 fusion.38
  190.9 0.1 reshape_reshape.7
  191.0 0.3 convolution_multiply_fusion
  191.3 0.2 fusion.40
  191.5 0.1 reshape_reshape.6
  191.6 0.7 fusion.23
  192.3 0.1 copy.37
  192.5 3.2 %convert_bitcast_fusion = bf16[16,193,512]{2,1,0:T(8,128)(2,1)S(1)} fusion(bf16[32,16,8,512]{3,2,1,0:T(8,128)(2,1)} %bitcast.91, bf16[1,256]{1,0:T(2,128)(2,1)S(1)} %bitcast.100, bf16[192,256]{1,0:T(8,128)(2,1)S(1)} %bitcast.95), kind=kOutput, calls=%fused_computation.14 | convolution fusion | flops 811279360 | bytes 7455232 | tf_op jit(solution)/shard_map/rc,csf->srf/dot_general | solution.py:149
  195.7 45.1 %all_to_all.46 = bf16[16,193,512]{2,1,0:T(8,128)(2,1)S(1)} all-to-all(bf16[16,193,512]{2,1,0:T(8,128)(2,1)S(1)} %convert_bitcast_fusion), channel_id=1, replica_groups=mesh['dp'=8,'tensor'=16] {'tensor'}, dimensions={0} | all-to-all | bytes 6324224 | tf_op jit(solution)/shard_map/all_to_all | solution.py:155
  240.8 0.5 reduce_sum.62
  241.3 0.8 concatenate.11
  (14 shorter events, 0.2 us)
Async XLA Ops:
  6.5 84.9 %all-gather.7.cloned.1.call-start = ((), (), s32[]{:S(2)}) async-start(), calls=%async_computation.7 | async-start | bytes 4456448 | tf_op jit(solution)/shard_map/all_gather | solution.py:102
  24.3 54.2 %all-to-all-start.1 = ((bf16[8,4,128,512]{3,2,1,0:T(8,128)(2,1)}), bf16[8,4,128,512]{3,2,1,0:T(8,128)(2,1)}, u32[]{:S(2)}, u32[]{:S(2)}) async-start(bf16[8,4,128,512]{3,2,1,0:T(8,128)(2,1)} %bitcast.88), calls=%async_computation.1 | async-start | bytes 8388608 | tf_op jit(solution)/shard_map/all_to_all | solution.py:125
  28.9 149.9 %all-gather.5.cloned.1.call-start = ((), (), s32[]{:S(2)}) async-start(), calls=%async_computation.6 | async-start | bytes 13369344 | tf_op jit(solution)/shard_map/all_gather | solution.py:131
  84.1 0.9 copy-start.1
  91.5 4.6 %copy-start = (bf16[8192,256]{0,1:T(8,128)(2,1)S(1)}, bf16[8192,256]{0,1:T(8,128)(2,1)}, u32[]{:S(2)}) copy-start(bf16[8192,256]{0,1:T(8,128)(2,1)} %copy.48) | copy-start | bytes 12582916
  97.4 17.0 %all-to-all-start.2 = ((f32[2,16,512]{2,0,1:T(2,128)}), f32[2,16,512]{2,0,1:T(2,128)S(1)}, u32[]{:S(2)}, u32[]{:S(2)}) async-start(f32[2,16,512]{2,0,1:T(2,128)} %bitcast.22), calls=%async_computation.2 | async-start | bytes 131072 | tf_op jit(solution)/shard_map/all_to_all | solution.py:43
  129.3 11.9 %all-to-all-start.4 = ((f32[16,2,512]{2,1,0:T(2,128)}), f32[16,2,512]{2,1,0:T(2,128)S(1)}, u32[]{:S(2)}, u32[]{:S(2)}) async-start(f32[16,2,512]{2,1,0:T(2,128)} %copy.39), calls=%async_computation.4 | async-start | bytes 131072 | tf_op jit(solution)/shard_map/all_to_all | solution.py:65
Sparse Core Ops, SparseCore 0:
  9.5 54.0 all-gather.6
  85.1 93.5 all-gather.4

commit v15 on v8

--- a/solution.py
+++ b/solution.py
@@ -101,7 +101,7 @@
         preferred_element_type=jnp.float32,
     )
     query_rows = query_sum.astype(jnp.bfloat16)
-    block_ids = neighbour_ids.reshape(per_reader)
+    block_ids = neighbour_ids.T.reshape(per_reader)
     owners = block_ids // db_count
     earlier = jnp.arange(per_reader)[:, None] > jnp.arange(per_reader)[None, :]
     slot_rank = jnp.sum(((owners[:, None] == owners[None, :]) & earlier).astype(jnp.int32), 1)
@@ -118,7 +118,7 @@
     )
     arrived = lax.all_to_all(outgoing, "dp", split_axis=0, concat_axis=0, tiled=True)
     arrived_rows = arrived.reshape(dp_count * capacity, ret_len, col_count)
-    arrived_slot = owners * capacity + slot_rank
+    arrived_slot = (owners * capacity + slot_rank).reshape(-1, group_count).T.reshape(per_reader)
     main_rows = per_reader - 2
     head_rows = jnp.take(arrived_rows, arrived_slot[:main_rows], axis=0, mode="clip")
     tail_rows = jnp.take(arrived_rows, arrived_slot[main_rows:], axis=0, mode="clip")

time: 247 us -> 247 us (level)
  no operation moved by 1% of the time
where the time goes in v15:
time: 247 us; the launch traced here: 246 us
  waiting for transfers between devices  90.2 us (37%)
  blocking collectives  68.1 us (28%)
  matrix products  25.4 us (10%)
  local copies, waits for them, and re-layouts  22.7 us (9%)
  starting transfers between devices  16.8 us (7%)
  between operations  13.6 us (6%)
  other arithmetic  9.74 us (4%)
    all_to_all x1, waiting for transfers between devices, shards(): lax.all_to_all(outgoing, 'dp', split_axis=0, concat_axis=0, tiled=True)  49.3 us
    all_to_all x1, blocking collectives, shards(): lax.all_to_all(partial_out, 'tensor', split_axis=0, concat_axis=0, tiled=...  45.1 us
    all_gather x1, waiting for transfers between devices, shards(): main_parts = lax.all_gather(head_rows, 'tensor', axis=0, tiled=False)  33.5 us
    all_to_all x1, blocking collectives, last_token(): lax.all_to_all(jnp.broadcast_to(partial_scores[None], (tensor_count,) + p...  13.5 us
    dot_general x1, matrix products, shards(): jnp.einsum('snkf,sfc->nkc', main_parts, w_both, preferred_element_type=jn...  12 us
    all_to_all x1, blocking collectives, shards(): lax.all_to_all(request_table, 'dp', split_axis=0, concat_axis=0, tiled=True)  9.49 us
    all_to_all x1, starting transfers between devices, last_token(): lax.all_to_all(spread_query.reshape(heads_count, tensor_count, col_count)...  8.54 us
    concatenate x1, other arithmetic, shards(): jnp.concatenate([w_key_parts, w_value_parts], axis=2)  7.47 us
  transfers between devices with their start and end apart: 5, of which 4 were waited for; matrix products, arithmetic and copies ran while one was open for 16% of the time, Pallas kernels for 0%

profile of v15, /device:TPU:0, one launch (start us, length us, event | category | flops | bytes accessed | tf_op | source)
XLA Modules:
  0.0 246.5 jit_solution(17886961534025877675)
XLA Ops:
  6.5 0.0 all-gather.7.cloned.1.call-start
  6.5 0.7 all-gather.7.cloned.1.call-update
  7.3 0.8 reshape.269
  8.0 0.2 convert_reduce_fusion
  8.2 0.1 iota_compare_fusion.1
  8.3 0.1 select_reduce_fusion
  8.4 0.1 copy.32
  8.5 9.5 %all_to_all.44 = s32[8,1,4]{2,1,0:T(1,128)S(1)} all-to-all(s32[8,1,4]{2,1,0:T(1,128)S(1)} %copy.32), channel_id=1, replica_groups=mesh['dp'=8,'tensor'=16] {'dp'}, dimensions={0} | all-to-all | bytes 256 | tf_op jit(solution)/shard_map/all_to_all | solution.py:115
  18.0 0.5 broadcast.241
  18.5 0.7 reduce.6
  19.1 0.1 reshape.286
  19.2 5.0 %gather_fusion = bf16[32,128,512]{2,1,0:T(8,128)(2,1)} fusion(bf16[32,128,512]{2,1,0:T(8,128)(2,1)} %param.9, s32[1024]{0:T(1024)S(1)} %pad_clamp_fusion.2), kind=kCustom, calls=%fused_computation | custom fusion | bytes 8388736 | tf_op jit(solution)/shard_map/jit(_take)/gather | solution.py:116
  24.2 0.0 copy-start.1
  24.2 4.7 %all-to-all-start.1 = ((bf16[8,4,128,512]{3,2,1,0:T(8,128)(2,1)}), bf16[8,4,128,512]{3,2,1,0:T(8,128)(2,1)}, u32[]{:S(2)}, u32[]{:S(2)}) async-start(bf16[8,4,128,512]{3,2,1,0:T(8,128)(2,1)} %bitcast.87), calls=%async_computation.1 | async-start | bytes 8388608 | tf_op jit(solution)/shard_map/all_to_all | solution.py:119
  28.9 0.0 all-gather.5.cloned.1.call-start
  29.0 0.1 reduce_sum.61
  29.1 0.0 copy-done.1
  29.1 0.1 copy.33
  29.2 0.1 reshape.294
  29.3 49.3 %all-to-all-done.1 = bf16[8,4,128,512]{3,2,1,0:T(8,128)(2,1)} async-done(((bf16[8,4,128,512]{3,2,1,0:T(8,128)(2,1)}), bf16[8,4,128,512]{3,2,1,0:T(8,128)(2,1)}, u32[]{:S(2)}, u32[]{:S(2)}) %all-to-all-start.1) | async-done | bytes 4194336 | tf_op jit(solution)/shard_map/all_to_all | solution.py:119
  78.6 3.7 %gather_fusion.1 = bf16[6,128,512]{2,1,0:T(8,128)(2,1)} fusion(bf16[32,128,512]{2,1,0:T(8,128)(2,1)} %bitcast.3, s32[1024]{0:T(1024)S(1)} %pad_clamp_fusion.1), kind=kCustom, calls=%fused_computation.1 | custom fusion | bytes 1572888 | tf_op jit(solution)/shard_map/jit(_take)/gather | solution.py:123
  82.3 0.0 all-gather.5.cloned.1.call-update
  82.3 6.4 %copy.48 = bf16[8192,256]{0,1:T(8,128)(2,1)} copy(bf16[8192,256]{1,0:T(8,128)(2,1)} %param.11) | data formatting | bytes 8388608 | tf_op jit(solution)/shard_map/reshape | solution.py:39
  88.7 0.2 slice_reduce_fusion
  88.9 0.0 all-gather.7.cloned.1.call-done
  88.9 0.0 copy-start
  88.9 4.4 %fusion.20 = bf16[193,256]{1,0:T(8,128)(2,1)S(1)} fusion(bf16[16,512,256]{2,1,0:T(8,128)(2,1)} %bitcast.103, bf16[16,256,512]{2,1,0:T(8,128)(2,1)} %bitcast.104), kind=kOutput, calls=%fused_computation.21 | convolution fusion | flops 809550080 | bytes 7569920 | tf_op jit(solution)/shard_map/srf,sfc->rc/dot_general | solution.py:97
  93.3 0.3 copy-done
  93.6 0.7 fusion.35
  94.2 0.7 copy.44
  94.9 8.5 %all-to-all-start.2 = ((f32[2,16,512]{2,0,1:T(2,128)}), f32[2,16,512]{2,0,1:T(2,128)S(1)}, u32[]{:S(2)}, u32[]{:S(2)}) async-start(f32[2,16,512]{2,0,1:T(2,128)} %bitcast.18), calls=%async_computation.2 | async-start | bytes 131072 | tf_op jit(solution)/shard_map/all_to_all | solution.py:43
  103.5 2.8 %gather_fusion.2 = bf16[2,128,512]{2,1,0:T(8,128)(2,1)S(1)} fusion(bf16[32,128,512]{2,1,0:T(8,128)(2,1)} %bitcast.3, s32[1024]{0:T(1024)S(1)} %pad_clamp_fusion), kind=kCustom, calls=%fused_computation.2 | custom fusion | bytes 524296 | tf_op jit(solution)/shard_map/jit(_take)/gather | solution.py:124
  106.3 5.7 %all-to-all-done.2 = f32[2,16,512]{2,0,1:T(2,128)S(1)} async-done(((f32[2,16,512]{2,0,1:T(2,128)}), f32[2,16,512]{2,0,1:T(2,128)S(1)}, u32[]{:S(2)}, u32[]{:S(2)}) %all-to-all-start.2) | async-done | bytes 65568 | tf_op jit(solution)/shard_map/all_to_all | solution.py:43
  112.0 0.3 fusion.40
  112.4 13.5 %all_to_all.45 = f32[16,32,256]{2,1,0:T(8,128)S(1)} all-to-all(f32[16,32,256]{2,1,0:T(8,128)S(1)} %broadcast_in_dim.17), channel_id=1, replica_groups=mesh['dp'=8,'tensor'=16] {'tensor'}, dimensions={0} | all-to-all | bytes 1048576 | tf_op jit(solution)/shard_map/all_to_all | solution.py:53
  125.9 0.1 multiply_reduce_fusion
  126.0 0.2 fusion.31
  126.2 0.1 divide_convert_fusion.2
  126.4 0.1 fusion.32
  126.5 0.7 copy.39
  127.2 3.5 %all-to-all-start.4 = ((f32[16,2,512]{2,1,0:T(2,128)}), f32[16,2,512]{2,1,0:T(2,128)S(1)}, u32[]{:S(2)}, u32[]{:S(2)}) async-start(f32[16,2,512]{2,1,0:T(2,128)} %copy.39), calls=%async_computation.4 | async-start | bytes 131072 | tf_op jit(solution)/shard_map/all_to_all | solution.py:65
  130.7 7.5 %pad_maximum_fusion = bf16[16,512,512]{2,1,0:T(8,128)(2,1)} fusion(bf16[16,512,256]{2,1,0:T(8,128)(2,1)} %bitcast.91, bf16[16,512,256]{2,1,0:T(8,128)(2,1)} %bitcast.89), kind=kLoop, calls=%fused_computation.4 | loop fusion | flops 16777216 | bytes 16777216 | tf_op jit(solution)/shard_map/concatenate | solution.py:128
  138.2 0.9 all-to-all-done.4
  139.1 3.6 %fusion.6 = f32[2,1,128]{2,1,0:T(1,128)S(1)} fusion(f32[2,8192,1]{1,0,2:T(2,128)S(1)} %bitcast.97, bf16[8192,256]{1,0:T(8,128)(2,1)} %param.12), kind=kOutput, calls=%fused_computation.10 | convolution fusion | flops 25165824 | bytes 4260864 | tf_op jit(solution)/shard_map/hf,fhd->hd/dot_general | solution.py:73
  142.8 33.5 %all-gather.5.cloned.1.call-done = bf16[96,128,512]{2,1,0:T(8,128)(2,1)} async-done(((bf16[6,128,512]{2,1,0:T(8,128)(2,1)}), bf16[96,128,512]{2,1,0:T(8,128)(2,1)}) %all-gather.5.cloned.1.call-update) | async-done | bytes 12582928 | tf_op jit(solution)/shard_map/all_gather | solution.py:125
  176.3 12.0 %bitcast_convert_fusion = bf16[6,128,512]{2,1,0:T(8,128)(2,1)S(1)} fusion(bf16[16,6,128,512]{3,2,1,0:T(8,128)(2,1)} %bitcast.102, bf16[16,512,512]{2,1,0:T(8,128)(2,1)} %pad_maximum_fusion), kind=kOutput, calls=%fused_computation.16 | convolution fusion | flops 6442844160 | bytes 21757952 | tf_op jit(solution)/shard_map/snkf,sfc->nkc/dot_general | solution.py:129
  188.4 0.1 fusion.38
  188.4 0.1 reshape_reshape.7
  188.5 0.3 convolution_multiply_fusion
  188.8 0.2 fusion.39
  189.0 0.1 reshape_reshape.6
  189.1 0.7 fusion.23
  189.9 0.1 copy.37
  190.0 3.2 %convert_bitcast_fusion = bf16[16,193,512]{2,1,0:T(8,128)(2,1)S(1)} fusion(bf16[32,16,8,512]{3,2,1,0:T(8,128)(2,1)} %bitcast.90, bf16[1,256]{1,0:T(2,128)(2,1)S(1)} %bitcast.100, bf16[192,256]{1,0:T(8,128)(2,1)S(1)} %bitcast.94), kind=kOutput, calls=%fused_computation.15 | convolution fusion | flops 811279360 | bytes 7455232 | tf_op jit(solution)/shard_map/rc,csf->srf/dot_general | solution.py:143
  193.2 45.1 %all_to_all.46 = bf16[16,193,512]{2,1,0:T(8,128)(2,1)S(1)} all-to-all(bf16[16,193,512]{2,1,0:T(8,128)(2,1)S(1)} %convert_bitcast_fusion), channel_id=1, replica_groups=mesh['dp'=8,'tensor'=16] {'tensor'}, dimensions={0} | all-to-all | bytes 6324224 | tf_op jit(solution)/shard_map/all_to_all | solution.py:149
  238.3 0.5 reduce_sum.65
  238.9 0.8 concatenate.11
  (15 shorter events, 0.3 us)
Async XLA Ops:
  6.5 82.4 %all-gather.7.cloned.1.call-start = ((), (), s32[]{:S(2)}) async-start(), calls=%async_computation.7 | async-start | bytes 4456448 | tf_op jit(solution)/shard_map/all_gather | solution.py:96
  24.2 4.9 %copy-start.1 = (s32[4,2]{0,1:T(2,128)S(1)}, s32[4,2]{0,1:T(2,128)}, u32[]{:S(2)}) copy-start(s32[4,2]{0,1:T(2,128)} %param.8) | copy-start | bytes 100
  24.2 54.4 %all-to-all-start.1 = ((bf16[8,4,128,512]{3,2,1,0:T(8,128)(2,1)}), bf16[8,4,128,512]{3,2,1,0:T(8,128)(2,1)}, u32[]{:S(2)}, u32[]{:S(2)}) async-start(bf16[8,4,128,512]{3,2,1,0:T(8,128)(2,1)} %bitcast.87), calls=%async_computation.1 | async-start | bytes 8388608 | tf_op jit(solution)/shard_map/all_to_all | solution.py:119
  28.9 147.4 %all-gather.5.cloned.1.call-start = ((), (), s32[]{:S(2)}) async-start(), calls=%async_computation.6 | async-start | bytes 13369344 | tf_op jit(solution)/shard_map/all_gather | solution.py:125
  88.9 4.7 %copy-start = (bf16[8192,256]{0,1:T(8,128)(2,1)S(1)}, bf16[8192,256]{0,1:T(8,128)(2,1)}, u32[]{:S(2)}) copy-start(bf16[8192,256]{0,1:T(8,128)(2,1)} %copy.48) | copy-start | bytes 12582916
  94.9 17.0 %all-to-all-start.2 = ((f32[2,16,512]{2,0,1:T(2,128)}), f32[2,16,512]{2,0,1:T(2,128)S(1)}, u32[]{:S(2)}, u32[]{:S(2)}) async-start(f32[2,16,512]{2,0,1:T(2,128)} %bitcast.18), calls=%async_computation.2 | async-start | bytes 131072 | tf_op jit(solution)/shard_map/all_to_all | solution.py:43
  127.2 11.9 %all-to-all-start.4 = ((f32[16,2,512]{2,1,0:T(2,128)}), f32[16,2,512]{2,1,0:T(2,128)S(1)}, u32[]{:S(2)}, u32[]{:S(2)}) async-start(f32[16,2,512]{2,1,0:T(2,128)} %copy.39), calls=%async_computation.4 | async-start | bytes 131072 | tf_op jit(solution)/shard_map/all_to_all | solution.py:65
Sparse Core Ops, SparseCore 0:
  9.5 53.9 all-gather.6
  82.5 93.8 all-gather.4

commit v16 on v11

--- a/solution.py
+++ b/solution.py
@@ -108,7 +108,7 @@
         preferred_element_type=jnp.float32,
     )
     query_rows = query_sum.astype(jnp.bfloat16)
-    block_ids = neighbour_ids.reshape(per_reader)
+    block_ids = neighbour_ids.T.reshape(per_reader)
     owners = block_ids // db_count
     earlier = jnp.arange(per_reader)[:, None] > jnp.arange(per_reader)[None, :]
     slot_rank = jnp.sum(((owners[:, None] == owners[None, :]) & earlier).astype(jnp.int32), 1)
@@ -125,7 +125,7 @@
     )
     arrived = lax.all_to_all(outgoing, "dp", split_axis=0, concat_axis=0, tiled=True)
     arrived_rows = arrived.reshape(dp_count * capacity, ret_len, col_count)
-    arrived_slot = owners * capacity + slot_rank
+    arrived_slot = (owners * capacity + slot_rank).reshape(-1, group_count).T.reshape(per_reader)
     main_rows = per_reader - 2
     head_rows = jnp.take(arrived_rows, arrived_slot[:main_rows], axis=0, mode="clip")
     tail_rows = jnp.take(arrived_rows, arrived_slot[main_rows:], axis=0, mode="clip")
@@ -146,7 +146,6 @@
         query_rows[main_groups * group_len], tail_rows, w_key, w_value, heads_local
     )
     live = jnp.concatenate([main_live, last_live[None]], 0)
-    live_rows = live.shape[0]
     partial_out = jnp.einsum(
         "rc,csf->srf",
         live,
@@ -155,7 +154,9 @@
     ).astype(jnp.bfloat16)
     spread = lax.all_to_all(partial_out, "tensor", split_axis=0, concat_axis=0, tiled=True)
     summed = jnp.sum(spread.astype(jnp.float32), axis=0).astype(jnp.bfloat16)
-    return jnp.concatenate([jnp.zeros((group_len - 1, summed.shape[1]), jnp.bfloat16), summed], 0)
+    return lax.dynamic_update_slice(
+        jnp.zeros((tok_rows, summed.shape[1]), jnp.bfloat16), summed, (group_len - 1, 0)
+    )
 
 
 def solution(mesh):
@@ -168,6 +169,7 @@
         P(None, "tensor"),
         P("tensor", None),
     )
+
     return jax.shard_map(
         shards, mesh=mesh, in_specs=placed, out_specs=P("dp", "tensor"), check_vma=False
     )

time: 246 us -> 246 us (level)
  no operation moved by 1% of the time
where the time goes in v16:
time: 246 us
  waiting for transfers between devices  80.8 us (33%)
  blocking collectives  76.8 us (31%)
  matrix products  25.3 us (10%)
  local copies, waits for them, and re-layouts  22.7 us (9%)
  starting transfers between devices  16.8 us (7%)
  between operations  13.6 us (6%)
  other arithmetic  9.69 us (4%)
    all_to_all x1, waiting for transfers between devices, shards(): lax.all_to_all(outgoing, 'dp', split_axis=0, concat_axis=0, tiled=True)  49.3 us
    all_to_all x1, blocking collectives, shards(): lax.all_to_all(partial_out, 'tensor', split_axis=0, concat_axis=0, tiled=...  45.9 us
    all_gather x1, waiting for transfers between devices, shards(): main_parts = lax.all_gather(head_rows, 'tensor', axis=0, tiled=False)  24.1 us
    dot_general x1, matrix products, shards(): jnp.einsum('snkf,sfc->nkc', main_parts, w_both, preferred_element_type=jn...  12 us
    all_to_all x1, blocking collectives, last_token(): lax.all_to_all(jnp.broadcast_to(own_soft[None], (tensor_count,) + own_sof...  10.8 us
    all_to_all x1, blocking collectives, last_token(): lax.all_to_all(partial_scores.reshape(tensor_count, heads_count, -1), 'te...  10.6 us
    all_to_all x1, blocking collectives, shards(): lax.all_to_all(request_table, 'dp', split_axis=0, concat_axis=0, tiled=True)  9.49 us
    all_to_all x1, starting transfers between devices, last_token(): lax.all_to_all(spread_query.reshape(heads_count, tensor_count, col_count)...  8.54 us
  transfers between devices with their start and end apart: 5, of which 4 were waited for; matrix products, arithmetic and copies ran while one was open for 16% of the time, Pallas kernels for 0%

profile of v16, /device:TPU:0, one launch (start us, length us, event | category | flops | bytes accessed | tf_op | source)
XLA Modules:
  0.0 245.6 jit_solution(3816405458921057905)
XLA Ops:
  6.5 0.0 all-gather.7.cloned.1.call-start
  6.5 0.7 all-gather.7.cloned.1.call-update
  7.3 0.8 reshape.244
  8.0 0.2 convert_reduce_fusion
  8.2 0.1 iota_compare_fusion.1
  8.3 0.1 select_reduce_fusion
  8.4 0.1 copy.33
  8.5 9.5 %all_to_all.49 = s32[8,1,4]{2,1,0:T(1,128)S(1)} all-to-all(s32[8,1,4]{2,1,0:T(1,128)S(1)} %copy.33), channel_id=1, replica_groups=mesh['dp'=8,'tensor'=16] {'dp'}, dimensions={0} | all-to-all | bytes 256 | tf_op jit(solution)/shard_map/all_to_all | solution.py:122
  18.0 0.5 broadcast.214
  18.5 0.7 reduce.6
  19.1 0.1 reshape.260
  19.2 5.0 %gather_fusion = bf16[32,128,512]{2,1,0:T(8,128)(2,1)} fusion(bf16[32,128,512]{2,1,0:T(8,128)(2,1)} %param.9, s32[1024]{0:T(1024)S(1)} %pad_clamp_fusion.2), kind=kCustom, calls=%fused_computation | custom fusion | bytes 8388736 | tf_op jit(solution)/shard_map/jit(_take)/gather | solution.py:123
  24.2 0.0 copy-start.1
  24.2 4.7 %all-to-all-start.1 = ((bf16[8,4,128,512]{3,2,1,0:T(8,128)(2,1)}), bf16[8,4,128,512]{3,2,1,0:T(8,128)(2,1)}, u32[]{:S(2)}, u32[]{:S(2)}) async-start(bf16[8,4,128,512]{3,2,1,0:T(8,128)(2,1)} %bitcast.88), calls=%async_computation.1 | async-start | bytes 8388608 | tf_op jit(solution)/shard_map/all_to_all | solution.py:126
  28.9 0.0 all-gather.5.cloned.1.call-start
  29.0 0.1 reduce_sum.61
  29.1 0.0 copy-done.1
  29.1 0.1 copy.34
  29.2 0.1 reshape.268
  29.3 49.3 %all-to-all-done.1 = bf16[8,4,128,512]{3,2,1,0:T(8,128)(2,1)} async-done(((bf16[8,4,128,512]{3,2,1,0:T(8,128)(2,1)}), bf16[8,4,128,512]{3,2,1,0:T(8,128)(2,1)}, u32[]{:S(2)}, u32[]{:S(2)}) %all-to-all-start.1) | async-done | bytes 4194336 | tf_op jit(solution)/shard_map/all_to_all | solution.py:126
  78.6 3.7 %gather_fusion.1 = bf16[6,128,512]{2,1,0:T(8,128)(2,1)} fusion(bf16[32,128,512]{2,1,0:T(8,128)(2,1)} %bitcast.3, s32[1024]{0:T(1024)S(1)} %pad_clamp_fusion.1), kind=kCustom, calls=%fused_computation.1 | custom fusion | bytes 1572888 | tf_op jit(solution)/shard_map/jit(_take)/gather | solution.py:130
  82.3 0.0 all-gather.5.cloned.1.call-update
  82.3 6.4 %copy.51 = bf16[8192,256]{0,1:T(8,128)(2,1)} copy(bf16[8192,256]{1,0:T(8,128)(2,1)} %param.11) | data formatting | bytes 8388608 | tf_op jit(solution)/shard_map/reshape | solution.py:39
  88.7 0.2 slice_reduce_fusion
  88.9 0.0 all-gather.7.cloned.1.call-done
  88.9 0.0 copy-start
  88.9 4.4 %fusion.20 = bf16[193,256]{1,0:T(8,128)(2,1)S(1)} fusion(bf16[16,512,256]{2,1,0:T(8,128)(2,1)} %bitcast.103, bf16[16,256,512]{2,1,0:T(8,128)(2,1)} %bitcast.104), kind=kOutput, calls=%fused_computation.21 | convolution fusion | flops 809550080 | bytes 7569920 | tf_op jit(solution)/shard_map/srf,sfc->rc/dot_general | solution.py:104
  93.3 0.3 copy-done
  93.6 0.7 fusion.37
  94.2 0.7 copy.47
  94.9 8.5 %all-to-all-start.2 = ((f32[2,16,512]{2,0,1:T(2,128)}), f32[2,16,512]{2,0,1:T(2,128)S(1)}, u32[]{:S(2)}, u32[]{:S(2)}) async-start(f32[2,16,512]{2,0,1:T(2,128)} %bitcast.18), calls=%async_computation.2 | async-start | bytes 131072 | tf_op jit(solution)/shard_map/all_to_all | solution.py:43
  103.5 2.8 %gather_fusion.2 = bf16[2,128,512]{2,1,0:T(8,128)(2,1)S(1)} fusion(bf16[32,128,512]{2,1,0:T(8,128)(2,1)} %bitcast.3, s32[1024]{0:T(1024)S(1)} %pad_clamp_fusion), kind=kCustom, calls=%fused_computation.2 | custom fusion | bytes 524296 | tf_op jit(solution)/shard_map/jit(_take)/gather | solution.py:131
  106.3 5.7 %all-to-all-done.2 = f32[2,16,512]{2,0,1:T(2,128)S(1)} async-done(((f32[2,16,512]{2,0,1:T(2,128)}), f32[2,16,512]{2,0,1:T(2,128)S(1)}, u32[]{:S(2)}, u32[]{:S(2)}) %all-to-all-start.2) | async-done | bytes 65568 | tf_op jit(solution)/shard_map/all_to_all | solution.py:43
  112.0 0.3 fusion.30
  112.3 10.6 %all_to_all.50 = f32[16,2,256]{2,1,0:T(2,128)S(1)} all-to-all(f32[16,2,256]{2,1,0:T(2,128)S(1)} %copy.40), channel_id=1, replica_groups=mesh['dp'=8,'tensor'=16] {'tensor'}, dimensions={0} | all-to-all | bytes 65536 | tf_op jit(solution)/shard_map/all_to_all | solution.py:53
  122.9 0.1 multiply_reduce_fusion
  123.1 0.2 fusion.40
  123.3 0.1 divide_convert_fusion.2
  123.4 10.8 %all_to_all.51 = bf16[16,2,256]{2,1,0:T(2,128)(2,1)S(1)} all-to-all(bf16[16,2,256]{2,1,0:T(2,128)(2,1)S(1)} %broadcast_in_dim.17), channel_id=1, replica_groups=mesh['dp'=8,'tensor'=16] {'tensor'}, dimensions={0} | all-to-all | bytes 32768 | tf_op jit(solution)/shard_map/all_to_all | solution.py:64
  134.2 0.1 fusion.34
  134.3 0.7 copy.42
  135.0 3.5 %all-to-all-start.5 = ((f32[16,2,512]{2,1,0:T(2,128)}), f32[16,2,512]{2,1,0:T(2,128)S(1)}, u32[]{:S(2)}, u32[]{:S(2)}) async-start(f32[16,2,512]{2,1,0:T(2,128)} %copy.42), calls=%async_computation.5 | async-start | bytes 131072 | tf_op jit(solution)/shard_map/all_to_all | solution.py:72
  138.5 7.4 %pad_maximum_fusion = bf16[16,512,512]{2,1,0:T(8,128)(2,1)} fusion(bf16[16,512,256]{2,1,0:T(8,128)(2,1)} %bitcast.92, bf16[16,512,256]{2,1,0:T(8,128)(2,1)} %bitcast.90), kind=kLoop, calls=%fused_computation.4 | loop fusion | flops 16777216 | bytes 16777216 | tf_op jit(solution)/shard_map/concatenate | solution.py:135
  146.0 0.9 all-to-all-done.5
  146.9 3.6 %fusion.6 = f32[2,1,128]{2,1,0:T(1,128)S(1)} fusion(f32[2,8192,1]{1,0,2:T(2,128)S(1)} %bitcast.97, bf16[8192,256]{1,0:T(8,128)(2,1)} %param.12), kind=kOutput, calls=%fused_computation.10 | convolution fusion | flops 25165824 | bytes 4260864 | tf_op jit(solution)/shard_map/hf,fhd->hd/dot_general | solution.py:80
  150.6 24.1 %all-gather.5.cloned.1.call-done = bf16[96,128,512]{2,1,0:T(8,128)(2,1)} async-done(((bf16[6,128,512]{2,1,0:T(8,128)(2,1)}), bf16[96,128,512]{2,1,0:T(8,128)(2,1)}) %all-gather.5.cloned.1.call-update) | async-done | bytes 12582928 | tf_op jit(solution)/shard_map/all_gather | solution.py:132
  174.7 12.0 %bitcast_convert_fusion = bf16[6,128,512]{2,1,0:T(8,128)(2,1)S(1)} fusion(bf16[16,6,128,512]{3,2,1,0:T(8,128)(2,1)} %bitcast.102, bf16[16,512,512]{2,1,0:T(8,128)(2,1)} %pad_maximum_fusion), kind=kOutput, calls=%fused_computation.16 | convolution fusion | flops 6442844160 | bytes 21757952 | tf_op jit(solution)/shard_map/snkf,sfc->nkc/dot_general | solution.py:136
  186.7 0.1 fusion.41
  186.8 0.1 reshape_reshape.7
  186.9 0.2 convolution_multiply_fusion
  187.2 0.2 fusion.42
  187.4 0.1 reshape_reshape.6
  187.5 0.7 fusion.23
  188.2 0.1 copy.38
  188.4 3.2 %convert_bitcast_fusion = bf16[16,193,512]{2,1,0:T(8,128)(2,1)S(1)} fusion(bf16[32,16,8,512]{3,2,1,0:T(8,128)(2,1)} %bitcast.91, bf16[1,256]{1,0:T(2,128)(2,1)S(1)} %bitcast.100, bf16[192,256]{1,0:T(8,128)(2,1)S(1)} %bitcast.95), kind=kOutput, calls=%fused_computation.15 | convolution fusion | flops 811279360 | bytes 7455232 | tf_op jit(solution)/shard_map/rc,csf->srf/dot_general | solution.py:149
  191.6 45.9 %all_to_all.52 = bf16[16,193,512]{2,1,0:T(8,128)(2,1)S(1)} all-to-all(bf16[16,193,512]{2,1,0:T(8,128)(2,1)S(1)} %convert_bitcast_fusion), channel_id=1, replica_groups=mesh['dp'=8,'tensor'=16] {'tensor'}, dimensions={0} | all-to-all | bytes 6324224 | tf_op jit(solution)/shard_map/all_to_all | solution.py:155
  237.5 0.5 reduce_sum.65
  238.0 0.8 dynamic_update_slice.3
  (14 shorter events, 0.2 us)
Async XLA Ops:
  6.5 82.4 %all-gather.7.cloned.1.call-start = ((), (), s32[]{:S(2)}) async-start(), calls=%async_computation.8 | async-start | bytes 4456448 | tf_op jit(solution)/shard_map/all_gather | solution.py:103
  24.2 4.9 %copy-start.1 = (s32[4,2]{0,1:T(2,128)S(1)}, s32[4,2]{0,1:T(2,128)}, u32[]{:S(2)}) copy-start(s32[4,2]{0,1:T(2,128)} %param.8) | copy-start | bytes 100
  24.2 54.4 %all-to-all-start.1 = ((bf16[8,4,128,512]{3,2,1,0:T(8,128)(2,1)}), bf16[8,4,128,512]{3,2,1,0:T(8,128)(2,1)}, u32[]{:S(2)}, u32[]{:S(2)}) async-start(bf16[8,4,128,512]{3,2,1,0:T(8,128)(2,1)} %bitcast.88), calls=%async_computation.1 | async-start | bytes 8388608 | tf_op jit(solution)/shard_map/all_to_all | solution.py:126
  28.9 145.7 %all-gather.5.cloned.1.call-start = ((), (), s32[]{:S(2)}) async-start(), calls=%async_computation.7 | async-start | bytes 13369344 | tf_op jit(solution)/shard_map/all_gather | solution.py:132
  88.9 4.7 %copy-start = (bf16[8192,256]{0,1:T(8,128)(2,1)S(1)}, bf16[8192,256]{0,1:T(8,128)(2,1)}, u32[]{:S(2)}) copy-start(bf16[8192,256]{0,1:T(8,128)(2,1)} %copy.51) | copy-start | bytes 12582916
  94.9 17.0 %all-to-all-start.2 = ((f32[2,16,512]{2,0,1:T(2,128)}), f32[2,16,512]{2,0,1:T(2,128)S(1)}, u32[]{:S(2)}, u32[]{:S(2)}) async-start(f32[2,16,512]{2,0,1:T(2,128)} %bitcast.18), calls=%async_computation.2 | async-start | bytes 131072 | tf_op jit(solution)/shard_map/all_to_all | solution.py:43
  135.0 11.9 %all-to-all-start.5 = ((f32[16,2,512]{2,1,0:T(2,128)}), f32[16,2,512]{2,1,0:T(2,128)S(1)}, u32[]{:S(2)}, u32[]{:S(2)}) async-start(f32[16,2,512]{2,1,0:T(2,128)} %copy.42), calls=%async_computation.5 | async-start | bytes 131072 | tf_op jit(solution)/shard_map/all_to_all | solution.py:72
Sparse Core Ops, SparseCore 0:
  9.5 53.9 all-gather.6
  82.5 92.1 all-gather.4
